TPU v7x, 512 devices: a whole 4x4x16 slice. The times are simulated.
512 devices in a mesh: chan: 128 (over y, z, core), tm: 4 (over x).
Axes of the slice: x: 4, y: 4, z: 16, core: 2. Of those that a mesh axis runs over, the one named last changes fastest.
Arguments:
- voltages: bfloat16 [512, 128, 2, 1024], P('chan', 'tm'), may hold values from -6 to 6
- filter_taps: float32 [12, 1024], replicated, may hold values from -1.75 to 1.75
- flagged: int32 [256], replicated, may hold values from 0 to 1023, as said below
- owners: int32 [1024], replicated, may hold values from 0 to 511, as said below
Outputs:
- visibilities: float32 [1024, 2, 512, 512], P(('chan', 'tm'))
Inputs may be any that keep to these rules, and one draw needn't show every extreme that they name: `flagged`: distinct channel numbers. `owners`: each device owns exactly 2 of the 1024 channels, flagged or not; device d is the one with chan index d // 4 and tm index d % 4.
All inputs are finite; a program needn't handle non-finite values.
Results may differ from a plain program's by a relative error of at most 0.0059.
Values may be sent and summed in bfloat16 or wider, within the bound.
No kernel may reach another device: no remote copies, remote signals or barrier semaphores. Data moves between devices by JAX's collectives and lax.ppermute only.
A program may use at most 64 MiB of HBM per device.

v0:
```python
import math

import jax
import jax.numpy as jnp
from jax import lax
from jax.sharding import PartitionSpec as P


def from_behind(value, axis, by):
    count = lax.axis_size(axis)
    pairs = [(i, i + by) for i in range(count) if 0 <= i + by < count]
    return lax.ppermute(value, axis, pairs)


def slot_table(flagged, owners, channels, capacity):
    channel_ids = jnp.arange(channels, dtype=jnp.int32)
    alive_mask = jnp.logical_not(jnp.any(flagged[:, None] == channel_ids[None, :], axis=0))
    earlier = (
        (owners[None, :] == owners[:, None])
        & alive_mask[None, :]
        & (channel_ids[None, :] < channel_ids[:, None])
    )
    order_rank = jnp.sum(earlier.astype(jnp.int32), axis=1)
    slot_of = owners * capacity + order_rank
    matches = (slot_of[None, :] == channel_ids[:, None]) & alive_mask[None, :]
    present = jnp.any(matches, axis=1)
    chosen = jnp.sum(jnp.where(matches, channel_ids[None, :], 0), axis=1)
    return (chosen, present)


def slot_tables(chosen, present, channels):
    low = 32
    high = channels // low
    step = 2.0 * math.pi / channels
    hi = jnp.arange(high, dtype=jnp.int32)
    lo = jnp.arange(low, dtype=jnp.int32)
    phase_hi = (chosen[:, None] * (hi[None, :] * low)) % channels
    phase_lo = (chosen[:, None] * lo[None, :]) % channels
    angle_hi = phase_hi.astype(jnp.float32) * step
    angle_lo = phase_lo.astype(jnp.float32) * step
    c1, s1 = jnp.cos(angle_hi)[:, :, None], jnp.sin(angle_hi)[:, :, None]
    c2, s2 = jnp.cos(angle_lo)[:, None, :], jnp.sin(angle_lo)[:, None, :]
    factor = 1.0 / math.sqrt(channels)
    keep = jnp.where(present, factor, 0.0).astype(jnp.float32)[:, None, None]
    cos_rows = ((c1 * c2 - s1 * s2) * keep).reshape(-1, channels)
    sin_rows = ((s1 * c2 + c1 * s2) * keep).reshape(-1, channels)
    return jnp.stack([cos_rows, sin_rows]).astype(jnp.bfloat16)


def local(voltages, filter_taps, flagged, owners):
    inp_dev = voltages.shape[0]
    spec_dev = voltages.shape[1]
    channels = voltages.shape[3]
    halo_depth = filter_taps.shape[0] - 1
    tail_block = voltages[:, spec_dev - halo_depth :]
    before = from_behind(tail_block, "tm", 1)
    joined = jnp.concatenate([before, voltages], axis=1).transpose(2, 0, 1, 3)
    running = jnp.zeros((2, inp_dev, spec_dev, channels), jnp.float32)
    for tap_index in range(halo_depth + 1):
        start_row = halo_depth - tap_index
        running = running + filter_taps[tap_index][None, None, None, :] * joined[
            :, :, start_row : start_row + spec_dev
        ].astype(jnp.float32)
    filtered = running.astype(jnp.bfloat16)

    chan_count = lax.axis_size("chan")
    time_count = lax.axis_size("tm")
    devices = chan_count * time_count
    capacity = channels // devices
    chosen, present = slot_table(flagged, owners, channels, capacity)
    tables = slot_tables(chosen, present, channels)
    parts = jnp.einsum("qsn,pitn->qspit", tables, filtered, preferred_element_type=jnp.float32)
    real_part = parts[0, :, 0] + parts[1, :, 1]
    imag_part = parts[0, :, 1] - parts[1, :, 0]
    spectra = jnp.stack([real_part, imag_part], axis=1).astype(jnp.bfloat16)
    sending = spectra.reshape(devices, capacity, 2, inp_dev, spec_dev)
    received = lax.all_to_all(sending, ("chan", "tm"), 0, 0, tiled=True)
    slots = received.reshape(chan_count, time_count, capacity, 2, inp_dev, spec_dev)
    slots = slots.transpose(2, 3, 0, 4, 1, 5).reshape(
        capacity, 2, chan_count * inp_dev, time_count * spec_dev
    )
    spec_all = time_count * spec_dev
    slot_real = slots[:, 0]
    slot_imag = slots[:, 1]
    first_rows = jnp.concatenate([slot_real, slot_imag], axis=-1)
    second_rows = jnp.concatenate([slot_imag, -slot_real], axis=-1)
    stacked_rows = jnp.stack([first_rows, second_rows], axis=1)
    visibility = jnp.einsum(
        "cpit,cjt->cpij", stacked_rows, first_rows, preferred_element_type=jnp.float32
    )
    return visibility / spec_all


def solution(mesh):
    return jax.shard_map(
        local,
        mesh=mesh,
        in_specs=(P("chan", "tm", None, None), P(), P(), P()),
        out_specs=P(("chan", "tm"), None, None, None),
        check_vma=False,
    )
```

profile of v0, /device:TPU:1, one launch (start us, length us, event | category | flops | bytes accessed | tf_op | source)
XLA Modules:
  0.0 108.5 jit_solution(17370486922327573479)
XLA Ops:
  0.0 1.1 %copy.41 = bf16[4,32,2,1024]{3,1,0,2:T(8,128)(2,1)S(1)} copy(bf16[4,32,2,1024]{3,2,1,0:T(2,128)(2,1)} %param.4) | data formatting | bytes 1048576 | tf_op args[0]
  1.2 0.1 slice.124
  1.2 3.9 %collective-permute-start = (bf16[4,11,2,1024]{3,1,0,2:T(8,128)(2,1)S(1)}, bf16[4,11,2,1024]{3,1,0,2:T(8,128)(2,1)S(1)}, u32[]{:S(2)}, u32[]{:S(2)}) collective-permute-start(bf16[4,11,2,1024]{3,1,0,2:T(8,128)(2,1)S(1)} %slice.124), channel_id=1, source_target_pairs={{0,1},{1,2},{2,3},{4,5},{5,6},{6,7},{8,9},{9,10},{10,11},{12,13},{... | collective-permute-start | bytes 540680 | tf_op jit(solution)/shard_map/ppermute | solution.py:12
  5.2 0.9 fusion.7
  6.1 1.4 %convert_reduce_fusion = s32[1024]{0:T(1024)S(1)} fusion(s32[1024]{0:T(1024)} %param.7, pred[1024]{0:T(1024)(128)(4,1)S(1)} %not.7), kind=kLoop, calls=%fused_computation.10 | loop fusion | flops 6290432 | bytes 9216 | tf_op jit(solution)/shard_map/reduce_sum | solution.py:23
  7.5 0.7 multiply_add_fusion.1
  8.2 0.9 select_reduce_fusion
  9.1 0.6 fusion.5
  9.7 1.1 fusion.36
  10.8 4.5 %multiply_subtract_fusion = (f32[1024,32,32]{0,2,1:T(8,128)}, f32[1024,32,32]{0,2,1:T(8,128)}) fusion(f32[1024,32]{0,1:T(8,128)S(1)} %get-tuple-element.29, f32[1024,32]{0,1:T(8,128)S(1)} %get-tuple-element.26, f32[1024,32]{0,1:T(8,128)S(1)} %get-tuple-element.30, f32[1024,32]{0,1:T(8,128)S(1)} %get-tuple-element.25), kind=kLoop, calls=%fused_computation.7 | loop fusion | flops 6291456 | bytes 8912896 | tf_op jit(solution)/shard_map/sub | solution.py:45
  15.3 5.3 %copy.39 = f32[1,1024,1024]{2,1,0:T(8,128)} copy(f32[1,1024,1024]{1,2,0:T(8,128)} %bitcast.53) | data formatting | bytes 8388608 | tf_op jit(solution)/shard_map/sub | solution.py:45
  20.7 5.3 %copy.40 = f32[1,1024,1024]{2,1,0:T(8,128)} copy(f32[1,1024,1024]{1,2,0:T(8,128)} %bitcast.52) | data formatting | bytes 8388608 | tf_op jit(solution)/shard_map/add | solution.py:46
  26.0 0.0 copy-start
  26.0 4.0 %multiply_convert_fusion.1 = (bf16[1,1024,1024]{2,1,0:T(8,128)(2,1)S(1)}, bf16[1,1024,1024]{2,1,0:T(8,128)(2,1)S(1)}) fusion(f32[1,1024,1024]{2,1,0:T(8,128)} %copy.39, f32[1024]{0:T(1024)S(1)} %broadcast_select_fusion, f32[1,1024,1024]{2,1,0:T(8,128)} %copy.40), kind=kLoop, calls=%fused_computation.6 | loop fusion | flops 4194304 | bytes 12587008 | tf_op jit(solution)/shard_map/convert.4
  30.0 0.0 copy-done
  30.1 0.0 collective-permute-done
  30.1 0.2 maximum_bitcast_fusion.2
  30.3 2.5 %fusion = f32[2,1024,2,4,32]{1,4,3,2,0:T(8,128)S(1)} fusion(bf16[1,1024,1024]{2,1,0:T(8,128)(2,1)S(1)} %get-tuple-element.28, bf16[1,1024,1024]{2,1,0:T(8,128)(2,1)S(1)} %get-tuple-element.27, bf16[2,4,43,1024]{3,2,1,0:T(8,128)(2,1)S(1)} %maximum_bitcast_fusion.2, f32[1024]{0:T(1024)S(1)} %bitcast.68, f32[1024]{0:T(1024)S(1)} %bitcast.69, ...), kind=kOutput, calls=%fused_computation.1 | convolution fusion | flops 1091567616 | bytes 12632064 | tf_op jit(solution)/shard_map/qsn,pitn->qspit/dot_general | solution.py:72
  32.7 0.1 fusion.9
  32.9 0.5 copy.43
  33.4 1.3 %copy.44 = bf16[1,1024,1,4,32]{4,1,3,2,0:T(8,128)(2,1)} copy(bf16[1,1024,1,4,32]{1,4,3,2,0:T(8,128)(2,1)S(1)} %get-tuple-element.6) | data formatting | bytes 524288 | tf_op jit(solution)/shard_map/convert.2
  34.7 3.9 %copy_bitcast_fusion.1 = bf16[512,2,4,2,32]{4,3,2,1,0:T(2,128)(2,1)S(1)} fusion(bf16[512,2,1,4,32]{4,1,0,3,2:T(2,128)(2,1)} %bitcast.57, bf16[512,2,1,4,32]{4,1,0,3,2:T(2,128)(2,1)S(1)} %bitcast.56), kind=kLoop, calls=%fused_computation.74 | loop fusion | flops 262144 | bytes 1048576
  38.6 1.4 %reshape.320 = bf16[512,2,256]{2,1,0:T(2,128)(2,1)S(1)} reshape(bf16[512,2,4,2,32]{4,3,2,1,0:T(2,128)(2,1)S(1)} %copy_bitcast_fusion.1) | data formatting | bytes 1048576
  39.9 59.4 %all_to_all.5 = bf16[512,2,256]{2,1,0:T(2,128)(2,1)S(1)} all-to-all(bf16[512,2,256]{2,1,0:T(2,128)(2,1)S(1)} %reshape.320), channel_id=1, replica_groups=mesh['chan'=128,'tm'=4] {'chan','tm'}, dimensions={0} | all-to-all | bytes 1048576 | tf_op jit(solution)/shard_map/all_to_all | solution.py:77
  99.3 1.0 reshape.321
  100.4 2.1 %copy.58 = bf16[128,4,2,2,4,32]{5,1,4,0,3,2:T(4,128)(2,1)} copy(bf16[128,4,2,2,4,32]{5,2,4,3,1,0:T(2,128)(2,1)S(1)} %bitcast.54) | data formatting | bytes 1048576 | tf_op jit(solution)/shard_map/reshape | solution.py:78
  102.5 3.1 %reshape.316 = bf16[2,2,512,128]{3,2,1,0:T(8,128)(2,1)S(1)} reshape(bf16[2,2,128,4,4,32]{5,4,3,2,1,0:T(4,128)(2,1)} %bitcast.55) | data formatting | bytes 1048576 | tf_op jit(solution)/shard_map/reshape | solution.py:79
  105.6 0.1 fusion.23
  105.8 2.8 %convolution_multiply_fusion = f32[2,2,512,512]{3,2,1,0:T(8,128)} fusion(bf16[2,512,128]{2,1,0:T(8,128)(2,1)S(1)} %get-tuple-element.8, bf16[2,512,128]{2,1,0:T(8,128)(2,1)S(1)} %get-tuple-element.7, bf16[2,1,512,256]{3,2,0,1:T(8,128)(2,1)S(1)} %get-tuple-element.12, bf16[2,1,512,256]{3,2,0,1:T(8,128)(2,1)S(1)} %get-tuple-element.11), kind=kOutput, calls=%fused_computation.15 | convolution fusion | flops 539492352 | bytes 5767168 | tf_op jit(solution)/shard_map/cpit,cjt->cpij/dot_general | solution.py:88
  (6 shorter events, 0.1 us)
Async XLA Ops:
  1.2 28.8 %collective-permute-start = (bf16[4,11,2,1024]{3,1,0,2:T(8,128)(2,1)S(1)}, bf16[4,11,2,1024]{3,1,0,2:T(8,128)(2,1)S(1)}, u32[]{:S(2)}, u32[]{:S(2)}) collective-permute-start(bf16[4,11,2,1024]{3,1,0,2:T(8,128)(2,1)S(1)} %slice.124), channel_id=1, source_target_pairs={{0,1},{1,2},{2,3},{4,5},{5,6},{6,7},{8,9},{9,10},{10,11},{12,13},{... | collective-permute-start | bytes 540680 | tf_op jit(solution)/shard_map/ppermute | solution.py:12
  26.0 4.0 %copy-start = (f32[12,1024]{1,0:T(8,128)S(1)}, f32[12,1024]{1,0:T(8,128)}, u32[]{:S(2)}) copy-start(f32[12,1024]{1,0:T(8,128)} %param.5) | copy-start | bytes 147460
where the time goes:
time: 109 us
  blocking collectives  59.4 us (54%)
  local copies, waits for them, and re-layouts  21.4 us (20%)
  other arithmetic  18.4 us (17%)
  matrix products  5.21 us (5%)
  starting transfers between devices  3.95 us (4%)
    all_to_all x1, blocking collectives, local(): received = lax.all_to_all(sending, ('chan', 'tm'), 0, 0, tiled=True)  59.4 us
    sub x1, local copies, waits for them, and re-layouts, slot_tables(): cos_rows = ((c1 * c2 - s1 * s2) * keep).reshape(-1, channels)  5.34 us
    add x1, local copies, waits for them, and re-layouts, slot_tables(): sin_rows = ((s1 * c2 + c1 * s2) * keep).reshape(-1, channels)  5.34 us
    sub x1, other arithmetic, slot_tables(): cos_rows = ((c1 * c2 - s1 * s2) * keep).reshape(-1, channels)  4.53 us
    another operation x2, other arithmetic  4.14 us
    ppermute x1, starting transfers between devices, from_behind(): return lax.ppermute(value, axis, pairs)  3.95 us
    unnamed x1, other arithmetic  3.88 us
    unnamed x5, local copies, waits for them, and re-layouts  3.57 us
  transfers between devices with their start and end apart: 1, of which 0 were waited for; matrix products, arithmetic and copies ran while one was open for 23% of the time, Pallas kernels for 0%

commit v1 on v0

--- a/solution.py
+++ b/solution.py
@@ -34,17 +34,15 @@
     step = 2.0 * math.pi / channels
     hi = jnp.arange(high, dtype=jnp.int32)
     lo = jnp.arange(low, dtype=jnp.int32)
-    phase_hi = (chosen[:, None] * (hi[None, :] * low)) % channels
-    phase_lo = (chosen[:, None] * lo[None, :]) % channels
-    angle_hi = phase_hi.astype(jnp.float32) * step
-    angle_lo = phase_lo.astype(jnp.float32) * step
-    c1, s1 = jnp.cos(angle_hi)[:, :, None], jnp.sin(angle_hi)[:, :, None]
-    c2, s2 = jnp.cos(angle_lo)[:, None, :], jnp.sin(angle_lo)[:, None, :]
+    angle_hi = ((hi[:, None] * low * chosen[None, :]) % channels).astype(jnp.float32) * step
+    angle_lo = ((lo[:, None] * chosen[None, :]) % channels).astype(jnp.float32) * step
+    c1, s1 = jnp.cos(angle_hi)[:, None, :], jnp.sin(angle_hi)[:, None, :]
+    c2, s2 = jnp.cos(angle_lo)[None, :, :], jnp.sin(angle_lo)[None, :, :]
     factor = 1.0 / math.sqrt(channels)
-    keep = jnp.where(present, factor, 0.0).astype(jnp.float32)[:, None, None]
-    cos_rows = ((c1 * c2 - s1 * s2) * keep).reshape(-1, channels)
-    sin_rows = ((s1 * c2 + c1 * s2) * keep).reshape(-1, channels)
-    return jnp.stack([cos_rows, sin_rows]).astype(jnp.bfloat16)
+    keep = jnp.where(present, factor, 0.0).astype(jnp.float32)[None, None, :]
+    cos_rows = ((c1 * c2 - s1 * s2) * keep).reshape(channels, -1)
+    sin_rows = ((s1 * c2 + c1 * s2) * keep).reshape(channels, -1)
+    return cos_rows.astype(jnp.bfloat16), sin_rows.astype(jnp.bfloat16)
 
 
 def local(voltages, filter_taps, flagged, owners):
@@ -61,34 +59,35 @@
         running = running + filter_taps[tap_index][None, None, None, :] * joined[
             :, :, start_row : start_row + spec_dev
         ].astype(jnp.float32)
-    filtered = running.astype(jnp.bfloat16)
+    filtered = running.astype(jnp.bfloat16).reshape(2, inp_dev * spec_dev, channels)
 
     chan_count = lax.axis_size("chan")
     time_count = lax.axis_size("tm")
     devices = chan_count * time_count
     capacity = channels // devices
     chosen, present = slot_table(flagged, owners, channels, capacity)
-    tables = slot_tables(chosen, present, channels)
-    parts = jnp.einsum("qsn,pitn->qspit", tables, filtered, preferred_element_type=jnp.float32)
-    real_part = parts[0, :, 0] + parts[1, :, 1]
-    imag_part = parts[0, :, 1] - parts[1, :, 0]
+    cos_rows, sin_rows = slot_tables(chosen, present, channels)
+    dims = (((0,), (2,)), ((), ()))
+    cos_part = lax.dot_general(cos_rows, filtered, dims, preferred_element_type=jnp.float32)
+    sin_part = lax.dot_general(sin_rows, filtered, dims, preferred_element_type=jnp.float32)
+    real_part = cos_part[:, 0] + sin_part[:, 1]
+    imag_part = cos_part[:, 1] - sin_part[:, 0]
     spectra = jnp.stack([real_part, imag_part], axis=1).astype(jnp.bfloat16)
-    sending = spectra.reshape(devices, capacity, 2, inp_dev, spec_dev)
+    rows = inp_dev * spec_dev
+    sending = spectra.reshape(devices, capacity * 2 * rows)
     received = lax.all_to_all(sending, ("chan", "tm"), 0, 0, tiled=True)
     slots = received.reshape(chan_count, time_count, capacity, 2, inp_dev, spec_dev)
-    slots = slots.transpose(2, 3, 0, 4, 1, 5).reshape(
-        capacity, 2, chan_count * inp_dev, time_count * spec_dev
+    first_rows = slots.transpose(2, 0, 4, 3, 1, 5).reshape(
+        capacity, chan_count * inp_dev, 2, time_count * spec_dev
     )
-    spec_all = time_count * spec_dev
-    slot_real = slots[:, 0]
-    slot_imag = slots[:, 1]
-    first_rows = jnp.concatenate([slot_real, slot_imag], axis=-1)
-    second_rows = jnp.concatenate([slot_imag, -slot_real], axis=-1)
+    second_rows = jnp.stack([first_rows[:, :, 1], -first_rows[:, :, 0]], axis=2)
+    first_rows = first_rows.reshape(capacity, chan_count * inp_dev, -1)
+    second_rows = second_rows.reshape(capacity, chan_count * inp_dev, -1)
     stacked_rows = jnp.stack([first_rows, second_rows], axis=1)
     visibility = jnp.einsum(
         "cpit,cjt->cpij", stacked_rows, first_rows, preferred_element_type=jnp.float32
     )
-    return visibility / spec_all
+    return visibility / (time_count * spec_dev)
 
 
 def solution(mesh):

time: 109 us -> 103 us (0.945)
  other arithmetic: 18.4 us -> 16 us
  local copies, waits for them, and re-layouts: 21.4 us -> 19.2 us
    another operation x2 -> x5, local copies, waits for them, and re-layouts: 1.8 us -> 9.27 us  [the longest x1 4.22 us: local(): first_rows = first_rows.reshape(capacity, chan_count * inp_dev, -1)]
    convert_element_type x0 -> x3, other arithmetic: none -> 6.83 us  [the longest x1 3.82 us: local(): spectra = jnp.stack([real_part, imag_part], axis=1).astype(jnp.bfloat16)]
    sub x1 -> x0, local copies, waits for them, and re-layouts: 5.34 us -> none  [slot_tables(): cos_rows = ((c1 * c2 - s1 * s2) * keep).reshape(-1, channels)]
    add x1 -> x0, local copies, waits for them, and re-layouts: 5.34 us -> none  [slot_tables(): sin_rows = ((s1 * c2 + c1 * s2) * keep).reshape(-1, channels)]
    transpose x0 -> x2, local copies, waits for them, and re-layouts: none -> 4.83 us  [local(): slots.transpose(2, 0, 4, 3, 1, 5)]
    sub x1 -> x0, other arithmetic: 4.53 us -> none  [slot_tables(): cos_rows = ((c1 * c2 - s1 * s2) * keep).reshape(-1, channels)]
    another operation x3, other arithmetic: 4.24 us -> 0.21 us
    unnamed x1 -> x0, other arithmetic: 3.88 us -> none
  transfers between devices with their start and end apart: 1 -> 1, of which waited for: 0 -> 0; matrix products, arithmetic and copies ran while one was open for 23% -> 7% of each run, Pallas kernels for 0% -> 0%
where the time goes in v1:
time: 103 us
  blocking collectives  59.4 us (58%)
  local copies, waits for them, and re-layouts  19.2 us (19%)
  other arithmetic  16 us (16%)
  matrix products  4.27 us (4%)
  starting transfers between devices  3.95 us (4%)
    all_to_all x1, blocking collectives, local(): received = lax.all_to_all(sending, ('chan', 'tm'), 0, 0, tiled=True)  59.4 us
    transpose x2, local copies, waits for them, and re-layouts, local(): slots.transpose(2, 0, 4, 3, 1, 5)  4.83 us
    another operation x1, local copies, waits for them, and re-layouts, local(): first_rows = first_rows.reshape(capacity, chan_count * inp_dev, -1)  4.22 us
    another operation x2, local copies, waits for them, and re-layouts, local(): stacked_rows = jnp.stack([first_rows, second_rows], axis=1)  3.97 us
    ppermute x1, starting transfers between devices, from_behind(): return lax.ppermute(value, axis, pairs)  3.95 us
    convert_element_type x1, other arithmetic, local(): spectra = jnp.stack([real_part, imag_part], axis=1).astype(jnp.bfloat16)  3.82 us
    all_to_all x1, other arithmetic, local(): received = lax.all_to_all(sending, ('chan', 'tm'), 0, 0, tiled=True)  3.18 us
    dot_general x1, matrix products, local(): jnp.einsum('cpit,cjt->cpij', stacked_rows, first_rows, preferred_element_...  2.75 us
  transfers between devices with their start and end apart: 1, of which 0 were waited for; matrix products, arithmetic and copies ran while one was open for 7% of the time, Pallas kernels for 0%

profile of v1, /device:TPU:1, one launch (start us, length us, event | category | flops | bytes accessed | tf_op | source)
XLA Modules:
  0.0 103.0 jit_solution(9314261974188897340)
XLA Ops:
  0.0 1.2 %copy.39 = bf16[4,32,2,1024]{3,1,0,2:T(8,128)(2,1)S(1)} copy(bf16[4,32,2,1024]{3,2,1,0:T(2,128)(2,1)} %param.4) | data formatting | bytes 1048576 | tf_op args[0]
  1.2 0.1 slice.124
  1.3 3.9 %collective-permute-start = (bf16[4,11,2,1024]{3,1,0,2:T(8,128)(2,1)S(1)}, bf16[4,11,2,1024]{3,1,0,2:T(8,128)(2,1)S(1)}, u32[]{:S(2)}, u32[]{:S(2)}) collective-permute-start(bf16[4,11,2,1024]{3,1,0,2:T(8,128)(2,1)S(1)} %slice.124), channel_id=1, source_target_pairs={{0,1},{1,2},{2,3},{4,5},{5,6},{6,7},{8,9},{9,10},{10,11},{12,13},{... | collective-permute-start | bytes 540680 | tf_op jit(solution)/shard_map/ppermute | solution.py:12
  5.2 0.9 fusion.6
  6.1 1.4 %convert_reduce_fusion = s32[1024]{0:T(1024)S(1)} fusion(s32[1024]{0:T(1024)} %param.7, pred[1024]{0:T(1024)(128)(4,1)S(1)} %not.7), kind=kLoop, calls=%fused_computation.4 | loop fusion | flops 6290432 | bytes 9216 | tf_op jit(solution)/shard_map/reduce_sum | solution.py:23
  7.5 0.7 multiply_add_fusion
  8.2 0.9 select_reduce_fusion
  9.1 0.6 fusion.2
  9.8 1.1 %fusion.22 = (f32[32,1024]{1,0:T(8,128)S(1)}, f32[32,1024]{1,0:T(8,128)S(1)}, f32[32,1024]{1,0:T(8,128)S(1)}, f32[32,1024]{1,0:T(8,128)S(1)}) fusion(s32[1024]{0:T(1024)S(1)} %select_reduce_fusion, s32[32]{0:T(128)S(1)} %iota_multiply_fusion), kind=kLoop, calls=%fused_computation.45 | loop fusion | flops 917504 | bytes 528512 | tf_op jit(solution)/shard_map/cos | solution.py:39
  10.8 1.4 %multiply_convert_fusion.1 = (bf16[32,32,1024]{2,1,0:T(8,128)(2,1)S(1)}, bf16[32,32,1024]{2,1,0:T(8,128)(2,1)S(1)}) fusion(f32[1024]{0:T(1024)S(1)} %broadcast_select_fusion, f32[32,1024]{1,0:T(8,128)S(1)} %get-tuple-element.25, f32[32,1024]{1,0:T(8,128)S(1)} %get-tuple-element.24, f32[32,1024]{1,0:T(8,128)S(1)} %get-tuple-element.26, ...), kind=kLoop, calls=%fused_computation.1 | loop fusion | flops 10485760 | bytes 4722688 | tf_op jit(solution)/shard_map/convert_element_type | solution.py:45
  12.3 0.2 maximum_bitcast_fusion
  12.5 1.6 %add_convert_fusion = bf16[2,4,32,1024]{3,2,1,0:T(8,128)(2,1)S(1)} fusion(bf16[2,4,43,1024]{3,2,1,0:T(8,128)(2,1)S(1)} %maximum_bitcast_fusion, f32[1024]{0:T(1024)S(1)} %bitcast.49, f32[1024]{0:T(1024)S(1)} %bitcast.50, f32[1024]{0:T(1024)S(1)} %bitcast.40, f32[1024]{0:T(1024)S(1)} %bitcast.41, f32[1024]{0:T(1024)S(1)} %bitcast.42, f32[1024]{0:T(1024)S(1)} %bitcast.43, ...), kind=kLoop, calls=%fused_computation.13 | loop fusion | flops 9437184 | bytes 6864896 | tf_op jit(solution)/shard_map/convert_element_type | solution.py:62
  14.1 0.8 fusion.26
  14.9 0.8 fusion.27
  15.6 0.1 fusion.8
  15.8 0.5 copy.43
  16.4 0.4 convert_element_type.119
  16.8 0.5 broadcast.266
  17.3 3.8 %reduce.1 = bf16[512,512]{1,0:T(8,128)(2,1)S(1)} reduce(bf16[512,1,512]{2,1,0:T(2,128)(2,1)S(1)} %convert_element_type.119, bf16[]{:T(256)} %broadcast.266), dimensions={1}, to_apply=%convert_element_type.119.reduce_sub_computation | reduce | bytes 1048578 | tf_op jit(solution)/shard_map/convert_element_type | solution.py:75
  21.2 0.1 reshape.245
  21.3 59.4 %all_to_all.6 = bf16[512,2,256]{2,1,0:T(2,128)(2,1)S(1)} all-to-all(bf16[512,2,256]{2,1,0:T(2,128)(2,1)S(1)} %reshape.245), channel_id=1, replica_groups=mesh['chan'=128,'tm'=4] {'chan','tm'}, dimensions={0} | all-to-all | bytes 1048576 | tf_op jit(solution)/shard_map/all_to_all | solution.py:78
  80.7 0.4 reshape.246
  81.1 3.2 %reduce = bf16[512,512]{1,0:T(8,128)(2,1)S(1)} reduce(bf16[512,1,512]{2,1,0:T(2,128)(2,1)S(1)} %reshape.246, bf16[]{:T(256)} %constant.37), dimensions={1}, to_apply=%all_to_all.4.reduce_sub_computation | reduce | bytes 1048578 | tf_op jit(solution)/shard_map/all_to_all | solution.py:78
  84.3 1.2 %reshape.238 = bf16[128,4,2,2,4,32]{5,4,3,2,1,0:T(4,128)(2,1)S(1)} reshape(bf16[512,512]{1,0:T(8,128)(2,1)S(1)} %reduce) | data formatting | bytes 1048576 | tf_op jit(solution)/shard_map/reshape | solution.py:79
  85.5 2.4 %copy.46 = bf16[2,128,4,2,4,32]{5,4,2,1,3,0:T(4,128)(2,1)} copy(bf16[2,128,4,2,4,32]{5,2,3,0,4,1:T(4,128)(2,1)S(1)} %bitcast.32) | data formatting | bytes 1048576 | tf_op jit(solution)/shard_map/transpose | solution.py:80
  87.9 2.4 %copy.45 = bf16[2,128,4,2,4,32]{5,4,3,2,1,0:T(4,128)(2,1)} copy(bf16[2,128,4,2,4,32]{5,2,3,0,4,1:T(4,128)(2,1)S(1)} %bitcast.33) | data formatting | bytes 1048576 | tf_op jit(solution)/shard_map/transpose | solution.py:80
  90.3 3.6 %stack_reshape_reshape.3 = bf16[2,1,512,256]{3,2,0,1:T(8,128)(2,1)S(1)} reshape(bf16[2,128,4,2,4,32]{5,4,3,2,1,0:T(4,128)(2,1)} %copy.45) | data formatting | bytes 1048576 | tf_op jit(solution)/shard_map/stack;reshape;reshape | solution.py:86
  94.0 4.2 %reshape.242 = bf16[2,512,256,1]{2,1,0,3:T(8,128)(2,1)} reshape(bf16[2,128,4,2,4,32]{5,4,3,2,1,0:T(4,128)(2,1)} %copy.45) | data formatting | bytes 1048576 | tf_op jit(solution)/shard_map/reshape;reshape | solution.py:84
  98.2 1.0 %reshape.239 = bf16[2,512,2,128]{3,1,2,0:T(8,128)(2,1)S(1)} reshape(bf16[2,128,4,2,4,32]{5,4,2,1,3,0:T(4,128)(2,1)S(1)} %copy-done) | data formatting | bytes 1048576 | tf_op jit(solution)/shard_map/reshape | solution.py:80
  99.4 0.5 copy.47
  99.9 0.3 stack_reshape.3
  100.3 2.8 %convolution_multiply_fusion = f32[2,2,512,512]{3,2,1,0:T(8,128)} fusion(bf16[2,1,512,256]{3,2,1,0:T(8,128)(2,1)S(1)} %stack_reshape.3, bf16[2,1,512,256]{3,2,1,0:T(8,128)(2,1)S(1)} %bitcast.36, bf16[2,512,256,1]{2,1,0,3:T(8,128)(2,1)S(1)} %copy-done.1), kind=kOutput, calls=%fused_computation.9 | convolution fusion | flops 538443776 | bytes 5767168 | tf_op jit(solution)/shard_map/cpit,cjt->cpij/dot_general | solution.py:87
  (14 shorter events, 0.2 us)
Async XLA Ops:
  0.0 12.3 %copy-start.2 = (f32[12,1024]{1,0:T(8,128)S(1)}, f32[12,1024]{1,0:T(8,128)}, u32[]{:S(2)}) copy-start(f32[12,1024]{1,0:T(8,128)} %param.5) | copy-start | bytes 147460
  1.3 11.1 %collective-permute-start = (bf16[4,11,2,1024]{3,1,0,2:T(8,128)(2,1)S(1)}, bf16[4,11,2,1024]{3,1,0,2:T(8,128)(2,1)S(1)}, u32[]{:S(2)}, u32[]{:S(2)}) collective-permute-start(bf16[4,11,2,1024]{3,1,0,2:T(8,128)(2,1)S(1)} %slice.124), channel_id=1, source_target_pairs={{0,1},{1,2},{2,3},{4,5},{5,6},{6,7},{8,9},{9,10},{10,11},{12,13},{... | collective-permute-start | bytes 540680 | tf_op jit(solution)/shard_map/ppermute | solution.py:12
  90.3 7.9 %copy-start = (bf16[2,128,4,2,4,32]{5,4,2,1,3,0:T(4,128)(2,1)S(1)}, bf16[2,128,4,2,4,32]{5,4,2,1,3,0:T(4,128)(2,1)}, u32[]{:S(2)}) copy-start(bf16[2,128,4,2,4,32]{5,4,2,1,3,0:T(4,128)(2,1)} %copy.46) | copy-start | bytes 1572868
  99.3 1.0 %copy-start.1 = (bf16[2,512,256,1]{2,1,0,3:T(8,128)(2,1)S(1)}, bf16[2,512,256,1]{2,1,0,3:T(8,128)(2,1)}, u32[]{:S(2)}) copy-start(bf16[2,512,256,1]{2,1,0,3:T(8,128)(2,1)} %reshape.242) | copy-start | bytes 1572868

commit v2 on v1

--- a/solution.py
+++ b/solution.py
@@ -1,8 +1,11 @@
+import functools
 import math
 
 import jax
 import jax.numpy as jnp
 from jax import lax
+from jax.experimental import pallas as pl
+from jax.experimental.pallas import tpu as pltpu
 from jax.sharding import PartitionSpec as P
 
 
@@ -45,6 +48,39 @@
     return cos_rows.astype(jnp.bfloat16), sin_rows.astype(jnp.bfloat16)
 
 
+def dft_kernel(x_ref, c0_ref, c1_ref, s0_ref, s1_ref, o_ref):
+    x = x_ref[...]
+    half = x.shape[0] // 2
+    for cap, (c_ref, s_ref) in enumerate(((c0_ref, s0_ref), (c1_ref, s1_ref))):
+        cos_part = jnp.dot(x, c_ref[...], preferred_element_type=jnp.float32)
+        sin_part = jnp.dot(x, s_ref[...], preferred_element_type=jnp.float32)
+        real_part = cos_part[:half] + sin_part[half:]
+        imag_part = cos_part[half:] - sin_part[:half]
+        o_ref[:, 2 * cap, :] = real_part.T.astype(o_ref.dtype)
+        o_ref[:, 2 * cap + 1, :] = imag_part.T.astype(o_ref.dtype)
+
+
+def dft_payload(filtered, cos_rows, sin_rows, devices, capacity):
+    channels = filtered.shape[1]
+    rows = filtered.shape[0] // 2
+    block = 128
+    steps = devices // block
+    table_spec = lambda cap: pl.BlockSpec((channels, block), lambda j: (0, j + cap * steps))
+    return pl.pallas_call(
+        dft_kernel,
+        grid=(steps,),
+        in_specs=[
+            pl.BlockSpec((2 * rows, channels), lambda j: (0, 0)),
+            table_spec(0),
+            table_spec(1),
+            table_spec(0),
+            table_spec(1),
+        ],
+        out_specs=pl.BlockSpec((block, capacity * 2, rows), lambda j: (j, 0, 0)),
+        out_shape=jax.ShapeDtypeStruct((devices, capacity * 2, rows), jnp.bfloat16),
+    )(filtered, cos_rows, cos_rows, sin_rows, sin_rows)
+
+
 def local(voltages, filter_taps, flagged, owners):
     inp_dev = voltages.shape[0]
     spec_dev = voltages.shape[1]
@@ -59,35 +95,67 @@
         running = running + filter_taps[tap_index][None, None, None, :] * joined[
             :, :, start_row : start_row + spec_dev
         ].astype(jnp.float32)
-    filtered = running.astype(jnp.bfloat16).reshape(2, inp_dev * spec_dev, channels)
+    filtered = running.astype(jnp.bfloat16).reshape(2 * inp_dev * spec_dev, channels)
 
     chan_count = lax.axis_size("chan")
     time_count = lax.axis_size("tm")
     devices = chan_count * time_count
     capacity = channels // devices
     chosen, present = slot_table(flagged, owners, channels, capacity)
+    chosen = chosen.reshape(chan_count, time_count, capacity).transpose(2, 1, 0).reshape(-1)
+    present = present.reshape(chan_count, time_count, capacity).transpose(2, 1, 0).reshape(-1)
     cos_rows, sin_rows = slot_tables(chosen, present, channels)
-    dims = (((0,), (2,)), ((), ()))
-    cos_part = lax.dot_general(cos_rows, filtered, dims, preferred_element_type=jnp.float32)
-    sin_part = lax.dot_general(sin_rows, filtered, dims, preferred_element_type=jnp.float32)
-    real_part = cos_part[:, 0] + sin_part[:, 1]
-    imag_part = cos_part[:, 1] - sin_part[:, 0]
-    spectra = jnp.stack([real_part, imag_part], axis=1).astype(jnp.bfloat16)
-    rows = inp_dev * spec_dev
-    sending = spectra.reshape(devices, capacity * 2 * rows)
-    received = lax.all_to_all(sending, ("chan", "tm"), 0, 0, tiled=True)
-    slots = received.reshape(chan_count, time_count, capacity, 2, inp_dev, spec_dev)
-    first_rows = slots.transpose(2, 0, 4, 3, 1, 5).reshape(
-        capacity, chan_count * inp_dev, 2, time_count * spec_dev
-    )
-    second_rows = jnp.stack([first_rows[:, :, 1], -first_rows[:, :, 0]], axis=2)
-    first_rows = first_rows.reshape(capacity, chan_count * inp_dev, -1)
-    second_rows = second_rows.reshape(capacity, chan_count * inp_dev, -1)
-    stacked_rows = jnp.stack([first_rows, second_rows], axis=1)
-    visibility = jnp.einsum(
-        "cpit,cjt->cpij", stacked_rows, first_rows, preferred_element_type=jnp.float32
-    )
-    return visibility / (time_count * spec_dev)
+    sending = dft_payload(filtered, cos_rows, sin_rows, devices, capacity)
+    received = lax.all_to_all(sending, ("tm", "chan"), 0, 0, tiled=True)
+    return correlate(received, time_count, chan_count, capacity, inp_dev)
+
+
+def correlate_kernel(r_ref, o_ref, xt_ref, *, time_count, inp_dev, caps):
+    for cap in range(caps):
+        pl.when(pl.program_id(0) == cap)(
+            functools.partial(correlate_slot, r_ref, o_ref, xt_ref, cap, time_count, inp_dev)
+        )
+
+
+def correlate_slot(r_ref, o_ref, xt_ref, cap, time_count, inp_dev):
+    chans = r_ref.shape[0] // time_count
+    spec_dev = r_ref.shape[2] // inp_dev
+    for reim in range(2):
+        for tm in range(time_count):
+            piece = r_ref[pl.ds(tm * chans, chans), cap * 2 + reim, :]
+            block = piece.astype(jnp.float32).T
+            row = (reim * time_count + tm) * spec_dev
+            for i in range(inp_dev):
+                xt_ref[row : row + spec_dev, i * chans : (i + 1) * chans] = block[
+                    i * spec_dev : (i + 1) * spec_dev
+                ]
+    inputs = inp_dev * chans
+    rows = lax.broadcasted_iota(jnp.int32, (inputs, inputs), 0)
+    cols = lax.broadcasted_iota(jnp.int32, (inputs, inputs), 1)
+    perm = (cols == (rows % inp_dev) * chans + rows // inp_dev).astype(jnp.bfloat16)
+    nt = (((1,), (1,)), ((), ()))
+    xt = xt_ref[...].astype(jnp.bfloat16)
+    x = lax.dot_general(perm, xt, nt, preferred_element_type=jnp.float32).astype(jnp.bfloat16)
+    half = x.shape[1] // 2
+    x2 = jnp.concatenate([x[:, half:], -x[:, :half]], axis=1)
+    scale = 1.0 / (time_count * spec_dev)
+    o_ref[0, 0] = lax.dot_general(x, x, nt, preferred_element_type=jnp.float32) * scale
+    o_ref[0, 1] = lax.dot_general(x2, x, nt, preferred_element_type=jnp.float32) * scale
+
+
+def correlate(received, time_count, chan_count, capacity, inp_dev):
+    width = received.shape[2]
+    spec_dev = width // inp_dev
+    inputs = chan_count * inp_dev
+    kernel = functools.partial(correlate_kernel, time_count=time_count, inp_dev=inp_dev, caps=capacity)
+    return pl.pallas_call(
+        kernel,
+        grid=(capacity,),
+        in_specs=[pl.BlockSpec(received.shape, lambda c: (0, 0, 0))],
+        out_specs=pl.BlockSpec((1, 2, inputs, inputs), lambda c: (c, 0, 0, 0)),
+        out_shape=jax.ShapeDtypeStruct((capacity, 2, inputs, inputs), jnp.float32),
+        scratch_shapes=[pltpu.VMEM((2 * time_count * spec_dev, inputs), jnp.float32)],
+    )(received)
 
 
 def solution(mesh):

time: 103 us -> 90.4 us (0.88)
  local copies, waits for them, and re-layouts: 19.2 us -> 2.11 us
  Pallas kernels: 0 us -> 11.9 us
  matrix products: 4.27 us -> 0 us
  other arithmetic: 16 us -> 12.7 us
    pallas_call x0 -> x2, Pallas kernels: none -> 11.9 us  [the longest x1 6.76 us: dft_payload(): pl.pallas_call(dft_kernel, grid=(steps,), in_specs=[pl.BlockSpec((2 * row...]
    another operation x5 -> x0, local copies, waits for them, and re-layouts: 9.27 us -> none  [the longest x1 4.22 us: local(): first_rows = first_rows.reshape(capacity, chan_count * inp_dev, -1)]
    transpose x2 -> x1, local copies, waits for them, and re-layouts: 4.83 us -> 0.1 us  [local(): chosen.reshape(chan_count, time_count, capacity).transpose(2, 1, 0)]
    dot_general x3 -> x0, matrix products: 4.27 us -> none  [the longest x1 2.75 us: local(): jnp.einsum('cpit,cjt->cpij', stacked_rows, first_rows, preferred_element_...]
    all_to_all x1 -> x0, other arithmetic: 3.18 us -> none  [local(): received = lax.all_to_all(sending, ('chan', 'tm'), 0, 0, tiled=True)]
    convert_element_type x2 -> x1, other arithmetic: 5.4 us -> 2.39 us  [local(): running.astype(jnp.bfloat16).reshape(2 * inp_dev * spec_dev, channels)]
    reshape x2 -> x1, local copies, waits for them, and re-layouts: 2.25 us -> 0.31 us  [local(): chosen.reshape(chan_count, time_count, capacity).transpose(2, 1, 0)]
    convert_element_type x1, other arithmetic: 1.43 us -> 3.3 us  [slot_tables(): return (cos_rows.astype(jnp.bfloat16), sin_rows.astype(jnp.bfloat16))]
  transfers between devices with their start and end apart: 1 -> 1, of which waited for: 0 -> 0; matrix products, arithmetic and copies ran while one was open for 7% -> 12% of each run, Pallas kernels for 0% -> 0%
where the time goes in v2:
time: 90.4 us; the launch traced here: 90 us
  blocking collectives  59.2 us (65%)
  other arithmetic  12.7 us (14%)
  Pallas kernels  11.9 us (13%)
  starting transfers between devices  3.95 us (4%)
  local copies, waits for them, and re-layouts  2.11 us (2%)
    all_to_all x1, blocking collectives, local(): received = lax.all_to_all(sending, ('tm', 'chan'), 0, 0, tiled=True)  59.2 us
    pallas_call x1, Pallas kernels, dft_payload(): pl.pallas_call(dft_kernel, grid=(steps,), in_specs=[pl.BlockSpec((2 * row...  6.76 us
    pallas_call x1, Pallas kernels, correlate(): pl.pallas_call(kernel, grid=(capacity,), in_specs=[pl.BlockSpec(received....  5.16 us
    ppermute x1, starting transfers between devices, from_behind(): return lax.ppermute(value, axis, pairs)  3.95 us
    convert_element_type x1, other arithmetic, slot_tables(): return (cos_rows.astype(jnp.bfloat16), sin_rows.astype(jnp.bfloat16))  3.3 us
    convert_element_type x1, other arithmetic, local(): running.astype(jnp.bfloat16).reshape(2 * inp_dev * spec_dev, channels)  2.39 us
  transfers between devices with their start and end apart: 1, of which 0 were waited for; matrix products, arithmetic and copies ran while one was open for 12% of the time, Pallas kernels for 0%

profile of v2, /device:TPU:1, one launch (start us, length us, event | category | flops | bytes accessed | tf_op | source)
XLA Modules:
  0.0 90.0 jit_solution(4923747721192949982)
XLA Ops:
  0.0 1.1 %copy.12 = bf16[4,32,2,1024]{3,1,0,2:T(8,128)(2,1)S(1)} copy(bf16[4,32,2,1024]{3,2,1,0:T(2,128)(2,1)} %param.4) | data formatting | bytes 1048576 | tf_op args[0]
  1.2 0.1 slice.100
  1.2 3.9 %collective-permute-start = (bf16[4,11,2,1024]{3,1,0,2:T(8,128)(2,1)S(1)}, bf16[4,11,2,1024]{3,1,0,2:T(8,128)(2,1)S(1)}, u32[]{:S(2)}, u32[]{:S(2)}) collective-permute-start(bf16[4,11,2,1024]{3,1,0,2:T(8,128)(2,1)S(1)} %slice.100), channel_id=1, source_target_pairs={{0,1},{1,2},{2,3},{4,5},{5,6},{6,7},{8,9},{9,10},{10,11},{12,13},{... | collective-permute-start | bytes 540680 | tf_op jit(solution)/shard_map/ppermute | solution.py:15
  5.2 0.9 fusion.5
  6.1 1.4 %convert_reduce_fusion = s32[1024]{0:T(1024)S(1)} fusion(s32[1024]{0:T(1024)} %param.7, pred[1024]{0:T(1024)(128)(4,1)S(1)} %not.7), kind=kLoop, calls=%fused_computation.8 | loop fusion | flops 6290432 | bytes 9216 | tf_op jit(solution)/shard_map/reduce_sum | solution.py:26
  7.5 0.7 multiply_add_fusion.1
  8.2 0.9 %select_reduce_fusion = s32[1024]{0:T(1024)S(1)} fusion(s32[1024]{0:T(1024)S(1)} %multiply_add_fusion.1, pred[1024]{0:T(1024)(128)(4,1)S(1)} %not.7), kind=kLoop, calls=%fused_computation.6 | loop fusion | flops 4193280 | bytes 9216 | tf_op jit(solution)/shard_map/reduce_sum | solution.py:30
  9.1 0.6 fusion.4
  9.7 0.3 reshape.184
  10.0 0.1 copy.14
  10.2 0.3 select_n.50
  10.5 0.1 copy.15
  10.6 1.1 %fusion.18 = (f32[32,1024]{1,0:T(8,128)S(1)}, f32[32,1024]{1,0:T(8,128)S(1)}, f32[32,1024]{1,0:T(8,128)S(1)}, f32[32,1024]{1,0:T(8,128)S(1)}) fusion(s32[1024]{0:T(1024)S(1)} %bitcast.31, s32[32]{0:T(128)S(1)} %iota_multiply_fusion), kind=kLoop, calls=%fused_computation.37 | loop fusion | flops 917504 | bytes 528512 | tf_op jit(solution)/shard_map/cos | solution.py:42
  11.7 1.2 %multiply_add_fusion = (f32[32,32,1024]{2,1,0:T(8,128)S(1)}, f32[32,32,1024]{2,1,0:T(8,128)S(1)}) fusion(f32[32,1024]{1,0:T(8,128)S(1)} %get-tuple-element.23, f32[32,1024]{1,0:T(8,128)S(1)} %get-tuple-element.20, f32[32,1024]{1,0:T(8,128)S(1)} %get-tuple-element.24, f32[32,1024]{1,0:T(8,128)S(1)} %get-tuple-element.19), kind=kLoop, calls=%fused_computation.4 | loop fusion | flops 6291456 | bytes 8912896 | tf_op jit(solution)/shard_map/add | solution.py:47
  12.9 0.0 copy-start
  12.9 3.3 %fusion = (bf16[1024,1024]{1,0:T(8,128)(2,1)}, bf16[1024,1024]{1,0:T(8,128)(2,1)}) fusion(f32[32,32,1024]{2,1,0:T(8,128)S(1)} %get-tuple-element.5, f32[1024]{0:T(1024)S(1)} %bitcast.30, f32[32,32,1024]{2,1,0:T(8,128)S(1)} %get-tuple-element.6), kind=kLoop, calls=%fused_computation.1 | loop fusion | flops 4194304 | bytes 12587008 | tf_op jit(solution)/shard_map/convert_element_type | solution.py:48
  16.2 0.0 copy-done
  16.3 0.0 collective-permute-done
  16.3 0.2 maximum_bitcast_fusion
  16.5 2.4 %add_convert_fusion = bf16[2,4,32,1024]{3,2,1,0:T(8,128)(2,1)} fusion(bf16[2,4,43,1024]{3,2,1,0:T(8,128)(2,1)S(1)} %maximum_bitcast_fusion, f32[1024]{0:T(1024)S(1)} %bitcast.42, f32[1024]{0:T(1024)S(1)} %bitcast.43, f32[1024]{0:T(1024)S(1)} %bitcast.33, f32[1024]{0:T(1024)S(1)} %bitcast.34, f32[1024]{0:T(1024)S(1)} %bitcast.35, f32[1024]{0:T(1024)S(1)} %bitcast.36, ...), kind=kLoop, calls=%fused_computation.14 | loop fusion | flops 9437184 | bytes 6864896 | tf_op jit(solution)/shard_map/convert_element_type | solution.py:98
  18.9 6.8 %shard_map.46 = bf16[512,4,128]{2,1,0:T(4,128)(2,1)} custom-call(bf16[256,1024]{1,0:T(8,128)(2,1)} %bitcast.27, bf16[1024,1024]{1,0:T(8,128)(2,1)} %get-tuple-element.22.c0_ref.c1_ref, bf16[1024,1024]{1,0:T(8,128)(2,1)} %get-tuple-element.22.c0_ref.c1_ref, bf16[1024,1024]{1,0:T(8,128)(2,1)} %get-tuple-element.21.s0_ref.s1_ref, ...), custom_call_target="tpu_custom_call" | custom-call | tf_op jit(solution)/shard_map/pallas_call | solution.py:69
  25.6 59.2 %all_to_all.5.r_ref = bf16[512,4,128]{2,1,0:T(4,128)(2,1)} all-to-all(bf16[512,4,128]{2,1,0:T(4,128)(2,1)} %shard_map.46), channel_id=1, replica_groups=mesh['chan'=128,'tm'=4] {'tm','chan'}, dimensions={0} | all-to-all | bytes 1048576 | tf_op jit(solution)/shard_map/all_to_all | solution.py:109
  84.8 5.2 %shard_map.47 = f32[2,2,512,512]{3,2,1,0:T(8,128)} custom-call(bf16[512,4,128]{2,1,0:T(4,128)(2,1)} %all_to_all.5.r_ref), custom_call_target="tpu_custom_call" | custom-call | tf_op jit(solution)/shard_map/pallas_call | solution.py:151
  (4 shorter events, 0.0 us)
Async XLA Ops:
  1.2 15.0 %collective-permute-start = (bf16[4,11,2,1024]{3,1,0,2:T(8,128)(2,1)S(1)}, bf16[4,11,2,1024]{3,1,0,2:T(8,128)(2,1)S(1)}, u32[]{:S(2)}, u32[]{:S(2)}) collective-permute-start(bf16[4,11,2,1024]{3,1,0,2:T(8,128)(2,1)S(1)} %slice.100), channel_id=1, source_target_pairs={{0,1},{1,2},{2,3},{4,5},{5,6},{6,7},{8,9},{9,10},{10,11},{12,13},{... | collective-permute-start | bytes 540680 | tf_op jit(solution)/shard_map/ppermute | solution.py:15
  12.9 3.3 %copy-start = (f32[12,1024]{1,0:T(8,128)S(1)}, f32[12,1024]{1,0:T(8,128)}, u32[]{:S(2)}) copy-start(f32[12,1024]{1,0:T(8,128)} %param.5) | copy-start | bytes 147460

commit v3 on v2

--- a/solution.py
+++ b/solution.py
@@ -15,20 +15,17 @@
     return lax.ppermute(value, axis, pairs)
 
 
-def slot_table(flagged, owners, channels, capacity):
+def slot_table(flagged, owners, channels, devices):
     channel_ids = jnp.arange(channels, dtype=jnp.int32)
     alive_mask = jnp.logical_not(jnp.any(flagged[:, None] == channel_ids[None, :], axis=0))
-    earlier = (
-        (owners[None, :] == owners[:, None])
-        & alive_mask[None, :]
-        & (channel_ids[None, :] < channel_ids[:, None])
-    )
-    order_rank = jnp.sum(earlier.astype(jnp.int32), axis=1)
-    slot_of = owners * capacity + order_rank
-    matches = (slot_of[None, :] == channel_ids[:, None]) & alive_mask[None, :]
-    present = jnp.any(matches, axis=1)
-    chosen = jnp.sum(jnp.where(matches, channel_ids[None, :], 0), axis=1)
-    return (chosen, present)
+    device_ids = jnp.arange(devices, dtype=jnp.int32)
+    mine = (owners[None, :] == device_ids[:, None]) & alive_mask[None, :]
+    count = jnp.sum(mine.astype(jnp.int32), axis=1)
+    lower = jnp.min(jnp.where(mine, channel_ids[None, :], channels), axis=1)
+    upper = jnp.max(jnp.where(mine, channel_ids[None, :], 0), axis=1)
+    chosen = jnp.stack([jnp.where(count > 0, lower, 0), jnp.where(count > 1, upper, 0)], axis=1)
+    present = jnp.stack([count > 0, count > 1], axis=1)
+    return (chosen.reshape(-1), present.reshape(-1))
 
 
 def slot_tables(chosen, present, channels):
@@ -63,7 +60,7 @@
 def dft_payload(filtered, cos_rows, sin_rows, devices, capacity):
     channels = filtered.shape[1]
     rows = filtered.shape[0] // 2
-    block = 128
+    block = 256
     steps = devices // block
     table_spec = lambda cap: pl.BlockSpec((channels, block), lambda j: (0, j + cap * steps))
     return pl.pallas_call(
@@ -101,7 +98,7 @@
     time_count = lax.axis_size("tm")
     devices = chan_count * time_count
     capacity = channels // devices
-    chosen, present = slot_table(flagged, owners, channels, capacity)
+    chosen, present = slot_table(flagged, owners, channels, devices)
     chosen = chosen.reshape(chan_count, time_count, capacity).transpose(2, 1, 0).reshape(-1)
     present = present.reshape(chan_count, time_count, capacity).transpose(2, 1, 0).reshape(-1)
     cos_rows, sin_rows = slot_tables(chosen, present, channels)

time: 90.4 us -> 87.2 us (0.965)
  other arithmetic: 12.7 us -> 11 us
  Pallas kernels: 11.9 us -> 10.6 us
    reduce_sum x2 -> x0, other arithmetic: 2.28 us -> none  [the longest x1 1.37 us: slot_table(): order_rank = jnp.sum(earlier.astype(jnp.int32), axis=1)]
    reduce_min x0 -> x1, other arithmetic: none -> 1.88 us  [slot_table(): lower = jnp.min(jnp.where(mine, channel_ids[None, :], channels), axis=1)]
    pallas_call x1, Pallas kernels: 6.76 us -> 5.43 us  [dft_payload(): pl.pallas_call(dft_kernel, grid=(steps,), in_specs=[pl.BlockSpec((2 * row...]
  transfers between devices with their start and end apart: 1 -> 1, of which waited for: 0 -> 0; matrix products, arithmetic and copies ran while one was open for 12% -> 11% of each run, Pallas kernels for 0% -> 0%
where the time goes in v3:
time: 87.2 us; the launch traced here: 86.9 us
  blocking collectives  59.2 us (68%)
  other arithmetic  11 us (13%)
  Pallas kernels  10.6 us (12%)
  starting transfers between devices  3.95 us (5%)
  local copies, waits for them, and re-layouts  2 us (2%)
    all_to_all x1, blocking collectives, local(): received = lax.all_to_all(sending, ('tm', 'chan'), 0, 0, tiled=True)  59.2 us
    pallas_call x1, Pallas kernels, dft_payload(): pl.pallas_call(dft_kernel, grid=(steps,), in_specs=[pl.BlockSpec((2 * row...  5.43 us
    pallas_call x1, Pallas kernels, correlate(): pl.pallas_call(kernel, grid=(capacity,), in_specs=[pl.BlockSpec(received....  5.15 us
    ppermute x1, starting transfers between devices, from_behind(): return lax.ppermute(value, axis, pairs)  3.95 us
    convert_element_type x1, other arithmetic, slot_tables(): return (cos_rows.astype(jnp.bfloat16), sin_rows.astype(jnp.bfloat16))  3.3 us
    convert_element_type x1, other arithmetic, local(): running.astype(jnp.bfloat16).reshape(2 * inp_dev * spec_dev, channels)  2.39 us
    reduce_min x1, other arithmetic, slot_table(): lower = jnp.min(jnp.where(mine, channel_ids[None, :], channels), axis=1)  1.88 us
  transfers between devices with their start and end apart: 1, of which 0 were waited for; matrix products, arithmetic and copies ran while one was open for 11% of the time, Pallas kernels for 0%

profile of v3, /device:TPU:1, one launch (start us, length us, event | category | flops | bytes accessed | tf_op | source)
XLA Modules:
  0.0 86.9 jit_solution(3021687793645826893)
XLA Ops:
  0.0 1.1 %copy.19 = bf16[4,32,2,1024]{3,1,0,2:T(8,128)(2,1)S(1)} copy(bf16[4,32,2,1024]{3,2,1,0:T(2,128)(2,1)} %param.4) | data formatting | bytes 1048576 | tf_op args[0]
  1.2 0.1 slice.100
  1.2 3.9 %collective-permute-start = (bf16[4,11,2,1024]{3,1,0,2:T(8,128)(2,1)S(1)}, bf16[4,11,2,1024]{3,1,0,2:T(8,128)(2,1)S(1)}, u32[]{:S(2)}, u32[]{:S(2)}) collective-permute-start(bf16[4,11,2,1024]{3,1,0,2:T(8,128)(2,1)S(1)} %slice.100), channel_id=1, source_target_pairs={{0,1},{1,2},{2,3},{4,5},{5,6},{6,7},{8,9},{9,10},{10,11},{12,13},{... | collective-permute-start | bytes 540680 | tf_op jit(solution)/shard_map/ppermute | solution.py:15
  5.2 0.9 %fusion.3 = pred[1024]{0:T(1024)(128)(4,1)S(1)} fusion(s32[256]{0:T(256)} %param.6), kind=kLoop, calls=%fused_computation.13 | loop fusion | flops 523264 | bytes 2048 | tf_op jit(solution)/shard_map/reduce_or | solution.py:20
  6.1 1.9 %select_reduce_fusion.1 = (s32[512]{0:T(512)S(1)}, s32[512]{0:T(512)S(1)}, s32[512]{0:T(512)S(1)}) fusion(s32[1024]{0:T(1024)} %param.7, pred[1024]{0:T(1024)(128)(4,1)S(1)} %not.7), kind=kLoop, calls=%fused_computation.7 | loop fusion | flops 4192768 | bytes 11264 | tf_op jit(solution)/shard_map/reduce_min | solution.py:24
  8.0 0.1 gt.41
  8.1 0.1 reduce_min.12
  8.2 0.1 copy.23
  8.3 0.1 copy.21
  8.4 0.1 gt.43
  8.6 0.1 reduce_max.12
  8.7 0.1 copy.24
  8.8 0.1 copy.22
  8.8 1.1 %fusion.16 = (f32[32,1024]{1,0:T(8,128)S(1)}, f32[32,1024]{1,0:T(8,128)S(1)}, f32[32,1024]{1,0:T(8,128)S(1)}, f32[32,1024]{1,0:T(8,128)S(1)}) fusion(s32[1024]{0:T(1024)S(1)} %bitcast.31, s32[32]{0:T(128)S(1)} %iota_multiply_fusion), kind=kLoop, calls=%fused_computation.35 | loop fusion | flops 917504 | bytes 528512 | tf_op jit(solution)/shard_map/cos | solution.py:39
  9.9 1.2 %multiply_add_fusion = (f32[32,32,1024]{2,1,0:T(8,128)S(1)}, f32[32,32,1024]{2,1,0:T(8,128)S(1)}) fusion(f32[32,1024]{1,0:T(8,128)S(1)} %get-tuple-element.26, f32[32,1024]{1,0:T(8,128)S(1)} %get-tuple-element.23, f32[32,1024]{1,0:T(8,128)S(1)} %get-tuple-element.27, f32[32,1024]{1,0:T(8,128)S(1)} %get-tuple-element.22), kind=kLoop, calls=%fused_computation.4 | loop fusion | flops 6291456 | bytes 8912896 | tf_op jit(solution)/shard_map/add | solution.py:44
  11.2 0.0 copy-start
  11.2 3.3 %fusion = (bf16[1024,1024]{1,0:T(8,128)(2,1)}, bf16[1024,1024]{1,0:T(8,128)(2,1)}) fusion(f32[32,32,1024]{2,1,0:T(8,128)S(1)} %get-tuple-element.8, f32[1024]{0:T(1024)S(1)} %bitcast.30, f32[32,32,1024]{2,1,0:T(8,128)S(1)} %get-tuple-element.9), kind=kLoop, calls=%fused_computation.1 | loop fusion | flops 4194304 | bytes 12587008 | tf_op jit(solution)/shard_map/convert_element_type | solution.py:45
  14.5 0.0 copy-done
  14.5 0.0 collective-permute-done
  14.5 0.2 maximum_bitcast_fusion
  14.7 2.4 %add_convert_fusion = bf16[2,4,32,1024]{3,2,1,0:T(8,128)(2,1)} fusion(bf16[2,4,43,1024]{3,2,1,0:T(8,128)(2,1)S(1)} %maximum_bitcast_fusion, f32[1024]{0:T(1024)S(1)} %bitcast.42, f32[1024]{0:T(1024)S(1)} %bitcast.43, f32[1024]{0:T(1024)S(1)} %bitcast.33, f32[1024]{0:T(1024)S(1)} %bitcast.34, f32[1024]{0:T(1024)S(1)} %bitcast.35, f32[1024]{0:T(1024)S(1)} %bitcast.36, ...), kind=kLoop, calls=%fused_computation.12 | loop fusion | flops 9437184 | bytes 6864896 | tf_op jit(solution)/shard_map/convert_element_type | solution.py:95
  17.1 5.4 %shard_map.46 = bf16[512,4,128]{2,1,0:T(4,128)(2,1)} custom-call(bf16[256,1024]{1,0:T(8,128)(2,1)} %bitcast.29, bf16[1024,1024]{1,0:T(8,128)(2,1)} %get-tuple-element.25.c0_ref.c1_ref, bf16[1024,1024]{1,0:T(8,128)(2,1)} %get-tuple-element.25.c0_ref.c1_ref, bf16[1024,1024]{1,0:T(8,128)(2,1)} %get-tuple-element.24.s0_ref.s1_ref, ...), custom_call_target="tpu_custom_call" | custom-call | tf_op jit(solution)/shard_map/pallas_call | solution.py:66
  22.5 59.2 %all_to_all.5.r_ref = bf16[512,4,128]{2,1,0:T(4,128)(2,1)} all-to-all(bf16[512,4,128]{2,1,0:T(4,128)(2,1)} %shard_map.46), channel_id=1, replica_groups=mesh['chan'=128,'tm'=4] {'tm','chan'}, dimensions={0} | all-to-all | bytes 1048576 | tf_op jit(solution)/shard_map/all_to_all | solution.py:106
  81.8 5.2 %shard_map.47 = f32[2,2,512,512]{3,2,1,0:T(8,128)} custom-call(bf16[512,4,128]{2,1,0:T(4,128)(2,1)} %all_to_all.5.r_ref), custom_call_target="tpu_custom_call" | custom-call | tf_op jit(solution)/shard_map/pallas_call | solution.py:148
  (8 shorter events, 0.1 us)
Async XLA Ops:
  1.2 13.3 %collective-permute-start = (bf16[4,11,2,1024]{3,1,0,2:T(8,128)(2,1)S(1)}, bf16[4,11,2,1024]{3,1,0,2:T(8,128)(2,1)S(1)}, u32[]{:S(2)}, u32[]{:S(2)}) collective-permute-start(bf16[4,11,2,1024]{3,1,0,2:T(8,128)(2,1)S(1)} %slice.100), channel_id=1, source_target_pairs={{0,1},{1,2},{2,3},{4,5},{5,6},{6,7},{8,9},{9,10},{10,11},{12,13},{... | collective-permute-start | bytes 540680 | tf_op jit(solution)/shard_map/ppermute | solution.py:15
  11.2 3.3 %copy-start = (f32[12,1024]{1,0:T(8,128)S(1)}, f32[12,1024]{1,0:T(8,128)}, u32[]{:S(2)}) copy-start(f32[12,1024]{1,0:T(8,128)} %param.5) | copy-start | bytes 147460

commit v4 on v3

--- a/solution.py
+++ b/solution.py
@@ -28,54 +28,56 @@
     return (chosen.reshape(-1), present.reshape(-1))
 
 
-def slot_tables(chosen, present, channels):
-    low = 32
-    high = channels // low
+def slot_factors(chosen, present, channels, lanes):
     step = 2.0 * math.pi / channels
-    hi = jnp.arange(high, dtype=jnp.int32)
-    lo = jnp.arange(low, dtype=jnp.int32)
-    angle_hi = ((hi[:, None] * low * chosen[None, :]) % channels).astype(jnp.float32) * step
-    angle_lo = ((lo[:, None] * chosen[None, :]) % channels).astype(jnp.float32) * step
-    c1, s1 = jnp.cos(angle_hi)[:, None, :], jnp.sin(angle_hi)[:, None, :]
-    c2, s2 = jnp.cos(angle_lo)[None, :, :], jnp.sin(angle_lo)[None, :, :]
-    factor = 1.0 / math.sqrt(channels)
-    keep = jnp.where(present, factor, 0.0).astype(jnp.float32)[None, None, :]
-    cos_rows = ((c1 * c2 - s1 * s2) * keep).reshape(channels, -1)
-    sin_rows = ((s1 * c2 + c1 * s2) * keep).reshape(channels, -1)
-    return cos_rows.astype(jnp.bfloat16), sin_rows.astype(jnp.bfloat16)
+    high = jnp.arange(channels // lanes, dtype=jnp.int32)
+    low = jnp.arange(lanes, dtype=jnp.int32)
+    angle_hi = ((chosen[:, None] * (high[None, :] * lanes)) % channels).astype(jnp.float32) * step
+    angle_lo = ((chosen[:, None] * low[None, :]) % channels).astype(jnp.float32) * step
+    keep = jnp.where(present, 1.0 / math.sqrt(channels), 0.0).astype(jnp.float32)[:, None]
+    return (jnp.cos(angle_hi), jnp.sin(angle_hi), jnp.cos(angle_lo) * keep, jnp.sin(angle_lo) * keep)
 
 
-def dft_kernel(x_ref, c0_ref, c1_ref, s0_ref, s1_ref, o_ref):
+def dft_kernel(x_ref, *refs):
+    factor_refs, o_ref = refs[:-1], refs[-1]
     x = x_ref[...]
     half = x.shape[0] // 2
-    for cap, (c_ref, s_ref) in enumerate(((c0_ref, s0_ref), (c1_ref, s1_ref))):
-        cos_part = jnp.dot(x, c_ref[...], preferred_element_type=jnp.float32)
-        sin_part = jnp.dot(x, s_ref[...], preferred_element_type=jnp.float32)
-        real_part = cos_part[:half] + sin_part[half:]
-        imag_part = cos_part[half:] - sin_part[:half]
-        o_ref[:, 2 * cap, :] = real_part.T.astype(o_ref.dtype)
-        o_ref[:, 2 * cap + 1, :] = imag_part.T.astype(o_ref.dtype)
+    nt = (((1,), (1,)), ((), ()))
+    for cap in range(len(factor_refs) // 4):
+        cv, sv, cl, sl = (r[...] for r in factor_refs[4 * cap : 4 * cap + 4])
+        cos_tiles = []
+        sin_tiles = []
+        for v in range(cv.shape[1]):
+            cv_v = cv[:, v : v + 1]
+            sv_v = sv[:, v : v + 1]
+            cos_tiles.append(cv_v * cl - sv_v * sl)
+            sin_tiles.append(sv_v * cl + cv_v * sl)
+        cos_rows = jnp.concatenate(cos_tiles, axis=1).astype(jnp.bfloat16)
+        sin_rows = jnp.concatenate(sin_tiles, axis=1).astype(jnp.bfloat16)
+        cos_part = lax.dot_general(cos_rows, x, nt, preferred_element_type=jnp.float32)
+        sin_part = lax.dot_general(sin_rows, x, nt, preferred_element_type=jnp.float32)
+        o_ref[:, 2 * cap, :] = (cos_part[:, :half] + sin_part[:, half:]).astype(o_ref.dtype)
+        o_ref[:, 2 * cap + 1, :] = (cos_part[:, half:] - sin_part[:, :half]).astype(o_ref.dtype)
 
 
-def dft_payload(filtered, cos_rows, sin_rows, devices, capacity):
+def dft_payload(filtered, factors, devices, capacity):
     channels = filtered.shape[1]
     rows = filtered.shape[0] // 2
     block = 256
     steps = devices // block
-    table_spec = lambda cap: pl.BlockSpec((channels, block), lambda j: (0, j + cap * steps))
+    specs = []
+    operands = []
+    for cap in range(capacity):
+        for f in factors:
+            specs.append(pl.BlockSpec((block, f.shape[1]), lambda j, cap=cap: (j + cap * steps, 0)))
+            operands.append(f)
     return pl.pallas_call(
         dft_kernel,
         grid=(steps,),
-        in_specs=[
-            pl.BlockSpec((2 * rows, channels), lambda j: (0, 0)),
-            table_spec(0),
-            table_spec(1),
-            table_spec(0),
-            table_spec(1),
-        ],
+        in_specs=[pl.BlockSpec((2 * rows, channels), lambda j: (0, 0))] + specs,
         out_specs=pl.BlockSpec((block, capacity * 2, rows), lambda j: (j, 0, 0)),
         out_shape=jax.ShapeDtypeStruct((devices, capacity * 2, rows), jnp.bfloat16),
-    )(filtered, cos_rows, cos_rows, sin_rows, sin_rows)
+    )(filtered, *operands)
 
 
 def local(voltages, filter_taps, flagged, owners):
@@ -101,8 +103,8 @@
     chosen, present = slot_table(flagged, owners, channels, devices)
     chosen = chosen.reshape(chan_count, time_count, capacity).transpose(2, 1, 0).reshape(-1)
     present = present.reshape(chan_count, time_count, capacity).transpose(2, 1, 0).reshape(-1)
-    cos_rows, sin_rows = slot_tables(chosen, present, channels)
-    sending = dft_payload(filtered, cos_rows, sin_rows, devices, capacity)
+    factors = slot_factors(chosen, present, channels, 128)
+    sending = dft_payload(filtered, factors, devices, capacity)
     received = lax.all_to_all(sending, ("tm", "chan"), 0, 0, tiled=True)
     return correlate(received, time_count, chan_count, capacity, inp_dev)
 

time: 87.2 us -> 89.5 us (1.026)
  Pallas kernels: 10.6 us -> 11.8 us
    mul x1 -> x2, other arithmetic: 0.01 us -> 3.46 us  [the longest x1 3.46 us: slot_factors(): jnp.sin(angle_lo) * keep]
    convert_element_type x1, other arithmetic: 3.3 us -> 0.11 us  [slot_factors(): (chosen[:, None] * (high[None, :] * lanes) % channels).astype(jnp.float32)]
    sin x0 -> x1, other arithmetic: none -> 2.8 us  [slot_factors(): jnp.sin(angle_hi)]
    pallas_call x1, Pallas kernels: 5.43 us -> 6.67 us  [dft_payload(): pl.pallas_call(dft_kernel, grid=(steps,), in_specs=[pl.BlockSpec((2 * row...]
    add x1 -> x0, other arithmetic: 1.22 us -> none  [slot_tables(): sin_rows = ((s1 * c2 + c1 * s2) * keep).reshape(channels, -1)]
    cos x1 -> x0, other arithmetic: 1.07 us -> none  [slot_tables(): c1, s1 = (jnp.cos(angle_hi)[:, None, :], jnp.sin(angle_hi)[:, None, :])]
where the time goes in v4:
time: 89.5 us; the launch traced here: 89.1 us
  blocking collectives  59.2 us (66%)
  Pallas kernels  11.8 us (13%)
  other arithmetic  11.7 us (13%)
  starting transfers between devices  3.95 us (4%)
  local copies, waits for them, and re-layouts  2.24 us (3%)
    all_to_all x1, blocking collectives, local(): received = lax.all_to_all(sending, ('tm', 'chan'), 0, 0, tiled=True)  59.2 us
    pallas_call x1, Pallas kernels, dft_payload(): pl.pallas_call(dft_kernel, grid=(steps,), in_specs=[pl.BlockSpec((2 * row...  6.67 us
    pallas_call x1, Pallas kernels, correlate(): pl.pallas_call(kernel, grid=(capacity,), in_specs=[pl.BlockSpec(received....  5.16 us
    ppermute x1, starting transfers between devices, from_behind(): return lax.ppermute(value, axis, pairs)  3.95 us
    mul x1, other arithmetic, slot_factors(): jnp.sin(angle_lo) * keep  3.46 us
    sin x1, other arithmetic, slot_factors(): jnp.sin(angle_hi)  2.8 us
    convert_element_type x1, other arithmetic, local(): running.astype(jnp.bfloat16).reshape(2 * inp_dev * spec_dev, channels)  2.38 us
    reduce_min x1, other arithmetic, slot_table(): lower = jnp.min(jnp.where(mine, channel_ids[None, :], channels), axis=1)  1.88 us
  transfers between devices with their start and end apart: 1, of which 0 were waited for; matrix products, arithmetic and copies ran while one was open for 11% of the time, Pallas kernels for 0%

profile of v4, /device:TPU:1, one launch (start us, length us, event | category | flops | bytes accessed | tf_op | source)
XLA Modules:
  0.0 89.1 jit_solution(17597156176683532317)
XLA Ops:
  0.0 1.1 %copy.19 = bf16[4,32,2,1024]{3,1,0,2:T(8,128)(2,1)S(1)} copy(bf16[4,32,2,1024]{3,2,1,0:T(2,128)(2,1)} %param.4) | data formatting | bytes 1048576 | tf_op args[0]
  1.2 0.0 copy-start
  1.2 0.1 slice.100
  1.2 3.9 %collective-permute-start = (bf16[4,11,2,1024]{3,1,0,2:T(8,128)(2,1)S(1)}, bf16[4,11,2,1024]{3,1,0,2:T(8,128)(2,1)S(1)}, u32[]{:S(2)}, u32[]{:S(2)}) collective-permute-start(bf16[4,11,2,1024]{3,1,0,2:T(8,128)(2,1)S(1)} %slice.100), channel_id=1, source_target_pairs={{0,1},{1,2},{2,3},{4,5},{5,6},{6,7},{8,9},{9,10},{10,11},{12,13},{... | collective-permute-start | bytes 540680 | tf_op jit(solution)/shard_map/ppermute | solution.py:15
  5.2 0.9 %fusion.1 = pred[1024]{0:T(1024)(128)(4,1)S(1)} fusion(s32[256]{0:T(256)} %param.6), kind=kLoop, calls=%fused_computation.7 | loop fusion | flops 523264 | bytes 2048 | tf_op jit(solution)/shard_map/reduce_or | solution.py:20
  6.1 1.9 %select_reduce_fusion.1 = (s32[512]{0:T(512)S(1)}, s32[512]{0:T(512)S(1)}, s32[512]{0:T(512)S(1)}) fusion(s32[1024]{0:T(1024)} %param.7, pred[1024]{0:T(1024)(128)(4,1)S(1)} %not.7), kind=kLoop, calls=%fused_computation.1 | loop fusion | flops 4192768 | bytes 11264 | tf_op jit(solution)/shard_map/reduce_min | solution.py:24
  8.0 0.1 gt.41
  8.1 0.1 copy.24
  8.2 0.1 gt.43
  8.4 0.1 copy.25
  8.4 0.1 reduce_min.12
  8.6 0.1 copy.21
  8.7 0.1 reduce_max.12
  8.8 0.1 copy.22
  8.9 0.1 fusion.8
  9.0 0.2 copy.23
  9.2 2.8 %multiply_sine_fusion = (f32[1024,8]{1,0:T(8,128)}, f32[1024,8]{1,0:T(8,128)}) fusion(f32[1024,8]{1,0:T(8,128)S(1)} %copy.23), kind=kLoop, calls=%fused_computation.20 | loop fusion | flops 8192 | bytes 98304 | tf_op jit(solution)/shard_map/sin | solution.py:38
  12.0 3.5 %sine_multiply_fusion = (f32[1024,128]{1,0:T(8,128)}, f32[1024,128]{1,0:T(8,128)}) fusion(f32[1024]{0:T(1024)S(1)} %bitcast.24, s32[1024]{0:T(1024)S(1)} %bitcast.23), kind=kLoop, calls=%fused_computation.15 | loop fusion | flops 2097152 | bytes 1056768 | tf_op jit(solution)/shard_map/mul | solution.py:38
  15.5 0.0 copy-done
  15.5 0.0 collective-permute-done
  15.5 0.2 maximum_bitcast_fusion
  15.7 2.4 %add_convert_fusion = bf16[2,4,32,1024]{3,2,1,0:T(8,128)(2,1)} fusion(bf16[2,4,43,1024]{3,2,1,0:T(8,128)(2,1)S(1)} %maximum_bitcast_fusion, f32[1024]{0:T(1024)S(1)} %bitcast.35, f32[1024]{0:T(1024)S(1)} %bitcast.36, f32[1024]{0:T(1024)S(1)} %bitcast.26, f32[1024]{0:T(1024)S(1)} %bitcast.27, f32[1024]{0:T(1024)S(1)} %bitcast.28, f32[1024]{0:T(1024)S(1)} %bitcast.29, ...), kind=kLoop, calls=%fused_computation.6 | loop fusion | flops 9437184 | bytes 6864896 | tf_op jit(solution)/shard_map/convert_element_type | solution.py:97
  18.1 6.7 %shard_map.46 = bf16[512,4,128]{2,1,0:T(4,128)(2,1)} custom-call(bf16[256,1024]{1,0:T(8,128)(2,1)} %bitcast.21, f32[1024,8]{1,0:T(8,128)} %get-tuple-element.9.refs_0_.refs_4_, f32[1024,8]{1,0:T(8,128)} %get-tuple-element.8.refs_1_.refs_5_, f32[1024,128]{1,0:T(8,128)} %get-tuple-element.23.refs_2_.refs_6_, f32[1024,128]{1,0:T(8,128)} %get-tuple-element.22.refs_3_.refs_7_, ...), custom_call_target="tpu_custom_call" | custom-call | tf_op jit(solution)/shard_map/pallas_call | solution.py:74
  24.7 59.2 %all_to_all.5.r_ref = bf16[512,4,128]{2,1,0:T(4,128)(2,1)} all-to-all(bf16[512,4,128]{2,1,0:T(4,128)(2,1)} %shard_map.46), channel_id=1, replica_groups=mesh['chan'=128,'tm'=4] {'tm','chan'}, dimensions={0} | all-to-all | bytes 1048576 | tf_op jit(solution)/shard_map/all_to_all | solution.py:108
  84.0 5.2 %shard_map.47 = f32[2,2,512,512]{3,2,1,0:T(8,128)} custom-call(bf16[512,4,128]{2,1,0:T(4,128)(2,1)} %all_to_all.5.r_ref), custom_call_target="tpu_custom_call" | custom-call | tf_op jit(solution)/shard_map/pallas_call | solution.py:150
  (8 shorter events, 0.1 us)
Async XLA Ops:
  1.2 14.3 %copy-start = (f32[12,1024]{1,0:T(8,128)S(1)}, f32[12,1024]{1,0:T(8,128)}, u32[]{:S(2)}) copy-start(f32[12,1024]{1,0:T(8,128)} %param.5) | copy-start | bytes 147460
  1.2 14.3 %collective-permute-start = (bf16[4,11,2,1024]{3,1,0,2:T(8,128)(2,1)S(1)}, bf16[4,11,2,1024]{3,1,0,2:T(8,128)(2,1)S(1)}, u32[]{:S(2)}, u32[]{:S(2)}) collective-permute-start(bf16[4,11,2,1024]{3,1,0,2:T(8,128)(2,1)S(1)} %slice.100), channel_id=1, source_target_pairs={{0,1},{1,2},{2,3},{4,5},{5,6},{6,7},{8,9},{9,10},{10,11},{12,13},{... | collective-permute-start | bytes 540680 | tf_op jit(solution)/shard_map/ppermute | solution.py:15

commit v5 on v3

--- a/solution.py
+++ b/solution.py
@@ -107,14 +107,21 @@
     return correlate(received, time_count, chan_count, capacity, inp_dev)
 
 
-def correlate_kernel(r_ref, o_ref, xt_ref, *, time_count, inp_dev, caps):
+def correlate_kernel(r_ref, o_ref, xt_ref, x_ref, x2_ref, *, time_count, inp_dev, caps):
     for cap in range(caps):
-        pl.when(pl.program_id(0) == cap)(
-            functools.partial(correlate_slot, r_ref, o_ref, xt_ref, cap, time_count, inp_dev)
+        pl.when((pl.program_id(0) == cap) & (pl.program_id(1) == 0))(
+            functools.partial(gather_slot, r_ref, xt_ref, x_ref, x2_ref, cap, time_count, inp_dev)
         )
+    block = o_ref.shape[2]
+    start = pl.multiple_of(pl.program_id(1) * block, block)
+    nt = (((1,), (1,)), ((), ()))
+    scale = 1.0 / (time_count * (r_ref.shape[2] // inp_dev))
+    x = x_ref[...]
+    o_ref[0, 0] = lax.dot_general(x_ref[pl.ds(start, block), :], x, nt, preferred_element_type=jnp.float32) * scale
+    o_ref[0, 1] = lax.dot_general(x2_ref[pl.ds(start, block), :], x, nt, preferred_element_type=jnp.float32) * scale
 
 
-def correlate_slot(r_ref, o_ref, xt_ref, cap, time_count, inp_dev):
+def gather_slot(r_ref, xt_ref, x_ref, x2_ref, cap, time_count, inp_dev):
     chans = r_ref.shape[0] // time_count
     spec_dev = r_ref.shape[2] // inp_dev
     for reim in range(2):
@@ -134,24 +141,27 @@
     xt = xt_ref[...].astype(jnp.bfloat16)
     x = lax.dot_general(perm, xt, nt, preferred_element_type=jnp.float32).astype(jnp.bfloat16)
     half = x.shape[1] // 2
-    x2 = jnp.concatenate([x[:, half:], -x[:, :half]], axis=1)
-    scale = 1.0 / (time_count * spec_dev)
-    o_ref[0, 0] = lax.dot_general(x, x, nt, preferred_element_type=jnp.float32) * scale
-    o_ref[0, 1] = lax.dot_general(x2, x, nt, preferred_element_type=jnp.float32) * scale
+    x_ref[...] = x
+    x2_ref[...] = jnp.concatenate([x[:, half:], -x[:, :half]], axis=1)
 
 
 def correlate(received, time_count, chan_count, capacity, inp_dev):
     width = received.shape[2]
     spec_dev = width // inp_dev
     inputs = chan_count * inp_dev
+    block = 128
     kernel = functools.partial(correlate_kernel, time_count=time_count, inp_dev=inp_dev, caps=capacity)
     return pl.pallas_call(
         kernel,
-        grid=(capacity,),
-        in_specs=[pl.BlockSpec(received.shape, lambda c: (0, 0, 0))],
-        out_specs=pl.BlockSpec((1, 2, inputs, inputs), lambda c: (c, 0, 0, 0)),
+        grid=(capacity, inputs // block),
+        in_specs=[pl.BlockSpec(received.shape, lambda c, r: (0, 0, 0))],
+        out_specs=pl.BlockSpec((1, 2, block, inputs), lambda c, r: (c, 0, r, 0)),
         out_shape=jax.ShapeDtypeStruct((capacity, 2, inputs, inputs), jnp.float32),
-        scratch_shapes=[pltpu.VMEM((2 * time_count * spec_dev, inputs), jnp.float32)],
+        scratch_shapes=[
+            pltpu.VMEM((2 * time_count * spec_dev, inputs), jnp.float32),
+            pltpu.VMEM((inputs, 2 * time_count * spec_dev), jnp.bfloat16),
+            pltpu.VMEM((inputs, 2 * time_count * spec_dev), jnp.bfloat16),
+        ],
     )(received)
 
 

time: 87.2 us -> 89.4 us (1.025)
  Pallas kernels: 10.6 us -> 12.8 us
    pallas_call x1, Pallas kernels: 5.15 us -> 7.39 us  [correlate(): pl.pallas_call(kernel, grid=(capacity, inputs // block), in_specs=[pl.Blo...]
  transfers between devices with their start and end apart: 1 -> 1, of which waited for: 0 -> 0; matrix products, arithmetic and copies ran while one was open for 11% -> 10% of each run, Pallas kernels for 0% -> 0%
where the time goes in v5:
time: 89.4 us; the launch traced here: 89.1 us
  blocking collectives  59.2 us (66%)
  Pallas kernels  12.8 us (14%)
  other arithmetic  11 us (12%)
  starting transfers between devices  3.95 us (4%)
  local copies, waits for them, and re-layouts  2 us (2%)
    all_to_all x1, blocking collectives, local(): received = lax.all_to_all(sending, ('tm', 'chan'), 0, 0, tiled=True)  59.2 us
    pallas_call x1, Pallas kernels, correlate(): pl.pallas_call(kernel, grid=(capacity, inputs // block), in_specs=[pl.Blo...  7.39 us
    pallas_call x1, Pallas kernels, dft_payload(): pl.pallas_call(dft_kernel, grid=(steps,), in_specs=[pl.BlockSpec((2 * row...  5.43 us
    ppermute x1, starting transfers between devices, from_behind(): return lax.ppermute(value, axis, pairs)  3.95 us
    convert_element_type x1, other arithmetic, slot_tables(): return (cos_rows.astype(jnp.bfloat16), sin_rows.astype(jnp.bfloat16))  3.3 us
    convert_element_type x1, other arithmetic, local(): running.astype(jnp.bfloat16).reshape(2 * inp_dev * spec_dev, channels)  2.39 us
    reduce_min x1, other arithmetic, slot_table(): lower = jnp.min(jnp.where(mine, channel_ids[None, :], channels), axis=1)  1.88 us
  transfers between devices with their start and end apart: 1, of which 0 were waited for; matrix products, arithmetic and copies ran while one was open for 10% of the time, Pallas kernels for 0%

profile of v5, /device:TPU:1, one launch (start us, length us, event | category | flops | bytes accessed | tf_op | source)
XLA Modules:
  0.0 89.1 jit_solution(8305685166782092747)
XLA Ops:
  0.0 1.1 %copy.19 = bf16[4,32,2,1024]{3,1,0,2:T(8,128)(2,1)S(1)} copy(bf16[4,32,2,1024]{3,2,1,0:T(2,128)(2,1)} %param.4) | data formatting | bytes 1048576 | tf_op args[0]
  1.2 0.1 slice.100
  1.2 3.9 %collective-permute-start = (bf16[4,11,2,1024]{3,1,0,2:T(8,128)(2,1)S(1)}, bf16[4,11,2,1024]{3,1,0,2:T(8,128)(2,1)S(1)}, u32[]{:S(2)}, u32[]{:S(2)}) collective-permute-start(bf16[4,11,2,1024]{3,1,0,2:T(8,128)(2,1)S(1)} %slice.100), channel_id=1, source_target_pairs={{0,1},{1,2},{2,3},{4,5},{5,6},{6,7},{8,9},{9,10},{10,11},{12,13},{... | collective-permute-start | bytes 540680 | tf_op jit(solution)/shard_map/ppermute | solution.py:15
  5.2 0.9 %fusion.3 = pred[1024]{0:T(1024)(128)(4,1)S(1)} fusion(s32[256]{0:T(256)} %param.6), kind=kLoop, calls=%fused_computation.13 | loop fusion | flops 523264 | bytes 2048 | tf_op jit(solution)/shard_map/reduce_or | solution.py:20
  6.1 1.9 %select_reduce_fusion.1 = (s32[512]{0:T(512)S(1)}, s32[512]{0:T(512)S(1)}, s32[512]{0:T(512)S(1)}) fusion(s32[1024]{0:T(1024)} %param.7, pred[1024]{0:T(1024)(128)(4,1)S(1)} %not.7), kind=kLoop, calls=%fused_computation.7 | loop fusion | flops 4192768 | bytes 11264 | tf_op jit(solution)/shard_map/reduce_min | solution.py:24
  8.0 0.1 gt.41
  8.1 0.1 reduce_min.12
  8.2 0.1 copy.23
  8.3 0.1 copy.21
  8.4 0.1 gt.43
  8.6 0.1 reduce_max.12
  8.7 0.1 copy.24
  8.8 0.1 copy.22
  8.8 1.1 %fusion.16 = (f32[32,1024]{1,0:T(8,128)S(1)}, f32[32,1024]{1,0:T(8,128)S(1)}, f32[32,1024]{1,0:T(8,128)S(1)}, f32[32,1024]{1,0:T(8,128)S(1)}) fusion(s32[1024]{0:T(1024)S(1)} %bitcast.31, s32[32]{0:T(128)S(1)} %iota_multiply_fusion), kind=kLoop, calls=%fused_computation.35 | loop fusion | flops 917504 | bytes 528512 | tf_op jit(solution)/shard_map/cos | solution.py:39
  9.9 1.2 %multiply_add_fusion = (f32[32,32,1024]{2,1,0:T(8,128)S(1)}, f32[32,32,1024]{2,1,0:T(8,128)S(1)}) fusion(f32[32,1024]{1,0:T(8,128)S(1)} %get-tuple-element.26, f32[32,1024]{1,0:T(8,128)S(1)} %get-tuple-element.23, f32[32,1024]{1,0:T(8,128)S(1)} %get-tuple-element.27, f32[32,1024]{1,0:T(8,128)S(1)} %get-tuple-element.22), kind=kLoop, calls=%fused_computation.4 | loop fusion | flops 6291456 | bytes 8912896 | tf_op jit(solution)/shard_map/add | solution.py:44
  11.2 0.0 copy-start
  11.2 3.3 %fusion = (bf16[1024,1024]{1,0:T(8,128)(2,1)}, bf16[1024,1024]{1,0:T(8,128)(2,1)}) fusion(f32[32,32,1024]{2,1,0:T(8,128)S(1)} %get-tuple-element.8, f32[1024]{0:T(1024)S(1)} %bitcast.30, f32[32,32,1024]{2,1,0:T(8,128)S(1)} %get-tuple-element.9), kind=kLoop, calls=%fused_computation.1 | loop fusion | flops 4194304 | bytes 12587008 | tf_op jit(solution)/shard_map/convert_element_type | solution.py:45
  14.5 0.0 copy-done
  14.5 0.0 collective-permute-done
  14.5 0.2 maximum_bitcast_fusion
  14.7 2.4 %add_convert_fusion = bf16[2,4,32,1024]{3,2,1,0:T(8,128)(2,1)} fusion(bf16[2,4,43,1024]{3,2,1,0:T(8,128)(2,1)S(1)} %maximum_bitcast_fusion, f32[1024]{0:T(1024)S(1)} %bitcast.42, f32[1024]{0:T(1024)S(1)} %bitcast.43, f32[1024]{0:T(1024)S(1)} %bitcast.33, f32[1024]{0:T(1024)S(1)} %bitcast.34, f32[1024]{0:T(1024)S(1)} %bitcast.35, f32[1024]{0:T(1024)S(1)} %bitcast.36, ...), kind=kLoop, calls=%fused_computation.12 | loop fusion | flops 9437184 | bytes 6864896 | tf_op jit(solution)/shard_map/convert_element_type | solution.py:95
  17.1 5.4 %shard_map.46 = bf16[512,4,128]{2,1,0:T(4,128)(2,1)} custom-call(bf16[256,1024]{1,0:T(8,128)(2,1)} %bitcast.29, bf16[1024,1024]{1,0:T(8,128)(2,1)} %get-tuple-element.25.c0_ref.c1_ref, bf16[1024,1024]{1,0:T(8,128)(2,1)} %get-tuple-element.25.c0_ref.c1_ref, bf16[1024,1024]{1,0:T(8,128)(2,1)} %get-tuple-element.24.s0_ref.s1_ref, ...), custom_call_target="tpu_custom_call" | custom-call | tf_op jit(solution)/shard_map/pallas_call | solution.py:66
  22.5 59.2 %all_to_all.5.r_ref = bf16[512,4,128]{2,1,0:T(4,128)(2,1)} all-to-all(bf16[512,4,128]{2,1,0:T(4,128)(2,1)} %shard_map.46), channel_id=1, replica_groups=mesh['chan'=128,'tm'=4] {'tm','chan'}, dimensions={0} | all-to-all | bytes 1048576 | tf_op jit(solution)/shard_map/all_to_all | solution.py:106
  81.7 7.4 %shard_map.47 = f32[2,2,512,512]{3,2,1,0:T(8,128)} custom-call(bf16[512,4,128]{2,1,0:T(4,128)(2,1)} %all_to_all.5.r_ref), custom_call_target="tpu_custom_call" | custom-call | tf_op jit(solution)/shard_map/pallas_call | solution.py:154
  (8 shorter events, 0.1 us)
Async XLA Ops:
  1.2 13.3 %collective-permute-start = (bf16[4,11,2,1024]{3,1,0,2:T(8,128)(2,1)S(1)}, bf16[4,11,2,1024]{3,1,0,2:T(8,128)(2,1)S(1)}, u32[]{:S(2)}, u32[]{:S(2)}) collective-permute-start(bf16[4,11,2,1024]{3,1,0,2:T(8,128)(2,1)S(1)} %slice.100), channel_id=1, source_target_pairs={{0,1},{1,2},{2,3},{4,5},{5,6},{6,7},{8,9},{9,10},{10,11},{12,13},{... | collective-permute-start | bytes 540680 | tf_op jit(solution)/shard_map/ppermute | solution.py:15
  11.2 3.3 %copy-start = (f32[12,1024]{1,0:T(8,128)S(1)}, f32[12,1024]{1,0:T(8,128)}, u32[]{:S(2)}) copy-start(f32[12,1024]{1,0:T(8,128)} %param.5) | copy-start | bytes 147460

commit v6 on v3

--- a/solution.py
+++ b/solution.py
@@ -60,7 +60,7 @@
 def dft_payload(filtered, cos_rows, sin_rows, devices, capacity):
     channels = filtered.shape[1]
     rows = filtered.shape[0] // 2
-    block = 256
+    block = 512
     steps = devices // block
     table_spec = lambda cap: pl.BlockSpec((channels, block), lambda j: (0, j + cap * steps))
     return pl.pallas_call(

time: 87.2 us -> 87.4 us (level)
  no operation moved by 1% of the time
where the time goes in v6:
time: 87.4 us; the launch traced here: 87.1 us
  blocking collectives  59.2 us (68%)
  other arithmetic  11 us (13%)
  Pallas kernels  10.8 us (12%)
  starting transfers between devices  3.95 us (5%)
  local copies, waits for them, and re-layouts  2 us (2%)
    all_to_all x1, blocking collectives, local(): received = lax.all_to_all(sending, ('tm', 'chan'), 0, 0, tiled=True)  59.2 us
    pallas_call x1, Pallas kernels, dft_payload(): pl.pallas_call(dft_kernel, grid=(steps,), in_specs=[pl.BlockSpec((2 * row...  5.67 us
    pallas_call x1, Pallas kernels, correlate(): pl.pallas_call(kernel, grid=(capacity,), in_specs=[pl.BlockSpec(received....  5.15 us
    ppermute x1, starting transfers between devices, from_behind(): return lax.ppermute(value, axis, pairs)  3.95 us
    convert_element_type x1, other arithmetic, slot_tables(): return (cos_rows.astype(jnp.bfloat16), sin_rows.astype(jnp.bfloat16))  3.3 us
    convert_element_type x1, other arithmetic, local(): running.astype(jnp.bfloat16).reshape(2 * inp_dev * spec_dev, channels)  2.39 us
    reduce_min x1, other arithmetic, slot_table(): lower = jnp.min(jnp.where(mine, channel_ids[None, :], channels), axis=1)  1.88 us
  transfers between devices with their start and end apart: 1, of which 0 were waited for; matrix products, arithmetic and copies ran while one was open for 11% of the time, Pallas kernels for 0%

profile of v6, /device:TPU:1, one launch (start us, length us, event | category | flops | bytes accessed | tf_op | source)
XLA Modules:
  0.0 87.1 jit_solution(16302234900600867211)
XLA Ops:
  0.0 1.1 %copy.19 = bf16[4,32,2,1024]{3,1,0,2:T(8,128)(2,1)S(1)} copy(bf16[4,32,2,1024]{3,2,1,0:T(2,128)(2,1)} %param.4) | data formatting | bytes 1048576 | tf_op args[0]
  1.2 0.1 slice.100
  1.2 3.9 %collective-permute-start = (bf16[4,11,2,1024]{3,1,0,2:T(8,128)(2,1)S(1)}, bf16[4,11,2,1024]{3,1,0,2:T(8,128)(2,1)S(1)}, u32[]{:S(2)}, u32[]{:S(2)}) collective-permute-start(bf16[4,11,2,1024]{3,1,0,2:T(8,128)(2,1)S(1)} %slice.100), channel_id=1, source_target_pairs={{0,1},{1,2},{2,3},{4,5},{5,6},{6,7},{8,9},{9,10},{10,11},{12,13},{... | collective-permute-start | bytes 540680 | tf_op jit(solution)/shard_map/ppermute | solution.py:15
  5.2 0.9 %fusion.3 = pred[1024]{0:T(1024)(128)(4,1)S(1)} fusion(s32[256]{0:T(256)} %param.6), kind=kLoop, calls=%fused_computation.13 | loop fusion | flops 523264 | bytes 2048 | tf_op jit(solution)/shard_map/reduce_or | solution.py:20
  6.1 1.9 %select_reduce_fusion.1 = (s32[512]{0:T(512)S(1)}, s32[512]{0:T(512)S(1)}, s32[512]{0:T(512)S(1)}) fusion(s32[1024]{0:T(1024)} %param.7, pred[1024]{0:T(1024)(128)(4,1)S(1)} %not.7), kind=kLoop, calls=%fused_computation.7 | loop fusion | flops 4192768 | bytes 11264 | tf_op jit(solution)/shard_map/reduce_min | solution.py:24
  8.0 0.1 gt.41
  8.1 0.1 reduce_min.12
  8.2 0.1 copy.23
  8.3 0.1 copy.21
  8.4 0.1 gt.43
  8.6 0.1 reduce_max.12
  8.7 0.1 copy.24
  8.8 0.1 copy.22
  8.8 1.1 %fusion.16 = (f32[32,1024]{1,0:T(8,128)S(1)}, f32[32,1024]{1,0:T(8,128)S(1)}, f32[32,1024]{1,0:T(8,128)S(1)}, f32[32,1024]{1,0:T(8,128)S(1)}) fusion(s32[1024]{0:T(1024)S(1)} %bitcast.31, s32[32]{0:T(128)S(1)} %iota_multiply_fusion), kind=kLoop, calls=%fused_computation.35 | loop fusion | flops 917504 | bytes 528512 | tf_op jit(solution)/shard_map/cos | solution.py:39
  9.9 1.2 %multiply_add_fusion = (f32[32,32,1024]{2,1,0:T(8,128)S(1)}, f32[32,32,1024]{2,1,0:T(8,128)S(1)}) fusion(f32[32,1024]{1,0:T(8,128)S(1)} %get-tuple-element.26, f32[32,1024]{1,0:T(8,128)S(1)} %get-tuple-element.23, f32[32,1024]{1,0:T(8,128)S(1)} %get-tuple-element.27, f32[32,1024]{1,0:T(8,128)S(1)} %get-tuple-element.22), kind=kLoop, calls=%fused_computation.4 | loop fusion | flops 6291456 | bytes 8912896 | tf_op jit(solution)/shard_map/add | solution.py:44
  11.2 0.0 copy-start
  11.2 3.3 %fusion = (bf16[1024,1024]{1,0:T(8,128)(2,1)}, bf16[1024,1024]{1,0:T(8,128)(2,1)}) fusion(f32[32,32,1024]{2,1,0:T(8,128)S(1)} %get-tuple-element.8, f32[1024]{0:T(1024)S(1)} %bitcast.30, f32[32,32,1024]{2,1,0:T(8,128)S(1)} %get-tuple-element.9), kind=kLoop, calls=%fused_computation.1 | loop fusion | flops 4194304 | bytes 12587008 | tf_op jit(solution)/shard_map/convert_element_type | solution.py:45
  14.5 0.0 copy-done
  14.5 0.0 collective-permute-done
  14.5 0.2 maximum_bitcast_fusion
  14.7 2.4 %add_convert_fusion = bf16[2,4,32,1024]{3,2,1,0:T(8,128)(2,1)} fusion(bf16[2,4,43,1024]{3,2,1,0:T(8,128)(2,1)S(1)} %maximum_bitcast_fusion, f32[1024]{0:T(1024)S(1)} %bitcast.42, f32[1024]{0:T(1024)S(1)} %bitcast.43, f32[1024]{0:T(1024)S(1)} %bitcast.33, f32[1024]{0:T(1024)S(1)} %bitcast.34, f32[1024]{0:T(1024)S(1)} %bitcast.35, f32[1024]{0:T(1024)S(1)} %bitcast.36, ...), kind=kLoop, calls=%fused_computation.12 | loop fusion | flops 9437184 | bytes 6864896 | tf_op jit(solution)/shard_map/convert_element_type | solution.py:95
  17.1 5.7 %shard_map.46 = bf16[512,4,128]{2,1,0:T(4,128)(2,1)} custom-call(bf16[256,1024]{1,0:T(8,128)(2,1)} %bitcast.29, bf16[1024,1024]{1,0:T(8,128)(2,1)} %get-tuple-element.25.c0_ref.c1_ref, bf16[1024,1024]{1,0:T(8,128)(2,1)} %get-tuple-element.25.c0_ref.c1_ref, bf16[1024,1024]{1,0:T(8,128)(2,1)} %get-tuple-element.24.s0_ref.s1_ref, ...), custom_call_target="tpu_custom_call" | custom-call | tf_op jit(solution)/shard_map/pallas_call | solution.py:66
  22.8 59.2 %all_to_all.5.r_ref = bf16[512,4,128]{2,1,0:T(4,128)(2,1)} all-to-all(bf16[512,4,128]{2,1,0:T(4,128)(2,1)} %shard_map.46), channel_id=1, replica_groups=mesh['chan'=128,'tm'=4] {'tm','chan'}, dimensions={0} | all-to-all | bytes 1048576 | tf_op jit(solution)/shard_map/all_to_all | solution.py:106
  82.0 5.2 %shard_map.47 = f32[2,2,512,512]{3,2,1,0:T(8,128)} custom-call(bf16[512,4,128]{2,1,0:T(4,128)(2,1)} %all_to_all.5.r_ref), custom_call_target="tpu_custom_call" | custom-call | tf_op jit(solution)/shard_map/pallas_call | solution.py:148
  (8 shorter events, 0.1 us)
Async XLA Ops:
  1.2 13.3 %collective-permute-start = (bf16[4,11,2,1024]{3,1,0,2:T(8,128)(2,1)S(1)}, bf16[4,11,2,1024]{3,1,0,2:T(8,128)(2,1)S(1)}, u32[]{:S(2)}, u32[]{:S(2)}) collective-permute-start(bf16[4,11,2,1024]{3,1,0,2:T(8,128)(2,1)S(1)} %slice.100), channel_id=1, source_target_pairs={{0,1},{1,2},{2,3},{4,5},{5,6},{6,7},{8,9},{9,10},{10,11},{12,13},{... | collective-permute-start | bytes 540680 | tf_op jit(solution)/shard_map/ppermute | solution.py:15
  11.2 3.3 %copy-start = (f32[12,1024]{1,0:T(8,128)S(1)}, f32[12,1024]{1,0:T(8,128)}, u32[]{:S(2)}) copy-start(f32[12,1024]{1,0:T(8,128)} %param.5) | copy-start | bytes 147460

commit v7 on v6

--- a/solution.py
+++ b/solution.py
@@ -17,12 +17,10 @@
 
 def slot_table(flagged, owners, channels, devices):
     channel_ids = jnp.arange(channels, dtype=jnp.int32)
-    alive_mask = jnp.logical_not(jnp.any(flagged[:, None] == channel_ids[None, :], axis=0))
-    device_ids = jnp.arange(devices, dtype=jnp.int32)
-    mine = (owners[None, :] == device_ids[:, None]) & alive_mask[None, :]
-    count = jnp.sum(mine.astype(jnp.int32), axis=1)
-    lower = jnp.min(jnp.where(mine, channel_ids[None, :], channels), axis=1)
-    upper = jnp.max(jnp.where(mine, channel_ids[None, :], 0), axis=1)
+    alive_mask = jnp.ones((channels,), jnp.bool_).at[flagged].set(False)
+    count = jnp.zeros((devices,), jnp.int32).at[owners].add(alive_mask.astype(jnp.int32))
+    lower = jnp.full((devices,), channels, jnp.int32).at[owners].min(jnp.where(alive_mask, channel_ids, channels))
+    upper = jnp.zeros((devices,), jnp.int32).at[owners].max(jnp.where(alive_mask, channel_ids, 0))
     chosen = jnp.stack([jnp.where(count > 0, lower, 0), jnp.where(count > 1, upper, 0)], axis=1)
     present = jnp.stack([count > 0, count > 1], axis=1)
     return (chosen.reshape(-1), present.reshape(-1))
@@ -36,12 +34,12 @@
     lo = jnp.arange(low, dtype=jnp.int32)
     angle_hi = ((hi[:, None] * low * chosen[None, :]) % channels).astype(jnp.float32) * step
     angle_lo = ((lo[:, None] * chosen[None, :]) % channels).astype(jnp.float32) * step
+    factor = 1.0 / math.sqrt(channels)
+    keep = jnp.where(present, factor, 0.0).astype(jnp.float32)[None, :]
     c1, s1 = jnp.cos(angle_hi)[:, None, :], jnp.sin(angle_hi)[:, None, :]
-    c2, s2 = jnp.cos(angle_lo)[None, :, :], jnp.sin(angle_lo)[None, :, :]
-    factor = 1.0 / math.sqrt(channels)
-    keep = jnp.where(present, factor, 0.0).astype(jnp.float32)[None, None, :]
-    cos_rows = ((c1 * c2 - s1 * s2) * keep).reshape(channels, -1)
-    sin_rows = ((s1 * c2 + c1 * s2) * keep).reshape(channels, -1)
+    c2, s2 = (jnp.cos(angle_lo) * keep)[None, :, :], (jnp.sin(angle_lo) * keep)[None, :, :]
+    cos_rows = (c1 * c2 - s1 * s2).reshape(channels, -1)
+    sin_rows = (s1 * c2 + c1 * s2).reshape(channels, -1)
     return cos_rows.astype(jnp.bfloat16), sin_rows.astype(jnp.bfloat16)
 
 

time: 87.4 us -> 109 us (1.25)
  other arithmetic: 11 us -> 31.2 us
  local copies, waits for them, and re-layouts: 2 us -> 3.57 us
    another operation x0 -> x2, other arithmetic: none -> 15.2 us  [the longest x1 7.61 us: slot_table(): jnp.zeros((devices,), jnp.int32).at[owners]]
    scatter-add x0 -> x1, other arithmetic: none -> 7.61 us  [slot_table(): jnp.zeros((devices,), jnp.int32).at[owners]]
    reduce_min x1 -> x0, other arithmetic: 1.88 us -> none  [slot_table(): lower = jnp.min(jnp.where(mine, channel_ids[None, :], channels), axis=1)]
    scatter x0 -> x1, local copies, waits for them, and re-layouts: none -> 1.48 us  [slot_table(): alive_mask = jnp.ones((channels,), jnp.bool_).at[flagged].set(False)]
    select_n x2 -> x3, other arithmetic: 0.03 us -> 1.38 us  [the longest x1 0.69 us: slot_table(): jnp.where(alive_mask, channel_ids, channels)]
    add x1 -> x0, other arithmetic: 1.22 us -> none  [slot_tables(): sin_rows = ((s1 * c2 + c1 * s2) * keep).reshape(channels, -1)]
  transfers between devices with their start and end apart: 1 -> 1, of which waited for: 0 -> 0; matrix products, arithmetic and copies ran while one was open for 11% -> 28% of each run, Pallas kernels for 0% -> 0%
where the time goes in v7:
time: 109 us
  blocking collectives  59.2 us (54%)
  other arithmetic  31.2 us (29%)
  Pallas kernels  10.8 us (10%)
  starting transfers between devices  3.95 us (4%)
  local copies, waits for them, and re-layouts  3.57 us (3%)
    all_to_all x1, blocking collectives, local(): received = lax.all_to_all(sending, ('tm', 'chan'), 0, 0, tiled=True)  59.2 us
    another operation x1, other arithmetic, slot_table(): jnp.zeros((devices,), jnp.int32).at[owners]  7.61 us
    another operation x1, other arithmetic, slot_table(): jnp.full((devices,), channels, jnp.int32).at[owners]  7.61 us
    scatter-add x1, other arithmetic, slot_table(): jnp.zeros((devices,), jnp.int32).at[owners]  7.61 us
    pallas_call x1, Pallas kernels, dft_payload(): pl.pallas_call(dft_kernel, grid=(steps,), in_specs=[pl.BlockSpec((2 * row...  5.67 us
    pallas_call x1, Pallas kernels, correlate(): pl.pallas_call(kernel, grid=(capacity,), in_specs=[pl.BlockSpec(received....  5.15 us
    ppermute x1, starting transfers between devices, from_behind(): return lax.ppermute(value, axis, pairs)  3.95 us
    convert_element_type x1, other arithmetic, slot_tables(): return (cos_rows.astype(jnp.bfloat16), sin_rows.astype(jnp.bfloat16))  3.33 us
  transfers between devices with their start and end apart: 1, of which 0 were waited for; matrix products, arithmetic and copies ran while one was open for 28% of the time, Pallas kernels for 0%

profile of v7, /device:TPU:1, one launch (start us, length us, event | category | flops | bytes accessed | tf_op | source)
XLA Modules:
  0.0 108.9 jit_solution(2307925945707386343)
XLA Ops:
  0.0 0.0 copy-start
  0.0 1.2 %copy.14 = bf16[4,32,2,1024]{3,1,0,2:T(8,128)(2,1)S(1)} copy(bf16[4,32,2,1024]{3,2,1,0:T(2,128)(2,1)} %param.4) | data formatting | bytes 1048576 | tf_op args[0]
  1.2 0.1 slice.100
  1.3 3.9 %collective-permute-start = (bf16[4,11,2,1024]{3,1,0,2:T(8,128)(2,1)S(1)}, bf16[4,11,2,1024]{3,1,0,2:T(8,128)(2,1)S(1)}, u32[]{:S(2)}, u32[]{:S(2)}) collective-permute-start(bf16[4,11,2,1024]{3,1,0,2:T(8,128)(2,1)S(1)} %slice.100), channel_id=1, source_target_pairs={{0,1},{1,2},{2,3},{4,5},{5,6},{6,7},{8,9},{9,10},{10,11},{12,13},{... | collective-permute-start | bytes 540680 | tf_op jit(solution)/shard_map/ppermute | solution.py:15
  5.2 0.7 compare_select_fusion.1
  5.9 1.5 %scatter_custom_fusion = pred[1024]{0:T(1024)(128)(4,1)S(1)} fusion(s32[256]{0:T(256)S(1)} %compare_select_fusion.1, pred[256]{0:T(512)(128)(4,1)S(1)} %broadcast.212, pred[]{:T(512)} %constant.16.clone.1), kind=kCustom, calls=%fused_computation.35 | custom fusion | bytes 1025 | tf_op jit(solution)/shard_map/scatter | solution.py:20
  7.4 0.7 iota_select_fusion.1
  8.1 7.6 %scatter_custom_fusion.1 = s32[512]{0:T(512)S(1)} fusion(s32[1024]{0:T(1024)S(1)} %get-tuple-element.33, s32[1024]{0:T(1024)S(1)} %convert_element_type.85, s32[]{:T(128)} %constant.14.clone.1), kind=kCustom, calls=%fused_computation.45 | custom fusion | flops 1024 | bytes 2052 | tf_op jit(solution)/shard_map/scatter-add | solution.py:21
  15.7 7.6 %scatter_custom_fusion.3 = s32[512]{0:T(512)S(1)} fusion(s32[1024]{0:T(1024)S(1)} %get-tuple-element.33, s32[1024]{0:T(1024)S(1)} %get-tuple-element.32, s32[]{:T(128)} %constant.14.clone.1), kind=kCustom, calls=%fused_computation.41 | custom fusion | flops 1024 | bytes 2052 | tf_op jit(solution)/shard_map/scatter-max | solution.py:23
  23.4 7.6 %scatter_custom_fusion.2 = s32[512]{0:T(512)S(1)} fusion(s32[1024]{0:T(1024)S(1)} %get-tuple-element.33, s32[1024]{0:T(1024)S(1)} %get-tuple-element.31, s32[]{:T(128)} %constant.17.clone.1), kind=kCustom, calls=%fused_computation.38 | custom fusion | flops 1024 | bytes 2052 | tf_op jit(solution)/shard_map/scatter-min | solution.py:22
  31.0 0.1 stack.21
  31.1 0.1 copy.18
  31.2 0.1 stack.22
  31.3 0.1 copy.19
  31.4 0.1 stack.18
  31.6 0.1 copy.16
  31.6 0.1 stack.19
  31.8 0.1 copy.17
  31.8 1.1 fusion.10
  32.9 3.3 %add_convert_fusion = (bf16[32,32,1024]{2,1,0:T(8,128)(2,1)}, bf16[32,32,1024]{2,1,0:T(8,128)(2,1)}) fusion(f32[32,1024]{1,0:T(8,128)S(1)} %get-tuple-element.27, f32[32,1024]{1,0:T(8,128)S(1)} %get-tuple-element.26, f32[32,1024]{1,0:T(8,128)S(1)} %get-tuple-element.28, f32[32,1024]{1,0:T(8,128)S(1)} %get-tuple-element.25), kind=kLoop, calls=%fused_computation.4 | loop fusion | flops 8388608 | bytes 4718592 | tf_op jit(solution)/shard_map/convert_element_type | solution.py:43
  36.2 0.0 copy-done
  36.3 0.0 collective-permute-done
  36.3 0.2 maximum_bitcast_fusion
  36.5 2.4 %add_convert_fusion.1 = bf16[2,4,32,1024]{3,2,1,0:T(8,128)(2,1)} fusion(bf16[2,4,43,1024]{3,2,1,0:T(8,128)(2,1)S(1)} %maximum_bitcast_fusion, f32[1024]{0:T(1024)S(1)} %bitcast.41, f32[1024]{0:T(1024)S(1)} %bitcast.42, f32[1024]{0:T(1024)S(1)} %bitcast.32, f32[1024]{0:T(1024)S(1)} %bitcast.33, f32[1024]{0:T(1024)S(1)} %bitcast.34, f32[1024]{0:T(1024)S(1)} %bitcast.35, ...), kind=kLoop, calls=%fused_computation.6 | loop fusion | flops 9437184 | bytes 6864896 | tf_op jit(solution)/shard_map/convert_element_type | solution.py:93
  38.9 5.7 %shard_map.46 = bf16[512,4,128]{2,1,0:T(4,128)(2,1)} custom-call(bf16[256,1024]{1,0:T(8,128)(2,1)} %bitcast.28, bf16[1024,1024]{1,0:T(8,128)(2,1)} %bitcast.26, bf16[1024,1024]{1,0:T(8,128)(2,1)} %bitcast.27, bf16[1024,1024]{1,0:T(8,128)(2,1)} %bitcast.24, bf16[1024,1024]{1,0:T(8,128)(2,1)} %bitcast.25), custom_call_target="tpu_custom_call" | custom-call | tf_op jit(solution)/shard_map/pallas_call | solution.py:64
  44.5 59.2 %all_to_all.5.r_ref = bf16[512,4,128]{2,1,0:T(4,128)(2,1)} all-to-all(bf16[512,4,128]{2,1,0:T(4,128)(2,1)} %shard_map.46), channel_id=1, replica_groups=mesh['chan'=128,'tm'=4] {'tm','chan'}, dimensions={0} | all-to-all | bytes 1048576 | tf_op jit(solution)/shard_map/all_to_all | solution.py:104
  103.7 5.2 %shard_map.47 = f32[2,2,512,512]{3,2,1,0:T(8,128)} custom-call(bf16[512,4,128]{2,1,0:T(4,128)(2,1)} %all_to_all.5.r_ref), custom_call_target="tpu_custom_call" | custom-call | tf_op jit(solution)/shard_map/pallas_call | solution.py:146
  (7 shorter events, 0.1 us)
Async XLA Ops:
  0.0 36.2 %copy-start = (f32[12,1024]{1,0:T(8,128)S(1)}, f32[12,1024]{1,0:T(8,128)}, u32[]{:S(2)}) copy-start(f32[12,1024]{1,0:T(8,128)} %param.5) | copy-start | bytes 147460
  1.3 35.0 %collective-permute-start = (bf16[4,11,2,1024]{3,1,0,2:T(8,128)(2,1)S(1)}, bf16[4,11,2,1024]{3,1,0,2:T(8,128)(2,1)S(1)}, u32[]{:S(2)}, u32[]{:S(2)}) collective-permute-start(bf16[4,11,2,1024]{3,1,0,2:T(8,128)(2,1)S(1)} %slice.100), channel_id=1, source_target_pairs={{0,1},{1,2},{2,3},{4,5},{5,6},{6,7},{8,9},{9,10},{10,11},{12,13},{... | collective-permute-start | bytes 540680 | tf_op jit(solution)/shard_map/ppermute | solution.py:15

commit v8 on v6

--- a/solution.py
+++ b/solution.py
@@ -19,10 +19,10 @@
     channel_ids = jnp.arange(channels, dtype=jnp.int32)
     alive_mask = jnp.logical_not(jnp.any(flagged[:, None] == channel_ids[None, :], axis=0))
     device_ids = jnp.arange(devices, dtype=jnp.int32)
-    mine = (owners[None, :] == device_ids[:, None]) & alive_mask[None, :]
-    count = jnp.sum(mine.astype(jnp.int32), axis=1)
-    lower = jnp.min(jnp.where(mine, channel_ids[None, :], channels), axis=1)
-    upper = jnp.max(jnp.where(mine, channel_ids[None, :], 0), axis=1)
+    mine = (owners[:, None] == device_ids[None, :]) & alive_mask[:, None]
+    count = jnp.sum(mine.astype(jnp.int32), axis=0)
+    lower = jnp.min(jnp.where(mine, channel_ids[:, None], channels), axis=0)
+    upper = jnp.max(jnp.where(mine, channel_ids[:, None], 0), axis=0)
     chosen = jnp.stack([jnp.where(count > 0, lower, 0), jnp.where(count > 1, upper, 0)], axis=1)
     present = jnp.stack([count > 0, count > 1], axis=1)
     return (chosen.reshape(-1), present.reshape(-1))

time: 87.4 us -> 87.4 us (level)
  no operation moved by 1% of the time
where the time goes in v8:
time: 87.4 us; the launch traced here: 87.1 us
  blocking collectives  59.2 us (68%)
  other arithmetic  11 us (13%)
  Pallas kernels  10.8 us (12%)
  starting transfers between devices  3.95 us (5%)
  local copies, waits for them, and re-layouts  2 us (2%)
    all_to_all x1, blocking collectives, local(): received = lax.all_to_all(sending, ('tm', 'chan'), 0, 0, tiled=True)  59.2 us
    pallas_call x1, Pallas kernels, dft_payload(): pl.pallas_call(dft_kernel, grid=(steps,), in_specs=[pl.BlockSpec((2 * row...  5.67 us
    pallas_call x1, Pallas kernels, correlate(): pl.pallas_call(kernel, grid=(capacity,), in_specs=[pl.BlockSpec(received....  5.15 us
    ppermute x1, starting transfers between devices, from_behind(): return lax.ppermute(value, axis, pairs)  3.95 us
    convert_element_type x1, other arithmetic, slot_tables(): return (cos_rows.astype(jnp.bfloat16), sin_rows.astype(jnp.bfloat16))  3.3 us
    convert_element_type x1, other arithmetic, local(): running.astype(jnp.bfloat16).reshape(2 * inp_dev * spec_dev, channels)  2.39 us
    reduce_min x1, other arithmetic, slot_table(): lower = jnp.min(jnp.where(mine, channel_ids[:, None], channels), axis=0)  1.83 us
  transfers between devices with their start and end apart: 1, of which 0 were waited for; matrix products, arithmetic and copies ran while one was open for 11% of the time, Pallas kernels for 0%

profile of v8, /device:TPU:1, one launch (start us, length us, event | category | flops | bytes accessed | tf_op | source)
XLA Modules:
  0.0 87.1 jit_solution(10436704363792372629)
XLA Ops:
  0.0 1.1 %copy.19 = bf16[4,32,2,1024]{3,1,0,2:T(8,128)(2,1)S(1)} copy(bf16[4,32,2,1024]{3,2,1,0:T(2,128)(2,1)} %param.4) | data formatting | bytes 1048576 | tf_op args[0]
  1.2 0.1 slice.100
  1.2 3.9 %collective-permute-start = (bf16[4,11,2,1024]{3,1,0,2:T(8,128)(2,1)S(1)}, bf16[4,11,2,1024]{3,1,0,2:T(8,128)(2,1)S(1)}, u32[]{:S(2)}, u32[]{:S(2)}) collective-permute-start(bf16[4,11,2,1024]{3,1,0,2:T(8,128)(2,1)S(1)} %slice.100), channel_id=1, source_target_pairs={{0,1},{1,2},{2,3},{4,5},{5,6},{6,7},{8,9},{9,10},{10,11},{12,13},{... | collective-permute-start | bytes 540680 | tf_op jit(solution)/shard_map/ppermute | solution.py:15
  5.2 0.9 %fusion.3 = pred[1024]{0:T(1024)(128)(4,1)S(1)} fusion(s32[256]{0:T(256)} %param.6), kind=kLoop, calls=%fused_computation.13 | loop fusion | flops 523264 | bytes 2048 | tf_op jit(solution)/shard_map/reduce_or | solution.py:20
  6.1 1.8 %select_reduce_fusion.1 = (s32[512]{0:T(512)S(1)}, s32[512]{0:T(512)S(1)}, s32[512]{0:T(512)S(1)}) fusion(s32[1024]{0:T(1024)} %param.7, pred[1024]{0:T(1024)(128)(4,1)S(1)} %not.7), kind=kLoop, calls=%fused_computation.7 | loop fusion | flops 4192768 | bytes 11264 | tf_op jit(solution)/shard_map/reduce_min | solution.py:24
  8.0 0.1 gt.41
  8.1 0.1 reduce_min.12
  8.2 0.1 copy.23
  8.3 0.1 copy.21
  8.4 0.1 gt.43
  8.5 0.1 reduce_max.12
  8.6 0.1 copy.24
  8.7 0.1 copy.22
  8.8 1.1 %fusion.16 = (f32[32,1024]{1,0:T(8,128)S(1)}, f32[32,1024]{1,0:T(8,128)S(1)}, f32[32,1024]{1,0:T(8,128)S(1)}, f32[32,1024]{1,0:T(8,128)S(1)}) fusion(s32[1024]{0:T(1024)S(1)} %bitcast.31, s32[32]{0:T(128)S(1)} %iota_multiply_fusion), kind=kLoop, calls=%fused_computation.35 | loop fusion | flops 917504 | bytes 528512 | tf_op jit(solution)/shard_map/cos | solution.py:39
  9.9 1.2 %multiply_add_fusion = (f32[32,32,1024]{2,1,0:T(8,128)S(1)}, f32[32,32,1024]{2,1,0:T(8,128)S(1)}) fusion(f32[32,1024]{1,0:T(8,128)S(1)} %get-tuple-element.26, f32[32,1024]{1,0:T(8,128)S(1)} %get-tuple-element.23, f32[32,1024]{1,0:T(8,128)S(1)} %get-tuple-element.27, f32[32,1024]{1,0:T(8,128)S(1)} %get-tuple-element.22), kind=kLoop, calls=%fused_computation.4 | loop fusion | flops 6291456 | bytes 8912896 | tf_op jit(solution)/shard_map/add | solution.py:44
  11.1 0.0 copy-start
  11.1 3.3 %fusion = (bf16[1024,1024]{1,0:T(8,128)(2,1)}, bf16[1024,1024]{1,0:T(8,128)(2,1)}) fusion(f32[32,32,1024]{2,1,0:T(8,128)S(1)} %get-tuple-element.8, f32[1024]{0:T(1024)S(1)} %bitcast.30, f32[32,32,1024]{2,1,0:T(8,128)S(1)} %get-tuple-element.9), kind=kLoop, calls=%fused_computation.1 | loop fusion | flops 4194304 | bytes 12587008 | tf_op jit(solution)/shard_map/convert_element_type | solution.py:45
  14.4 0.0 copy-done
  14.5 0.0 collective-permute-done
  14.5 0.2 maximum_bitcast_fusion
  14.7 2.4 %add_convert_fusion = bf16[2,4,32,1024]{3,2,1,0:T(8,128)(2,1)} fusion(bf16[2,4,43,1024]{3,2,1,0:T(8,128)(2,1)S(1)} %maximum_bitcast_fusion, f32[1024]{0:T(1024)S(1)} %bitcast.42, f32[1024]{0:T(1024)S(1)} %bitcast.43, f32[1024]{0:T(1024)S(1)} %bitcast.33, f32[1024]{0:T(1024)S(1)} %bitcast.34, f32[1024]{0:T(1024)S(1)} %bitcast.35, f32[1024]{0:T(1024)S(1)} %bitcast.36, ...), kind=kLoop, calls=%fused_computation.12 | loop fusion | flops 9437184 | bytes 6864896 | tf_op jit(solution)/shard_map/convert_element_type | solution.py:95
  17.1 5.7 %shard_map.46 = bf16[512,4,128]{2,1,0:T(4,128)(2,1)} custom-call(bf16[256,1024]{1,0:T(8,128)(2,1)} %bitcast.29, bf16[1024,1024]{1,0:T(8,128)(2,1)} %get-tuple-element.25.c0_ref.c1_ref, bf16[1024,1024]{1,0:T(8,128)(2,1)} %get-tuple-element.25.c0_ref.c1_ref, bf16[1024,1024]{1,0:T(8,128)(2,1)} %get-tuple-element.24.s0_ref.s1_ref, ...), custom_call_target="tpu_custom_call" | custom-call | tf_op jit(solution)/shard_map/pallas_call | solution.py:66
  22.7 59.2 %all_to_all.5.r_ref = bf16[512,4,128]{2,1,0:T(4,128)(2,1)} all-to-all(bf16[512,4,128]{2,1,0:T(4,128)(2,1)} %shard_map.46), channel_id=1, replica_groups=mesh['chan'=128,'tm'=4] {'tm','chan'}, dimensions={0} | all-to-all | bytes 1048576 | tf_op jit(solution)/shard_map/all_to_all | solution.py:106
  82.0 5.2 %shard_map.47 = f32[2,2,512,512]{3,2,1,0:T(8,128)} custom-call(bf16[512,4,128]{2,1,0:T(4,128)(2,1)} %all_to_all.5.r_ref), custom_call_target="tpu_custom_call" | custom-call | tf_op jit(solution)/shard_map/pallas_call | solution.py:148
  (8 shorter events, 0.1 us)
Async XLA Ops:
  1.2 13.2 %collective-permute-start = (bf16[4,11,2,1024]{3,1,0,2:T(8,128)(2,1)S(1)}, bf16[4,11,2,1024]{3,1,0,2:T(8,128)(2,1)S(1)}, u32[]{:S(2)}, u32[]{:S(2)}) collective-permute-start(bf16[4,11,2,1024]{3,1,0,2:T(8,128)(2,1)S(1)} %slice.100), channel_id=1, source_target_pairs={{0,1},{1,2},{2,3},{4,5},{5,6},{6,7},{8,9},{9,10},{10,11},{12,13},{... | collective-permute-start | bytes 540680 | tf_op jit(solution)/shard_map/ppermute | solution.py:15
  11.1 3.3 %copy-start = (f32[12,1024]{1,0:T(8,128)S(1)}, f32[12,1024]{1,0:T(8,128)}, u32[]{:S(2)}) copy-start(f32[12,1024]{1,0:T(8,128)} %param.5) | copy-start | bytes 147460

commit v9 on v8

--- a/solution.py
+++ b/solution.py
@@ -48,13 +48,12 @@
 def dft_kernel(x_ref, c0_ref, c1_ref, s0_ref, s1_ref, o_ref):
     x = x_ref[...]
     half = x.shape[0] // 2
+    tn = (((0,), (1,)), ((), ()))
     for cap, (c_ref, s_ref) in enumerate(((c0_ref, s0_ref), (c1_ref, s1_ref))):
-        cos_part = jnp.dot(x, c_ref[...], preferred_element_type=jnp.float32)
-        sin_part = jnp.dot(x, s_ref[...], preferred_element_type=jnp.float32)
-        real_part = cos_part[:half] + sin_part[half:]
-        imag_part = cos_part[half:] - sin_part[:half]
-        o_ref[:, 2 * cap, :] = real_part.T.astype(o_ref.dtype)
-        o_ref[:, 2 * cap + 1, :] = imag_part.T.astype(o_ref.dtype)
+        cos_part = lax.dot_general(c_ref[...], x, tn, preferred_element_type=jnp.float32)
+        sin_part = lax.dot_general(s_ref[...], x, tn, preferred_element_type=jnp.float32)
+        o_ref[:, 2 * cap, :] = (cos_part[:, :half] + sin_part[:, half:]).astype(o_ref.dtype)
+        o_ref[:, 2 * cap + 1, :] = (cos_part[:, half:] - sin_part[:, :half]).astype(o_ref.dtype)
 
 
 def dft_payload(filtered, cos_rows, sin_rows, devices, capacity):

time: 87.4 us -> 87.4 us (level)
  no operation moved by 1% of the time
where the time goes in v9:
time: 87.4 us; the launch traced here: 87.1 us
  blocking collectives  59.2 us (68%)
  other arithmetic  11 us (13%)
  Pallas kernels  10.8 us (12%)
  starting transfers between devices  3.95 us (5%)
  local copies, waits for them, and re-layouts  2 us (2%)
    all_to_all x1, blocking collectives, local(): received = lax.all_to_all(sending, ('tm', 'chan'), 0, 0, tiled=True)  59.2 us
    pallas_call x1, Pallas kernels, dft_payload(): pl.pallas_call(dft_kernel, grid=(steps,), in_specs=[pl.BlockSpec((2 * row...  5.62 us
    pallas_call x1, Pallas kernels, correlate(): pl.pallas_call(kernel, grid=(capacity,), in_specs=[pl.BlockSpec(received....  5.15 us
    ppermute x1, starting transfers between devices, from_behind(): return lax.ppermute(value, axis, pairs)  3.95 us
    convert_element_type x1, other arithmetic, slot_tables(): return (cos_rows.astype(jnp.bfloat16), sin_rows.astype(jnp.bfloat16))  3.3 us
    convert_element_type x1, other arithmetic, local(): running.astype(jnp.bfloat16).reshape(2 * inp_dev * spec_dev, channels)  2.39 us
    reduce_min x1, other arithmetic, slot_table(): lower = jnp.min(jnp.where(mine, channel_ids[:, None], channels), axis=0)  1.83 us
  transfers between devices with their start and end apart: 1, of which 0 were waited for; matrix products, arithmetic and copies ran while one was open for 11% of the time, Pallas kernels for 0%

profile of v9, /device:TPU:1, one launch (start us, length us, event | category | flops | bytes accessed | tf_op | source)
XLA Modules:
  0.0 87.1 jit_solution(2493995858642827692)
XLA Ops:
  0.0 1.1 %copy.19 = bf16[4,32,2,1024]{3,1,0,2:T(8,128)(2,1)S(1)} copy(bf16[4,32,2,1024]{3,2,1,0:T(2,128)(2,1)} %param.4) | data formatting | bytes 1048576 | tf_op args[0]
  1.2 0.1 slice.100
  1.2 3.9 %collective-permute-start = (bf16[4,11,2,1024]{3,1,0,2:T(8,128)(2,1)S(1)}, bf16[4,11,2,1024]{3,1,0,2:T(8,128)(2,1)S(1)}, u32[]{:S(2)}, u32[]{:S(2)}) collective-permute-start(bf16[4,11,2,1024]{3,1,0,2:T(8,128)(2,1)S(1)} %slice.100), channel_id=1, source_target_pairs={{0,1},{1,2},{2,3},{4,5},{5,6},{6,7},{8,9},{9,10},{10,11},{12,13},{... | collective-permute-start | bytes 540680 | tf_op jit(solution)/shard_map/ppermute | solution.py:15
  5.2 0.9 %fusion.3 = pred[1024]{0:T(1024)(128)(4,1)S(1)} fusion(s32[256]{0:T(256)} %param.6), kind=kLoop, calls=%fused_computation.13 | loop fusion | flops 523264 | bytes 2048 | tf_op jit(solution)/shard_map/reduce_or | solution.py:20
  6.1 1.8 %select_reduce_fusion.1 = (s32[512]{0:T(512)S(1)}, s32[512]{0:T(512)S(1)}, s32[512]{0:T(512)S(1)}) fusion(s32[1024]{0:T(1024)} %param.7, pred[1024]{0:T(1024)(128)(4,1)S(1)} %not.7), kind=kLoop, calls=%fused_computation.7 | loop fusion | flops 4192768 | bytes 11264 | tf_op jit(solution)/shard_map/reduce_min | solution.py:24
  8.0 0.1 gt.41
  8.1 0.1 reduce_min.12
  8.2 0.1 copy.23
  8.3 0.1 copy.21
  8.4 0.1 gt.43
  8.5 0.1 reduce_max.12
  8.6 0.1 copy.24
  8.7 0.1 copy.22
  8.8 1.1 %fusion.16 = (f32[32,1024]{1,0:T(8,128)S(1)}, f32[32,1024]{1,0:T(8,128)S(1)}, f32[32,1024]{1,0:T(8,128)S(1)}, f32[32,1024]{1,0:T(8,128)S(1)}) fusion(s32[1024]{0:T(1024)S(1)} %bitcast.31, s32[32]{0:T(128)S(1)} %iota_multiply_fusion), kind=kLoop, calls=%fused_computation.35 | loop fusion | flops 917504 | bytes 528512 | tf_op jit(solution)/shard_map/cos | solution.py:39
  9.9 1.2 %multiply_add_fusion = (f32[32,32,1024]{2,1,0:T(8,128)S(1)}, f32[32,32,1024]{2,1,0:T(8,128)S(1)}) fusion(f32[32,1024]{1,0:T(8,128)S(1)} %get-tuple-element.26, f32[32,1024]{1,0:T(8,128)S(1)} %get-tuple-element.23, f32[32,1024]{1,0:T(8,128)S(1)} %get-tuple-element.27, f32[32,1024]{1,0:T(8,128)S(1)} %get-tuple-element.22), kind=kLoop, calls=%fused_computation.4 | loop fusion | flops 6291456 | bytes 8912896 | tf_op jit(solution)/shard_map/add | solution.py:44
  11.1 0.0 copy-start
  11.1 3.3 %fusion = (bf16[1024,1024]{1,0:T(8,128)(2,1)}, bf16[1024,1024]{1,0:T(8,128)(2,1)}) fusion(f32[32,32,1024]{2,1,0:T(8,128)S(1)} %get-tuple-element.8, f32[1024]{0:T(1024)S(1)} %bitcast.30, f32[32,32,1024]{2,1,0:T(8,128)S(1)} %get-tuple-element.9), kind=kLoop, calls=%fused_computation.1 | loop fusion | flops 4194304 | bytes 12587008 | tf_op jit(solution)/shard_map/convert_element_type | solution.py:45
  14.4 0.0 copy-done
  14.5 0.0 collective-permute-done
  14.5 0.2 maximum_bitcast_fusion
  14.7 2.4 %add_convert_fusion = bf16[2,4,32,1024]{3,2,1,0:T(8,128)(2,1)} fusion(bf16[2,4,43,1024]{3,2,1,0:T(8,128)(2,1)S(1)} %maximum_bitcast_fusion, f32[1024]{0:T(1024)S(1)} %bitcast.42, f32[1024]{0:T(1024)S(1)} %bitcast.43, f32[1024]{0:T(1024)S(1)} %bitcast.33, f32[1024]{0:T(1024)S(1)} %bitcast.34, f32[1024]{0:T(1024)S(1)} %bitcast.35, f32[1024]{0:T(1024)S(1)} %bitcast.36, ...), kind=kLoop, calls=%fused_computation.12 | loop fusion | flops 9437184 | bytes 6864896 | tf_op jit(solution)/shard_map/convert_element_type | solution.py:94
  17.1 5.6 %shard_map.46 = bf16[512,4,128]{2,1,0:T(4,128)(2,1)} custom-call(bf16[256,1024]{1,0:T(8,128)(2,1)} %bitcast.29, bf16[1024,1024]{1,0:T(8,128)(2,1)} %get-tuple-element.25.c0_ref.c1_ref, bf16[1024,1024]{1,0:T(8,128)(2,1)} %get-tuple-element.25.c0_ref.c1_ref, bf16[1024,1024]{1,0:T(8,128)(2,1)} %get-tuple-element.24.s0_ref.s1_ref, ...), custom_call_target="tpu_custom_call" | custom-call | tf_op jit(solution)/shard_map/pallas_call | solution.py:65
  22.7 59.2 %all_to_all.5.r_ref = bf16[512,4,128]{2,1,0:T(4,128)(2,1)} all-to-all(bf16[512,4,128]{2,1,0:T(4,128)(2,1)} %shard_map.46), channel_id=1, replica_groups=mesh['chan'=128,'tm'=4] {'tm','chan'}, dimensions={0} | all-to-all | bytes 1048576 | tf_op jit(solution)/shard_map/all_to_all | solution.py:105
  81.9 5.2 %shard_map.47 = f32[2,2,512,512]{3,2,1,0:T(8,128)} custom-call(bf16[512,4,128]{2,1,0:T(4,128)(2,1)} %all_to_all.5.r_ref), custom_call_target="tpu_custom_call" | custom-call | tf_op jit(solution)/shard_map/pallas_call | solution.py:147
  (8 shorter events, 0.1 us)
Async XLA Ops:
  1.2 13.2 %collective-permute-start = (bf16[4,11,2,1024]{3,1,0,2:T(8,128)(2,1)S(1)}, bf16[4,11,2,1024]{3,1,0,2:T(8,128)(2,1)S(1)}, u32[]{:S(2)}, u32[]{:S(2)}) collective-permute-start(bf16[4,11,2,1024]{3,1,0,2:T(8,128)(2,1)S(1)} %slice.100), channel_id=1, source_target_pairs={{0,1},{1,2},{2,3},{4,5},{5,6},{6,7},{8,9},{9,10},{10,11},{12,13},{... | collective-permute-start | bytes 540680 | tf_op jit(solution)/shard_map/ppermute | solution.py:15
  11.1 3.3 %copy-start = (f32[12,1024]{1,0:T(8,128)S(1)}, f32[12,1024]{1,0:T(8,128)}, u32[]{:S(2)}) copy-start(f32[12,1024]{1,0:T(8,128)} %param.5) | copy-start | bytes 147460

commit v10 on v9

--- a/solution.py
+++ b/solution.py
@@ -28,7 +28,7 @@
     return (chosen.reshape(-1), present.reshape(-1))
 
 
-def slot_tables(chosen, present, channels):
+def slot_factors(chosen, present, channels):
     low = 32
     high = channels // low
     step = 2.0 * math.pi / channels
@@ -36,45 +36,46 @@
     lo = jnp.arange(low, dtype=jnp.int32)
     angle_hi = ((hi[:, None] * low * chosen[None, :]) % channels).astype(jnp.float32) * step
     angle_lo = ((lo[:, None] * chosen[None, :]) % channels).astype(jnp.float32) * step
-    c1, s1 = jnp.cos(angle_hi)[:, None, :], jnp.sin(angle_hi)[:, None, :]
-    c2, s2 = jnp.cos(angle_lo)[None, :, :], jnp.sin(angle_lo)[None, :, :]
-    factor = 1.0 / math.sqrt(channels)
-    keep = jnp.where(present, factor, 0.0).astype(jnp.float32)[None, None, :]
-    cos_rows = ((c1 * c2 - s1 * s2) * keep).reshape(channels, -1)
-    sin_rows = ((s1 * c2 + c1 * s2) * keep).reshape(channels, -1)
-    return cos_rows.astype(jnp.bfloat16), sin_rows.astype(jnp.bfloat16)
+    keep = jnp.where(present, 1.0 / math.sqrt(channels), 0.0).astype(jnp.float32)[None, :]
+    return (jnp.cos(angle_hi), jnp.sin(angle_hi), jnp.cos(angle_lo) * keep, jnp.sin(angle_lo) * keep)
 
 
-def dft_kernel(x_ref, c0_ref, c1_ref, s0_ref, s1_ref, o_ref):
+def dft_kernel(x_ref, *refs):
+    factor_refs, o_ref = refs[:-1], refs[-1]
     x = x_ref[...]
     half = x.shape[0] // 2
+    channels = x.shape[1]
     tn = (((0,), (1,)), ((), ()))
-    for cap, (c_ref, s_ref) in enumerate(((c0_ref, s0_ref), (c1_ref, s1_ref))):
-        cos_part = lax.dot_general(c_ref[...], x, tn, preferred_element_type=jnp.float32)
-        sin_part = lax.dot_general(s_ref[...], x, tn, preferred_element_type=jnp.float32)
+    for cap in range(len(factor_refs) // 4):
+        c1, s1, c2, s2 = (r[...] for r in factor_refs[4 * cap : 4 * cap + 4])
+        c1, s1 = c1[:, None, :], s1[:, None, :]
+        c2, s2 = c2[None, :, :], s2[None, :, :]
+        cos_rows = (c1 * c2 - s1 * s2).reshape(channels, -1).astype(jnp.bfloat16)
+        sin_rows = (s1 * c2 + c1 * s2).reshape(channels, -1).astype(jnp.bfloat16)
+        cos_part = lax.dot_general(cos_rows, x, tn, preferred_element_type=jnp.float32)
+        sin_part = lax.dot_general(sin_rows, x, tn, preferred_element_type=jnp.float32)
         o_ref[:, 2 * cap, :] = (cos_part[:, :half] + sin_part[:, half:]).astype(o_ref.dtype)
         o_ref[:, 2 * cap + 1, :] = (cos_part[:, half:] - sin_part[:, :half]).astype(o_ref.dtype)
 
 
-def dft_payload(filtered, cos_rows, sin_rows, devices, capacity):
+def dft_payload(filtered, factors, devices, capacity):
     channels = filtered.shape[1]
     rows = filtered.shape[0] // 2
     block = 512
     steps = devices // block
-    table_spec = lambda cap: pl.BlockSpec((channels, block), lambda j: (0, j + cap * steps))
+    specs = []
+    operands = []
+    for cap in range(capacity):
+        for f in factors:
+            specs.append(pl.BlockSpec((f.shape[0], block), lambda j, cap=cap: (0, j + cap * steps)))
+            operands.append(f)
     return pl.pallas_call(
         dft_kernel,
         grid=(steps,),
-        in_specs=[
-            pl.BlockSpec((2 * rows, channels), lambda j: (0, 0)),
-            table_spec(0),
-            table_spec(1),
-            table_spec(0),
-            table_spec(1),
-        ],
+        in_specs=[pl.BlockSpec((2 * rows, channels), lambda j: (0, 0))] + specs,
         out_specs=pl.BlockSpec((block, capacity * 2, rows), lambda j: (j, 0, 0)),
         out_shape=jax.ShapeDtypeStruct((devices, capacity * 2, rows), jnp.bfloat16),
-    )(filtered, cos_rows, cos_rows, sin_rows, sin_rows)
+    )(filtered, *operands)
 
 
 def local(voltages, filter_taps, flagged, owners):
@@ -100,8 +101,8 @@
     chosen, present = slot_table(flagged, owners, channels, devices)
     chosen = chosen.reshape(chan_count, time_count, capacity).transpose(2, 1, 0).reshape(-1)
     present = present.reshape(chan_count, time_count, capacity).transpose(2, 1, 0).reshape(-1)
-    cos_rows, sin_rows = slot_tables(chosen, present, channels)
-    sending = dft_payload(filtered, cos_rows, sin_rows, devices, capacity)
+    factors = slot_factors(chosen, present, channels)
+    sending = dft_payload(filtered, factors, devices, capacity)
     received = lax.all_to_all(sending, ("tm", "chan"), 0, 0, tiled=True)
     return correlate(received, time_count, chan_count, capacity, inp_dev)
 

time: 87.4 us -> 84 us (0.961)
  other arithmetic: 11 us -> 7.11 us
  blocking collectives: 59.2 us -> 60.5 us
  Pallas kernels: 10.8 us -> 9.91 us
    convert_element_type x1 -> x0, other arithmetic: 3.3 us -> none  [slot_tables(): return (cos_rows.astype(jnp.bfloat16), sin_rows.astype(jnp.bfloat16))]
    mul x1 -> x2, other arithmetic: 0.01 us -> 1.78 us  [the longest x1 1.78 us: slot_factors(): jnp.sin(angle_lo) * keep]
    all_to_all x1, blocking collectives: 59.2 us -> 60.5 us  [local(): received = lax.all_to_all(sending, ('tm', 'chan'), 0, 0, tiled=True)]
    add x1 -> x0, other arithmetic: 1.22 us -> none  [slot_tables(): sin_rows = ((s1 * c2 + c1 * s2) * keep).reshape(channels, -1)]
    cos x1 -> x0, other arithmetic: 1.07 us -> none  [slot_tables(): c1, s1 = (jnp.cos(angle_hi)[:, None, :], jnp.sin(angle_hi)[:, None, :])]
  transfers between devices with their start and end apart: 1 -> 1, of which waited for: 0 -> 0; matrix products, arithmetic and copies ran while one was open for 11% -> 6% of each run, Pallas kernels for 0% -> 0%
where the time goes in v10:
time: 84 us; the launch traced here: 83.7 us
  blocking collectives  60.5 us (72%)
  Pallas kernels  9.91 us (12%)
  other arithmetic  7.11 us (8%)
  starting transfers between devices  3.95 us (5%)
  local copies, waits for them, and re-layouts  2.08 us (2%)
    all_to_all x1, blocking collectives, local(): received = lax.all_to_all(sending, ('tm', 'chan'), 0, 0, tiled=True)  60.5 us
    pallas_call x1, Pallas kernels, correlate(): pl.pallas_call(kernel, grid=(capacity,), in_specs=[pl.BlockSpec(received....  5.15 us
    pallas_call x1, Pallas kernels, dft_payload(): pl.pallas_call(dft_kernel, grid=(steps,), in_specs=[pl.BlockSpec((2 * row...  4.76 us
    ppermute x1, starting transfers between devices, from_behind(): return lax.ppermute(value, axis, pairs)  3.95 us
    convert_element_type x1, other arithmetic, local(): running.astype(jnp.bfloat16).reshape(2 * inp_dev * spec_dev, channels)  2.38 us
    reduce_min x1, other arithmetic, slot_table(): lower = jnp.min(jnp.where(mine, channel_ids[:, None], channels), axis=0)  1.83 us
    mul x1, other arithmetic, slot_factors(): jnp.sin(angle_lo) * keep  1.78 us
  transfers between devices with their start and end apart: 1, of which 0 were waited for; matrix products, arithmetic and copies ran while one was open for 6% of the time, Pallas kernels for 0%

profile of v10, /device:TPU:1, one launch (start us, length us, event | category | flops | bytes accessed | tf_op | source)
XLA Modules:
  0.0 83.7 jit_solution(1371979174322578149)
XLA Ops:
  0.0 0.0 copy-start
  0.0 1.2 %copy.19 = bf16[4,32,2,1024]{3,1,0,2:T(8,128)(2,1)S(1)} copy(bf16[4,32,2,1024]{3,2,1,0:T(2,128)(2,1)} %param.4) | data formatting | bytes 1048576 | tf_op args[0]
  1.2 0.1 slice.100
  1.3 3.9 %collective-permute-start = (bf16[4,11,2,1024]{3,1,0,2:T(8,128)(2,1)S(1)}, bf16[4,11,2,1024]{3,1,0,2:T(8,128)(2,1)S(1)}, u32[]{:S(2)}, u32[]{:S(2)}) collective-permute-start(bf16[4,11,2,1024]{3,1,0,2:T(8,128)(2,1)S(1)} %slice.100), channel_id=1, source_target_pairs={{0,1},{1,2},{2,3},{4,5},{5,6},{6,7},{8,9},{9,10},{10,11},{12,13},{... | collective-permute-start | bytes 540680 | tf_op jit(solution)/shard_map/ppermute | solution.py:15
  5.2 0.9 %fusion.1 = pred[1024]{0:T(1024)(128)(4,1)S(1)} fusion(s32[256]{0:T(256)} %param.6), kind=kLoop, calls=%fused_computation.7 | loop fusion | flops 523264 | bytes 2048 | tf_op jit(solution)/shard_map/reduce_or | solution.py:20
  6.1 1.8 %select_reduce_fusion.1 = (s32[512]{0:T(512)S(1)}, s32[512]{0:T(512)S(1)}, s32[512]{0:T(512)S(1)}) fusion(s32[1024]{0:T(1024)} %param.7, pred[1024]{0:T(1024)(128)(4,1)S(1)} %not.7), kind=kLoop, calls=%fused_computation.1 | loop fusion | flops 4192768 | bytes 11264 | tf_op jit(solution)/shard_map/reduce_min | solution.py:24
  8.0 0.1 gt.41
  8.1 0.1 copy.23
  8.2 0.1 gt.43
  8.3 0.1 copy.24
  8.4 0.1 reduce_min.12
  8.6 0.1 copy.21
  8.6 0.1 reduce_max.12
  8.8 0.1 copy.22
  8.9 1.8 %sine_multiply_fusion = (f32[32,1024]{1,0:T(8,128)}, f32[32,1024]{1,0:T(8,128)}, f32[32,1024]{1,0:T(8,128)}, f32[32,1024]{1,0:T(8,128)}) fusion(f32[1024]{0:T(1024)S(1)} %bitcast.22, s32[1024]{0:T(1024)S(1)} %bitcast.23, s32[32]{0:T(128)S(1)} %iota_multiply_fusion), kind=kLoop, calls=%fused_computation.23 | loop fusion | flops 983040 | bytes 532608 | tf_op jit(solution)/shard_map/mul | solution.py:40
  10.7 0.0 copy-done
  10.7 0.0 collective-permute-done
  10.7 0.2 maximum_bitcast_fusion
  10.9 2.4 %add_convert_fusion = bf16[2,4,32,1024]{3,2,1,0:T(8,128)(2,1)} fusion(bf16[2,4,43,1024]{3,2,1,0:T(8,128)(2,1)S(1)} %maximum_bitcast_fusion, f32[1024]{0:T(1024)S(1)} %bitcast.34, f32[1024]{0:T(1024)S(1)} %bitcast.35, f32[1024]{0:T(1024)S(1)} %bitcast.25, f32[1024]{0:T(1024)S(1)} %bitcast.26, f32[1024]{0:T(1024)S(1)} %bitcast.27, f32[1024]{0:T(1024)S(1)} %bitcast.28, ...), kind=kLoop, calls=%fused_computation.6 | loop fusion | flops 9437184 | bytes 6864896 | tf_op jit(solution)/shard_map/convert_element_type | solution.py:95
  13.3 4.8 %shard_map.46 = bf16[512,4,128]{2,1,0:T(4,128)(2,1)} custom-call(bf16[256,1024]{1,0:T(8,128)(2,1)} %bitcast.21, f32[32,1024]{1,0:T(8,128)} %get-tuple-element.24.refs_0_.refs_4_, f32[32,1024]{1,0:T(8,128)} %get-tuple-element.25.refs_1_.refs_5_, f32[32,1024]{1,0:T(8,128)} %get-tuple-element.21.refs_2_.refs_6_, f32[32,1024]{1,0:T(8,128)} %get-tuple-element.20.refs_3_.refs_7_, ...), custom_call_target="tpu_custom_call" | custom-call | tf_op jit(solution)/shard_map/pallas_call | solution.py:72
  18.0 60.5 %all_to_all.5.r_ref = bf16[512,4,128]{2,1,0:T(4,128)(2,1)} all-to-all(bf16[512,4,128]{2,1,0:T(4,128)(2,1)} %shard_map.46), channel_id=1, replica_groups=mesh['chan'=128,'tm'=4] {'tm','chan'}, dimensions={0} | all-to-all | bytes 1048576 | tf_op jit(solution)/shard_map/all_to_all | solution.py:106
  78.6 5.2 %shard_map.47 = f32[2,2,512,512]{3,2,1,0:T(8,128)} custom-call(bf16[512,4,128]{2,1,0:T(4,128)(2,1)} %all_to_all.5.r_ref), custom_call_target="tpu_custom_call" | custom-call | tf_op jit(solution)/shard_map/pallas_call | solution.py:148
  (8 shorter events, 0.1 us)
Async XLA Ops:
  0.0 10.7 %copy-start = (f32[12,1024]{1,0:T(8,128)S(1)}, f32[12,1024]{1,0:T(8,128)}, u32[]{:S(2)}) copy-start(f32[12,1024]{1,0:T(8,128)} %param.5) | copy-start | bytes 147460
  1.3 9.4 %collective-permute-start = (bf16[4,11,2,1024]{3,1,0,2:T(8,128)(2,1)S(1)}, bf16[4,11,2,1024]{3,1,0,2:T(8,128)(2,1)S(1)}, u32[]{:S(2)}, u32[]{:S(2)}) collective-permute-start(bf16[4,11,2,1024]{3,1,0,2:T(8,128)(2,1)S(1)} %slice.100), channel_id=1, source_target_pairs={{0,1},{1,2},{2,3},{4,5},{5,6},{6,7},{8,9},{9,10},{10,11},{12,13},{... | collective-permute-start | bytes 540680 | tf_op jit(solution)/shard_map/ppermute | solution.py:15

commit v11 on v10

--- a/solution.py
+++ b/solution.py
@@ -120,7 +120,7 @@
     for reim in range(2):
         for tm in range(time_count):
             piece = r_ref[pl.ds(tm * chans, chans), cap * 2 + reim, :]
-            block = piece.astype(jnp.float32).T
+            block = piece.T
             row = (reim * time_count + tm) * spec_dev
             for i in range(inp_dev):
                 xt_ref[row : row + spec_dev, i * chans : (i + 1) * chans] = block[
@@ -131,7 +131,7 @@
     cols = lax.broadcasted_iota(jnp.int32, (inputs, inputs), 1)
     perm = (cols == (rows % inp_dev) * chans + rows // inp_dev).astype(jnp.bfloat16)
     nt = (((1,), (1,)), ((), ()))
-    xt = xt_ref[...].astype(jnp.bfloat16)
+    xt = xt_ref[...]
     x = lax.dot_general(perm, xt, nt, preferred_element_type=jnp.float32).astype(jnp.bfloat16)
     half = x.shape[1] // 2
     x2 = jnp.concatenate([x[:, half:], -x[:, :half]], axis=1)
@@ -151,7 +151,7 @@
         in_specs=[pl.BlockSpec(received.shape, lambda c: (0, 0, 0))],
         out_specs=pl.BlockSpec((1, 2, inputs, inputs), lambda c: (c, 0, 0, 0)),
         out_shape=jax.ShapeDtypeStruct((capacity, 2, inputs, inputs), jnp.float32),
-        scratch_shapes=[pltpu.VMEM((2 * time_count * spec_dev, inputs), jnp.float32)],
+        scratch_shapes=[pltpu.VMEM((2 * time_count * spec_dev, inputs), jnp.bfloat16)],
     )(received)
 
 

time: 84 us -> 84.2 us (level)
  no operation moved by 1% of the time
where the time goes in v11:
time: 84.2 us; the launch traced here: 83.9 us
  blocking collectives  60.6 us (72%)
  Pallas kernels  10.1 us (12%)
  other arithmetic  7.11 us (8%)
  starting transfers between devices  3.95 us (5%)
  local copies, waits for them, and re-layouts  2.08 us (2%)
    all_to_all x1, blocking collectives, local(): received = lax.all_to_all(sending, ('tm', 'chan'), 0, 0, tiled=True)  60.6 us
    pallas_call x1, Pallas kernels, correlate(): pl.pallas_call(kernel, grid=(capacity,), in_specs=[pl.BlockSpec(received....  5.35 us
    pallas_call x1, Pallas kernels, dft_payload(): pl.pallas_call(dft_kernel, grid=(steps,), in_specs=[pl.BlockSpec((2 * row...  4.76 us
    ppermute x1, starting transfers between devices, from_behind(): return lax.ppermute(value, axis, pairs)  3.95 us
    convert_element_type x1, other arithmetic, local(): running.astype(jnp.bfloat16).reshape(2 * inp_dev * spec_dev, channels)  2.38 us
    reduce_min x1, other arithmetic, slot_table(): lower = jnp.min(jnp.where(mine, channel_ids[:, None], channels), axis=0)  1.83 us
    mul x1, other arithmetic, slot_factors(): jnp.sin(angle_lo) * keep  1.78 us
  transfers between devices with their start and end apart: 1, of which 0 were waited for; matrix products, arithmetic and copies ran while one was open for 6% of the time, Pallas kernels for 0%

profile of v11, /device:TPU:1, one launch (start us, length us, event | category | flops | bytes accessed | tf_op | source)
XLA Modules:
  0.0 83.9 jit_solution(16404739311700536012)
XLA Ops:
  0.0 0.0 copy-start
  0.0 1.2 %copy.19 = bf16[4,32,2,1024]{3,1,0,2:T(8,128)(2,1)S(1)} copy(bf16[4,32,2,1024]{3,2,1,0:T(2,128)(2,1)} %param.4) | data formatting | bytes 1048576 | tf_op args[0]
  1.2 0.1 slice.100
  1.3 3.9 %collective-permute-start = (bf16[4,11,2,1024]{3,1,0,2:T(8,128)(2,1)S(1)}, bf16[4,11,2,1024]{3,1,0,2:T(8,128)(2,1)S(1)}, u32[]{:S(2)}, u32[]{:S(2)}) collective-permute-start(bf16[4,11,2,1024]{3,1,0,2:T(8,128)(2,1)S(1)} %slice.100), channel_id=1, source_target_pairs={{0,1},{1,2},{2,3},{4,5},{5,6},{6,7},{8,9},{9,10},{10,11},{12,13},{... | collective-permute-start | bytes 540680 | tf_op jit(solution)/shard_map/ppermute | solution.py:15
  5.2 0.9 %fusion.1 = pred[1024]{0:T(1024)(128)(4,1)S(1)} fusion(s32[256]{0:T(256)} %param.6), kind=kLoop, calls=%fused_computation.7 | loop fusion | flops 523264 | bytes 2048 | tf_op jit(solution)/shard_map/reduce_or | solution.py:20
  6.1 1.8 %select_reduce_fusion.1 = (s32[512]{0:T(512)S(1)}, s32[512]{0:T(512)S(1)}, s32[512]{0:T(512)S(1)}) fusion(s32[1024]{0:T(1024)} %param.7, pred[1024]{0:T(1024)(128)(4,1)S(1)} %not.7), kind=kLoop, calls=%fused_computation.1 | loop fusion | flops 4192768 | bytes 11264 | tf_op jit(solution)/shard_map/reduce_min | solution.py:24
  8.0 0.1 gt.41
  8.1 0.1 copy.23
  8.2 0.1 gt.43
  8.3 0.1 copy.24
  8.4 0.1 reduce_min.12
  8.6 0.1 copy.21
  8.6 0.1 reduce_max.12
  8.8 0.1 copy.22
  8.9 1.8 %sine_multiply_fusion = (f32[32,1024]{1,0:T(8,128)}, f32[32,1024]{1,0:T(8,128)}, f32[32,1024]{1,0:T(8,128)}, f32[32,1024]{1,0:T(8,128)}) fusion(f32[1024]{0:T(1024)S(1)} %bitcast.22, s32[1024]{0:T(1024)S(1)} %bitcast.23, s32[32]{0:T(128)S(1)} %iota_multiply_fusion), kind=kLoop, calls=%fused_computation.23 | loop fusion | flops 983040 | bytes 532608 | tf_op jit(solution)/shard_map/mul | solution.py:40
  10.7 0.0 copy-done
  10.7 0.0 collective-permute-done
  10.7 0.2 maximum_bitcast_fusion
  10.9 2.4 %add_convert_fusion = bf16[2,4,32,1024]{3,2,1,0:T(8,128)(2,1)} fusion(bf16[2,4,43,1024]{3,2,1,0:T(8,128)(2,1)S(1)} %maximum_bitcast_fusion, f32[1024]{0:T(1024)S(1)} %bitcast.34, f32[1024]{0:T(1024)S(1)} %bitcast.35, f32[1024]{0:T(1024)S(1)} %bitcast.25, f32[1024]{0:T(1024)S(1)} %bitcast.26, f32[1024]{0:T(1024)S(1)} %bitcast.27, f32[1024]{0:T(1024)S(1)} %bitcast.28, ...), kind=kLoop, calls=%fused_computation.6 | loop fusion | flops 9437184 | bytes 6864896 | tf_op jit(solution)/shard_map/convert_element_type | solution.py:95
  13.3 4.8 %shard_map.46 = bf16[512,4,128]{2,1,0:T(4,128)(2,1)} custom-call(bf16[256,1024]{1,0:T(8,128)(2,1)} %bitcast.21, f32[32,1024]{1,0:T(8,128)} %get-tuple-element.24.refs_0_.refs_4_, f32[32,1024]{1,0:T(8,128)} %get-tuple-element.25.refs_1_.refs_5_, f32[32,1024]{1,0:T(8,128)} %get-tuple-element.21.refs_2_.refs_6_, f32[32,1024]{1,0:T(8,128)} %get-tuple-element.20.refs_3_.refs_7_, ...), custom_call_target="tpu_custom_call" | custom-call | tf_op jit(solution)/shard_map/pallas_call | solution.py:72
  18.0 60.6 %all_to_all.5.r_ref = bf16[512,4,128]{2,1,0:T(4,128)(2,1)} all-to-all(bf16[512,4,128]{2,1,0:T(4,128)(2,1)} %shard_map.46), channel_id=1, replica_groups=mesh['chan'=128,'tm'=4] {'tm','chan'}, dimensions={0} | all-to-all | bytes 1048576 | tf_op jit(solution)/shard_map/all_to_all | solution.py:106
  78.6 5.3 %shard_map.47 = f32[2,2,512,512]{3,2,1,0:T(8,128)} custom-call(bf16[512,4,128]{2,1,0:T(4,128)(2,1)} %all_to_all.5.r_ref), custom_call_target="tpu_custom_call" | custom-call | tf_op jit(solution)/shard_map/pallas_call | solution.py:148
  (8 shorter events, 0.1 us)
Async XLA Ops:
  0.0 10.7 %copy-start = (f32[12,1024]{1,0:T(8,128)S(1)}, f32[12,1024]{1,0:T(8,128)}, u32[]{:S(2)}) copy-start(f32[12,1024]{1,0:T(8,128)} %param.5) | copy-start | bytes 147460
  1.3 9.4 %collective-permute-start = (bf16[4,11,2,1024]{3,1,0,2:T(8,128)(2,1)S(1)}, bf16[4,11,2,1024]{3,1,0,2:T(8,128)(2,1)S(1)}, u32[]{:S(2)}, u32[]{:S(2)}) collective-permute-start(bf16[4,11,2,1024]{3,1,0,2:T(8,128)(2,1)S(1)} %slice.100), channel_id=1, source_target_pairs={{0,1},{1,2},{2,3},{4,5},{5,6},{6,7},{8,9},{9,10},{10,11},{12,13},{... | collective-permute-start | bytes 540680 | tf_op jit(solution)/shard_map/ppermute | solution.py:15

commit v12 on v10

--- a/solution.py
+++ b/solution.py
@@ -61,7 +61,7 @@
 def dft_payload(filtered, factors, devices, capacity):
     channels = filtered.shape[1]
     rows = filtered.shape[0] // 2
-    block = 512
+    block = 256
     steps = devices // block
     specs = []
     operands = []

time: 84 us -> 84.4 us (level)
  no operation moved by 1% of the time
where the time goes in v12:
time: 84.4 us; the launch traced here: 84.1 us
  blocking collectives  60.5 us (72%)
  Pallas kernels  10.2 us (12%)
  other arithmetic  7.11 us (8%)
  starting transfers between devices  3.95 us (5%)
  local copies, waits for them, and re-layouts  2.08 us (2%)
    all_to_all x1, blocking collectives, local(): received = lax.all_to_all(sending, ('tm', 'chan'), 0, 0, tiled=True)  60.5 us
    pallas_call x1, Pallas kernels, correlate(): pl.pallas_call(kernel, grid=(capacity,), in_specs=[pl.BlockSpec(received....  5.15 us
    pallas_call x1, Pallas kernels, dft_payload(): pl.pallas_call(dft_kernel, grid=(steps,), in_specs=[pl.BlockSpec((2 * row...  5.09 us
    ppermute x1, starting transfers between devices, from_behind(): return lax.ppermute(value, axis, pairs)  3.95 us
    convert_element_type x1, other arithmetic, local(): running.astype(jnp.bfloat16).reshape(2 * inp_dev * spec_dev, channels)  2.38 us
    reduce_min x1, other arithmetic, slot_table(): lower = jnp.min(jnp.where(mine, channel_ids[:, None], channels), axis=0)  1.83 us
    mul x1, other arithmetic, slot_factors(): jnp.sin(angle_lo) * keep  1.78 us
  transfers between devices with their start and end apart: 1, of which 0 were waited for; matrix products, arithmetic and copies ran while one was open for 6% of the time, Pallas kernels for 0%

profile of v12, /device:TPU:1, one launch (start us, length us, event | category | flops | bytes accessed | tf_op | source)
XLA Modules:
  0.0 84.1 jit_solution(10824816116089523507)
XLA Ops:
  0.0 0.0 copy-start
  0.0 1.2 %copy.19 = bf16[4,32,2,1024]{3,1,0,2:T(8,128)(2,1)S(1)} copy(bf16[4,32,2,1024]{3,2,1,0:T(2,128)(2,1)} %param.4) | data formatting | bytes 1048576 | tf_op args[0]
  1.2 0.1 slice.100
  1.3 3.9 %collective-permute-start = (bf16[4,11,2,1024]{3,1,0,2:T(8,128)(2,1)S(1)}, bf16[4,11,2,1024]{3,1,0,2:T(8,128)(2,1)S(1)}, u32[]{:S(2)}, u32[]{:S(2)}) collective-permute-start(bf16[4,11,2,1024]{3,1,0,2:T(8,128)(2,1)S(1)} %slice.100), channel_id=1, source_target_pairs={{0,1},{1,2},{2,3},{4,5},{5,6},{6,7},{8,9},{9,10},{10,11},{12,13},{... | collective-permute-start | bytes 540680 | tf_op jit(solution)/shard_map/ppermute | solution.py:15
  5.2 0.9 %fusion.1 = pred[1024]{0:T(1024)(128)(4,1)S(1)} fusion(s32[256]{0:T(256)} %param.6), kind=kLoop, calls=%fused_computation.7 | loop fusion | flops 523264 | bytes 2048 | tf_op jit(solution)/shard_map/reduce_or | solution.py:20
  6.1 1.8 %select_reduce_fusion.1 = (s32[512]{0:T(512)S(1)}, s32[512]{0:T(512)S(1)}, s32[512]{0:T(512)S(1)}) fusion(s32[1024]{0:T(1024)} %param.7, pred[1024]{0:T(1024)(128)(4,1)S(1)} %not.7), kind=kLoop, calls=%fused_computation.1 | loop fusion | flops 4192768 | bytes 11264 | tf_op jit(solution)/shard_map/reduce_min | solution.py:24
  8.0 0.1 gt.41
  8.1 0.1 copy.23
  8.2 0.1 gt.43
  8.3 0.1 copy.24
  8.4 0.1 reduce_min.12
  8.6 0.1 copy.21
  8.6 0.1 reduce_max.12
  8.8 0.1 copy.22
  8.9 1.8 %sine_multiply_fusion = (f32[32,1024]{1,0:T(8,128)}, f32[32,1024]{1,0:T(8,128)}, f32[32,1024]{1,0:T(8,128)}, f32[32,1024]{1,0:T(8,128)}) fusion(f32[1024]{0:T(1024)S(1)} %bitcast.22, s32[1024]{0:T(1024)S(1)} %bitcast.23, s32[32]{0:T(128)S(1)} %iota_multiply_fusion), kind=kLoop, calls=%fused_computation.23 | loop fusion | flops 983040 | bytes 532608 | tf_op jit(solution)/shard_map/mul | solution.py:40
  10.7 0.0 copy-done
  10.7 0.0 collective-permute-done
  10.7 0.2 maximum_bitcast_fusion
  10.9 2.4 %add_convert_fusion = bf16[2,4,32,1024]{3,2,1,0:T(8,128)(2,1)} fusion(bf16[2,4,43,1024]{3,2,1,0:T(8,128)(2,1)S(1)} %maximum_bitcast_fusion, f32[1024]{0:T(1024)S(1)} %bitcast.34, f32[1024]{0:T(1024)S(1)} %bitcast.35, f32[1024]{0:T(1024)S(1)} %bitcast.25, f32[1024]{0:T(1024)S(1)} %bitcast.26, f32[1024]{0:T(1024)S(1)} %bitcast.27, f32[1024]{0:T(1024)S(1)} %bitcast.28, ...), kind=kLoop, calls=%fused_computation.6 | loop fusion | flops 9437184 | bytes 6864896 | tf_op jit(solution)/shard_map/convert_element_type | solution.py:95
  13.3 5.1 %shard_map.46 = bf16[512,4,128]{2,1,0:T(4,128)(2,1)} custom-call(bf16[256,1024]{1,0:T(8,128)(2,1)} %bitcast.21, f32[32,1024]{1,0:T(8,128)} %get-tuple-element.24.refs_0_.refs_4_, f32[32,1024]{1,0:T(8,128)} %get-tuple-element.25.refs_1_.refs_5_, f32[32,1024]{1,0:T(8,128)} %get-tuple-element.21.refs_2_.refs_6_, f32[32,1024]{1,0:T(8,128)} %get-tuple-element.20.refs_3_.refs_7_, ...), custom_call_target="tpu_custom_call" | custom-call | tf_op jit(solution)/shard_map/pallas_call | solution.py:72
  18.4 60.5 %all_to_all.5.r_ref = bf16[512,4,128]{2,1,0:T(4,128)(2,1)} all-to-all(bf16[512,4,128]{2,1,0:T(4,128)(2,1)} %shard_map.46), channel_id=1, replica_groups=mesh['chan'=128,'tm'=4] {'tm','chan'}, dimensions={0} | all-to-all | bytes 1048576 | tf_op jit(solution)/shard_map/all_to_all | solution.py:106
  78.9 5.2 %shard_map.47 = f32[2,2,512,512]{3,2,1,0:T(8,128)} custom-call(bf16[512,4,128]{2,1,0:T(4,128)(2,1)} %all_to_all.5.r_ref), custom_call_target="tpu_custom_call" | custom-call | tf_op jit(solution)/shard_map/pallas_call | solution.py:148
  (8 shorter events, 0.1 us)
Async XLA Ops:
  0.0 10.7 %copy-start = (f32[12,1024]{1,0:T(8,128)S(1)}, f32[12,1024]{1,0:T(8,128)}, u32[]{:S(2)}) copy-start(f32[12,1024]{1,0:T(8,128)} %param.5) | copy-start | bytes 147460
  1.3 9.4 %collective-permute-start = (bf16[4,11,2,1024]{3,1,0,2:T(8,128)(2,1)S(1)}, bf16[4,11,2,1024]{3,1,0,2:T(8,128)(2,1)S(1)}, u32[]{:S(2)}, u32[]{:S(2)}) collective-permute-start(bf16[4,11,2,1024]{3,1,0,2:T(8,128)(2,1)S(1)} %slice.100), channel_id=1, source_target_pairs={{0,1},{1,2},{2,3},{4,5},{5,6},{6,7},{8,9},{9,10},{10,11},{12,13},{... | collective-permute-start | bytes 540680 | tf_op jit(solution)/shard_map/ppermute | solution.py:15

commit v13 on v10

--- a/solution.py
+++ b/solution.py
@@ -32,12 +32,18 @@
     low = 32
     high = channels // low
     step = 2.0 * math.pi / channels
-    hi = jnp.arange(high, dtype=jnp.int32)
+    top = jnp.arange(high // 4, dtype=jnp.int32)
+    rest = jnp.arange(4, dtype=jnp.int32)
     lo = jnp.arange(low, dtype=jnp.int32)
-    angle_hi = ((hi[:, None] * low * chosen[None, :]) % channels).astype(jnp.float32) * step
+    angle_top = ((top[:, None] * (4 * low) * chosen[None, :]) % channels).astype(jnp.float32) * step
+    angle_rest = ((rest[:, None] * low * chosen[None, :]) % channels).astype(jnp.float32) * step
     angle_lo = ((lo[:, None] * chosen[None, :]) % channels).astype(jnp.float32) * step
+    ct, st = jnp.cos(angle_top)[:, None, :], jnp.sin(angle_top)[:, None, :]
+    cr, sr = jnp.cos(angle_rest)[None, :, :], jnp.sin(angle_rest)[None, :, :]
+    cos_hi = (ct * cr - st * sr).reshape(high, -1)
+    sin_hi = (st * cr + ct * sr).reshape(high, -1)
     keep = jnp.where(present, 1.0 / math.sqrt(channels), 0.0).astype(jnp.float32)[None, :]
-    return (jnp.cos(angle_hi), jnp.sin(angle_hi), jnp.cos(angle_lo) * keep, jnp.sin(angle_lo) * keep)
+    return (cos_hi, sin_hi, jnp.cos(angle_lo) * keep, jnp.sin(angle_lo) * keep)
 
 
 def dft_kernel(x_ref, *refs):

time: 84 us -> 84.1 us (level)
  local copies, waits for them, and re-layouts: 2.08 us -> 3.46 us
  blocking collectives: 60.5 us -> 59.2 us
    all_to_all x1, blocking collectives: 60.5 us -> 59.2 us  [local(): received = lax.all_to_all(sending, ('tm', 'chan'), 0, 0, tiled=True)]
    mul x2 -> x3, other arithmetic: 1.78 us -> 1.26 us  [the longest x1 1.25 us: slot_factors(): return (cos_hi, sin_hi, jnp.cos(angle_lo) * keep, jnp.sin(angle_lo) * keep)]
  transfers between devices with their start and end apart: 1 -> 1, of which waited for: 0 -> 0; matrix products, arithmetic and copies ran while one was open for 6% -> 8% of each run, Pallas kernels for 0% -> 0%
where the time goes in v13:
time: 84.1 us; the launch traced here: 83.8 us
  blocking collectives  59.2 us (70%)
  Pallas kernels  9.91 us (12%)
  other arithmetic  7.1 us (8%)
  starting transfers between devices  3.95 us (5%)
  local copies, waits for them, and re-layouts  3.46 us (4%)
    all_to_all x1, blocking collectives, local(): received = lax.all_to_all(sending, ('tm', 'chan'), 0, 0, tiled=True)  59.2 us
    pallas_call x1, Pallas kernels, correlate(): pl.pallas_call(kernel, grid=(capacity,), in_specs=[pl.BlockSpec(received....  5.15 us
    pallas_call x1, Pallas kernels, dft_payload(): pl.pallas_call(dft_kernel, grid=(steps,), in_specs=[pl.BlockSpec((2 * row...  4.75 us
    ppermute x1, starting transfers between devices, from_behind(): return lax.ppermute(value, axis, pairs)  3.95 us
    convert_element_type x1, other arithmetic, local(): running.astype(jnp.bfloat16).reshape(2 * inp_dev * spec_dev, channels)  2.37 us
    reduce_min x1, other arithmetic, slot_table(): lower = jnp.min(jnp.where(mine, channel_ids[:, None], channels), axis=0)  1.83 us
  transfers between devices with their start and end apart: 1, of which 0 were waited for; matrix products, arithmetic and copies ran while one was open for 8% of the time, Pallas kernels for 0%

profile of v13, /device:TPU:1, one launch (start us, length us, event | category | flops | bytes accessed | tf_op | source)
XLA Modules:
  0.0 83.8 jit_solution(10972025531690906672)
XLA Ops:
  0.0 0.0 copy-start
  0.0 1.2 %copy.19 = bf16[4,32,2,1024]{3,1,0,2:T(8,128)(2,1)S(1)} copy(bf16[4,32,2,1024]{3,2,1,0:T(2,128)(2,1)} %param.4) | data formatting | bytes 1048576 | tf_op args[0]
  1.2 0.1 slice.100
  1.3 3.9 %collective-permute-start = (bf16[4,11,2,1024]{3,1,0,2:T(8,128)(2,1)S(1)}, bf16[4,11,2,1024]{3,1,0,2:T(8,128)(2,1)S(1)}, u32[]{:S(2)}, u32[]{:S(2)}) collective-permute-start(bf16[4,11,2,1024]{3,1,0,2:T(8,128)(2,1)S(1)} %slice.100), channel_id=1, source_target_pairs={{0,1},{1,2},{2,3},{4,5},{5,6},{6,7},{8,9},{9,10},{10,11},{12,13},{... | collective-permute-start | bytes 540680 | tf_op jit(solution)/shard_map/ppermute | solution.py:15
  5.2 0.9 %fusion.1 = pred[1024]{0:T(1024)(128)(4,1)S(1)} fusion(s32[256]{0:T(256)} %param.6), kind=kLoop, calls=%fused_computation.7 | loop fusion | flops 523264 | bytes 2048 | tf_op jit(solution)/shard_map/reduce_or | solution.py:20
  6.2 1.8 %select_reduce_fusion.1 = (s32[512]{0:T(512)S(1)}, s32[512]{0:T(512)S(1)}, s32[512]{0:T(512)S(1)}) fusion(s32[1024]{0:T(1024)} %param.7, pred[1024]{0:T(1024)(128)(4,1)S(1)} %not.7), kind=kLoop, calls=%fused_computation.1 | loop fusion | flops 4192768 | bytes 11264 | tf_op jit(solution)/shard_map/reduce_min | solution.py:24
  8.0 0.1 gt.41
  8.1 0.1 copy.23
  8.2 0.1 gt.43
  8.4 0.1 copy.24
  8.4 0.1 reduce_min.12
  8.6 0.1 copy.21
  8.6 0.1 reduce_max.12
  8.8 0.1 copy.22
  8.9 0.2 fusion.17
  9.1 0.2 fusion.15
  9.3 0.1 multiply_add_fusion
  9.4 0.7 add.86.refs_1_.refs_5_
  10.1 0.7 sub.8.refs_0_.refs_4_
  10.8 1.3 %sine_multiply_fusion = (f32[32,1024]{1,0:T(8,128)}, f32[32,1024]{1,0:T(8,128)}) fusion(f32[1024]{0:T(1024)S(1)} %bitcast.25, s32[1024]{0:T(1024)S(1)} %bitcast.24), kind=kLoop, calls=%fused_computation.15 | loop fusion | flops 524288 | bytes 270336 | tf_op jit(solution)/shard_map/mul | solution.py:46
  12.0 0.0 copy-done
  12.1 0.0 collective-permute-done
  12.1 0.2 maximum_bitcast_fusion
  12.3 2.4 %add_convert_fusion = bf16[2,4,32,1024]{3,2,1,0:T(8,128)(2,1)} fusion(bf16[2,4,43,1024]{3,2,1,0:T(8,128)(2,1)S(1)} %maximum_bitcast_fusion, f32[1024]{0:T(1024)S(1)} %bitcast.36, f32[1024]{0:T(1024)S(1)} %bitcast.37, f32[1024]{0:T(1024)S(1)} %bitcast.27, f32[1024]{0:T(1024)S(1)} %bitcast.28, f32[1024]{0:T(1024)S(1)} %bitcast.29, f32[1024]{0:T(1024)S(1)} %bitcast.30, ...), kind=kLoop, calls=%fused_computation.6 | loop fusion | flops 9437184 | bytes 6864896 | tf_op jit(solution)/shard_map/convert_element_type | solution.py:101
  14.7 4.8 %shard_map.46 = bf16[512,4,128]{2,1,0:T(4,128)(2,1)} custom-call(bf16[256,1024]{1,0:T(8,128)(2,1)} %bitcast.21, f32[32,1024]{1,0:T(8,128)} %sub.8.refs_0_.refs_4_, f32[32,1024]{1,0:T(8,128)} %add.86.refs_1_.refs_5_, f32[32,1024]{1,0:T(8,128)} %get-tuple-element.23.refs_2_.refs_6_, f32[32,1024]{1,0:T(8,128)} %get-tuple-element.22.refs_3_.refs_7_, ...), custom_call_target="tpu_custom_call" | custom-call | tf_op jit(solution)/shard_map/pallas_call | solution.py:78
  19.4 59.2 %all_to_all.5.r_ref = bf16[512,4,128]{2,1,0:T(4,128)(2,1)} all-to-all(bf16[512,4,128]{2,1,0:T(4,128)(2,1)} %shard_map.46), channel_id=1, replica_groups=mesh['chan'=128,'tm'=4] {'tm','chan'}, dimensions={0} | all-to-all | bytes 1048576 | tf_op jit(solution)/shard_map/all_to_all | solution.py:112
  78.6 5.2 %shard_map.47 = f32[2,2,512,512]{3,2,1,0:T(8,128)} custom-call(bf16[512,4,128]{2,1,0:T(4,128)(2,1)} %all_to_all.5.r_ref), custom_call_target="tpu_custom_call" | custom-call | tf_op jit(solution)/shard_map/pallas_call | solution.py:154
  (9 shorter events, 0.1 us)
Async XLA Ops:
  0.0 12.0 %copy-start = (f32[12,1024]{1,0:T(8,128)S(1)}, f32[12,1024]{1,0:T(8,128)}, u32[]{:S(2)}) copy-start(f32[12,1024]{1,0:T(8,128)} %param.5) | copy-start | bytes 147460
  1.3 10.8 %collective-permute-start = (bf16[4,11,2,1024]{3,1,0,2:T(8,128)(2,1)S(1)}, bf16[4,11,2,1024]{3,1,0,2:T(8,128)(2,1)S(1)}, u32[]{:S(2)}, u32[]{:S(2)}) collective-permute-start(bf16[4,11,2,1024]{3,1,0,2:T(8,128)(2,1)S(1)} %slice.100), channel_id=1, source_target_pairs={{0,1},{1,2},{2,3},{4,5},{5,6},{6,7},{8,9},{9,10},{10,11},{12,13},{... | collective-permute-start | bytes 540680 | tf_op jit(solution)/shard_map/ppermute | solution.py:15

commit v14 on v10

--- a/solution.py
+++ b/solution.py
@@ -109,9 +109,7 @@
 
 def correlate_kernel(r_ref, o_ref, xt_ref, *, time_count, inp_dev, caps):
     for cap in range(caps):
-        pl.when(pl.program_id(0) == cap)(
-            functools.partial(correlate_slot, r_ref, o_ref, xt_ref, cap, time_count, inp_dev)
-        )
+        correlate_slot(r_ref, o_ref.at[cap : cap + 1], xt_ref, cap, time_count, inp_dev)
 
 
 def correlate_slot(r_ref, o_ref, xt_ref, cap, time_count, inp_dev):
@@ -147,9 +145,9 @@
     kernel = functools.partial(correlate_kernel, time_count=time_count, inp_dev=inp_dev, caps=capacity)
     return pl.pallas_call(
         kernel,
-        grid=(capacity,),
+        grid=(1,),
         in_specs=[pl.BlockSpec(received.shape, lambda c: (0, 0, 0))],
-        out_specs=pl.BlockSpec((1, 2, inputs, inputs), lambda c: (c, 0, 0, 0)),
+        out_specs=pl.BlockSpec((capacity, 2, inputs, inputs), lambda c: (0, 0, 0, 0)),
         out_shape=jax.ShapeDtypeStruct((capacity, 2, inputs, inputs), jnp.float32),
         scratch_shapes=[pltpu.VMEM((2 * time_count * spec_dev, inputs), jnp.float32)],
     )(received)

time: 84 us -> 84.2 us (level)
  no operation moved by 1% of the time
where the time goes in v14:
time: 84.2 us; the launch traced here: 84 us
  blocking collectives  60.5 us (72%)
  Pallas kernels  10.1 us (12%)
  other arithmetic  7.11 us (8%)
  starting transfers between devices  3.95 us (5%)
  local copies, waits for them, and re-layouts  2.08 us (2%)
    all_to_all x1, blocking collectives, local(): received = lax.all_to_all(sending, ('tm', 'chan'), 0, 0, tiled=True)  60.5 us
    pallas_call x1, Pallas kernels, correlate(): pl.pallas_call(kernel, grid=(1,), in_specs=[pl.BlockSpec(received.shape,...  5.38 us
    pallas_call x1, Pallas kernels, dft_payload(): pl.pallas_call(dft_kernel, grid=(steps,), in_specs=[pl.BlockSpec((2 * row...  4.76 us
    ppermute x1, starting transfers between devices, from_behind(): return lax.ppermute(value, axis, pairs)  3.95 us
    convert_element_type x1, other arithmetic, local(): running.astype(jnp.bfloat16).reshape(2 * inp_dev * spec_dev, channels)  2.38 us
    reduce_min x1, other arithmetic, slot_table(): lower = jnp.min(jnp.where(mine, channel_ids[:, None], channels), axis=0)  1.83 us
    mul x1, other arithmetic, slot_factors(): jnp.sin(angle_lo) * keep  1.78 us
  transfers between devices with their start and end apart: 1, of which 0 were waited for; matrix products, arithmetic and copies ran while one was open for 6% of the time, Pallas kernels for 0%

profile of v14, /device:TPU:1, one launch (start us, length us, event | category | flops | bytes accessed | tf_op | source)
XLA Modules:
  0.0 84.0 jit_solution(17212971698095363397)
XLA Ops:
  0.0 0.0 copy-start
  0.0 1.2 %copy.19 = bf16[4,32,2,1024]{3,1,0,2:T(8,128)(2,1)S(1)} copy(bf16[4,32,2,1024]{3,2,1,0:T(2,128)(2,1)} %param.4) | data formatting | bytes 1048576 | tf_op args[0]
  1.2 0.1 slice.100
  1.3 3.9 %collective-permute-start = (bf16[4,11,2,1024]{3,1,0,2:T(8,128)(2,1)S(1)}, bf16[4,11,2,1024]{3,1,0,2:T(8,128)(2,1)S(1)}, u32[]{:S(2)}, u32[]{:S(2)}) collective-permute-start(bf16[4,11,2,1024]{3,1,0,2:T(8,128)(2,1)S(1)} %slice.100), channel_id=1, source_target_pairs={{0,1},{1,2},{2,3},{4,5},{5,6},{6,7},{8,9},{9,10},{10,11},{12,13},{... | collective-permute-start | bytes 540680 | tf_op jit(solution)/shard_map/ppermute | solution.py:15
  5.2 0.9 %fusion.1 = pred[1024]{0:T(1024)(128)(4,1)S(1)} fusion(s32[256]{0:T(256)} %param.6), kind=kLoop, calls=%fused_computation.7 | loop fusion | flops 523264 | bytes 2048 | tf_op jit(solution)/shard_map/reduce_or | solution.py:20
  6.1 1.8 %select_reduce_fusion.1 = (s32[512]{0:T(512)S(1)}, s32[512]{0:T(512)S(1)}, s32[512]{0:T(512)S(1)}) fusion(s32[1024]{0:T(1024)} %param.7, pred[1024]{0:T(1024)(128)(4,1)S(1)} %not.7), kind=kLoop, calls=%fused_computation.1 | loop fusion | flops 4192768 | bytes 11264 | tf_op jit(solution)/shard_map/reduce_min | solution.py:24
  8.0 0.1 gt.41
  8.1 0.1 copy.23
  8.2 0.1 gt.43
  8.3 0.1 copy.24
  8.4 0.1 reduce_min.12
  8.6 0.1 copy.21
  8.6 0.1 reduce_max.12
  8.8 0.1 copy.22
  8.9 1.8 %sine_multiply_fusion = (f32[32,1024]{1,0:T(8,128)}, f32[32,1024]{1,0:T(8,128)}, f32[32,1024]{1,0:T(8,128)}, f32[32,1024]{1,0:T(8,128)}) fusion(f32[1024]{0:T(1024)S(1)} %bitcast.22, s32[1024]{0:T(1024)S(1)} %bitcast.23, s32[32]{0:T(128)S(1)} %iota_multiply_fusion), kind=kLoop, calls=%fused_computation.23 | loop fusion | flops 983040 | bytes 532608 | tf_op jit(solution)/shard_map/mul | solution.py:40
  10.7 0.0 copy-done
  10.7 0.0 collective-permute-done
  10.7 0.2 maximum_bitcast_fusion
  10.9 2.4 %add_convert_fusion = bf16[2,4,32,1024]{3,2,1,0:T(8,128)(2,1)} fusion(bf16[2,4,43,1024]{3,2,1,0:T(8,128)(2,1)S(1)} %maximum_bitcast_fusion, f32[1024]{0:T(1024)S(1)} %bitcast.34, f32[1024]{0:T(1024)S(1)} %bitcast.35, f32[1024]{0:T(1024)S(1)} %bitcast.25, f32[1024]{0:T(1024)S(1)} %bitcast.26, f32[1024]{0:T(1024)S(1)} %bitcast.27, f32[1024]{0:T(1024)S(1)} %bitcast.28, ...), kind=kLoop, calls=%fused_computation.6 | loop fusion | flops 9437184 | bytes 6864896 | tf_op jit(solution)/shard_map/convert_element_type | solution.py:95
  13.3 4.8 %shard_map.46 = bf16[512,4,128]{2,1,0:T(4,128)(2,1)} custom-call(bf16[256,1024]{1,0:T(8,128)(2,1)} %bitcast.21, f32[32,1024]{1,0:T(8,128)} %get-tuple-element.24.refs_0_.refs_4_, f32[32,1024]{1,0:T(8,128)} %get-tuple-element.25.refs_1_.refs_5_, f32[32,1024]{1,0:T(8,128)} %get-tuple-element.21.refs_2_.refs_6_, f32[32,1024]{1,0:T(8,128)} %get-tuple-element.20.refs_3_.refs_7_, ...), custom_call_target="tpu_custom_call" | custom-call | tf_op jit(solution)/shard_map/pallas_call | solution.py:72
  18.0 60.5 %all_to_all.5.r_ref = bf16[512,4,128]{2,1,0:T(4,128)(2,1)} all-to-all(bf16[512,4,128]{2,1,0:T(4,128)(2,1)} %shard_map.46), channel_id=1, replica_groups=mesh['chan'=128,'tm'=4] {'tm','chan'}, dimensions={0} | all-to-all | bytes 1048576 | tf_op jit(solution)/shard_map/all_to_all | solution.py:106
  78.6 5.4 %shard_map.47 = f32[2,2,512,512]{3,2,1,0:T(8,128)} custom-call(bf16[512,4,128]{2,1,0:T(4,128)(2,1)} %all_to_all.5.r_ref), custom_call_target="tpu_custom_call" | custom-call | tf_op jit(solution)/shard_map/pallas_call | solution.py:146
  (8 shorter events, 0.1 us)
Async XLA Ops:
  0.0 10.7 %copy-start = (f32[12,1024]{1,0:T(8,128)S(1)}, f32[12,1024]{1,0:T(8,128)}, u32[]{:S(2)}) copy-start(f32[12,1024]{1,0:T(8,128)} %param.5) | copy-start | bytes 147460
  1.3 9.4 %collective-permute-start = (bf16[4,11,2,1024]{3,1,0,2:T(8,128)(2,1)S(1)}, bf16[4,11,2,1024]{3,1,0,2:T(8,128)(2,1)S(1)}, u32[]{:S(2)}, u32[]{:S(2)}) collective-permute-start(bf16[4,11,2,1024]{3,1,0,2:T(8,128)(2,1)S(1)} %slice.100), channel_id=1, source_target_pairs={{0,1},{1,2},{2,3},{4,5},{5,6},{6,7},{8,9},{9,10},{10,11},{12,13},{... | collective-permute-start | bytes 540680 | tf_op jit(solution)/shard_map/ppermute | solution.py:15

commit v15 on v10

--- a/solution.py
+++ b/solution.py
@@ -135,9 +135,9 @@
     x = lax.dot_general(perm, xt, nt, preferred_element_type=jnp.float32).astype(jnp.bfloat16)
     half = x.shape[1] // 2
     x2 = jnp.concatenate([x[:, half:], -x[:, :half]], axis=1)
-    scale = 1.0 / (time_count * spec_dev)
-    o_ref[0, 0] = lax.dot_general(x, x, nt, preferred_element_type=jnp.float32) * scale
-    o_ref[0, 1] = lax.dot_general(x2, x, nt, preferred_element_type=jnp.float32) * scale
+    scale = jnp.asarray(1.0 / (time_count * spec_dev), jnp.bfloat16)
+    o_ref[0, 0] = lax.dot_general(x * scale, x, nt, preferred_element_type=jnp.float32)
+    o_ref[0, 1] = lax.dot_general(x2 * scale, x, nt, preferred_element_type=jnp.float32)
 
 
 def correlate(received, time_count, chan_count, capacity, inp_dev):

time: 84 us -> 84 us (level)
  no operation moved by 1% of the time
where the time goes in v15:
time: 84 us; the launch traced here: 83.7 us
  blocking collectives  60.5 us (72%)
  Pallas kernels  9.9 us (12%)
  other arithmetic  7.11 us (8%)
  starting transfers between devices  3.95 us (5%)
  local copies, waits for them, and re-layouts  2.08 us (2%)
    all_to_all x1, blocking collectives, local(): received = lax.all_to_all(sending, ('tm', 'chan'), 0, 0, tiled=True)  60.5 us
    pallas_call x1, Pallas kernels, correlate(): pl.pallas_call(kernel, grid=(capacity,), in_specs=[pl.BlockSpec(received....  5.14 us
    pallas_call x1, Pallas kernels, dft_payload(): pl.pallas_call(dft_kernel, grid=(steps,), in_specs=[pl.BlockSpec((2 * row...  4.76 us
    ppermute x1, starting transfers between devices, from_behind(): return lax.ppermute(value, axis, pairs)  3.95 us
    convert_element_type x1, other arithmetic, local(): running.astype(jnp.bfloat16).reshape(2 * inp_dev * spec_dev, channels)  2.38 us
    reduce_min x1, other arithmetic, slot_table(): lower = jnp.min(jnp.where(mine, channel_ids[:, None], channels), axis=0)  1.83 us
    mul x1, other arithmetic, slot_factors(): jnp.sin(angle_lo) * keep  1.78 us
  transfers between devices with their start and end apart: 1, of which 0 were waited for; matrix products, arithmetic and copies ran while one was open for 6% of the time, Pallas kernels for 0%

profile of v15, /device:TPU:1, one launch (start us, length us, event | category | flops | bytes accessed | tf_op | source)
XLA Modules:
  0.0 83.7 jit_solution(11650831032200950159)
XLA Ops:
  0.0 0.0 copy-start
  0.0 1.2 %copy.19 = bf16[4,32,2,1024]{3,1,0,2:T(8,128)(2,1)S(1)} copy(bf16[4,32,2,1024]{3,2,1,0:T(2,128)(2,1)} %param.4) | data formatting | bytes 1048576 | tf_op args[0]
  1.2 0.1 slice.100
  1.3 3.9 %collective-permute-start = (bf16[4,11,2,1024]{3,1,0,2:T(8,128)(2,1)S(1)}, bf16[4,11,2,1024]{3,1,0,2:T(8,128)(2,1)S(1)}, u32[]{:S(2)}, u32[]{:S(2)}) collective-permute-start(bf16[4,11,2,1024]{3,1,0,2:T(8,128)(2,1)S(1)} %slice.100), channel_id=1, source_target_pairs={{0,1},{1,2},{2,3},{4,5},{5,6},{6,7},{8,9},{9,10},{10,11},{12,13},{... | collective-permute-start | bytes 540680 | tf_op jit(solution)/shard_map/ppermute | solution.py:15
  5.2 0.9 %fusion.1 = pred[1024]{0:T(1024)(128)(4,1)S(1)} fusion(s32[256]{0:T(256)} %param.6), kind=kLoop, calls=%fused_computation.7 | loop fusion | flops 523264 | bytes 2048 | tf_op jit(solution)/shard_map/reduce_or | solution.py:20
  6.1 1.8 %select_reduce_fusion.1 = (s32[512]{0:T(512)S(1)}, s32[512]{0:T(512)S(1)}, s32[512]{0:T(512)S(1)}) fusion(s32[1024]{0:T(1024)} %param.7, pred[1024]{0:T(1024)(128)(4,1)S(1)} %not.7), kind=kLoop, calls=%fused_computation.1 | loop fusion | flops 4192768 | bytes 11264 | tf_op jit(solution)/shard_map/reduce_min | solution.py:24
  8.0 0.1 gt.41
  8.1 0.1 copy.23
  8.2 0.1 gt.43
  8.3 0.1 copy.24
  8.4 0.1 reduce_min.12
  8.6 0.1 copy.21
  8.6 0.1 reduce_max.12
  8.8 0.1 copy.22
  8.9 1.8 %sine_multiply_fusion = (f32[32,1024]{1,0:T(8,128)}, f32[32,1024]{1,0:T(8,128)}, f32[32,1024]{1,0:T(8,128)}, f32[32,1024]{1,0:T(8,128)}) fusion(f32[1024]{0:T(1024)S(1)} %bitcast.22, s32[1024]{0:T(1024)S(1)} %bitcast.23, s32[32]{0:T(128)S(1)} %iota_multiply_fusion), kind=kLoop, calls=%fused_computation.23 | loop fusion | flops 983040 | bytes 532608 | tf_op jit(solution)/shard_map/mul | solution.py:40
  10.7 0.0 copy-done
  10.7 0.0 collective-permute-done
  10.7 0.2 maximum_bitcast_fusion
  10.9 2.4 %add_convert_fusion = bf16[2,4,32,1024]{3,2,1,0:T(8,128)(2,1)} fusion(bf16[2,4,43,1024]{3,2,1,0:T(8,128)(2,1)S(1)} %maximum_bitcast_fusion, f32[1024]{0:T(1024)S(1)} %bitcast.34, f32[1024]{0:T(1024)S(1)} %bitcast.35, f32[1024]{0:T(1024)S(1)} %bitcast.25, f32[1024]{0:T(1024)S(1)} %bitcast.26, f32[1024]{0:T(1024)S(1)} %bitcast.27, f32[1024]{0:T(1024)S(1)} %bitcast.28, ...), kind=kLoop, calls=%fused_computation.6 | loop fusion | flops 9437184 | bytes 6864896 | tf_op jit(solution)/shard_map/convert_element_type | solution.py:95
  13.3 4.8 %shard_map.46 = bf16[512,4,128]{2,1,0:T(4,128)(2,1)} custom-call(bf16[256,1024]{1,0:T(8,128)(2,1)} %bitcast.21, f32[32,1024]{1,0:T(8,128)} %get-tuple-element.24.refs_0_.refs_4_, f32[32,1024]{1,0:T(8,128)} %get-tuple-element.25.refs_1_.refs_5_, f32[32,1024]{1,0:T(8,128)} %get-tuple-element.21.refs_2_.refs_6_, f32[32,1024]{1,0:T(8,128)} %get-tuple-element.20.refs_3_.refs_7_, ...), custom_call_target="tpu_custom_call" | custom-call | tf_op jit(solution)/shard_map/pallas_call | solution.py:72
  18.0 60.5 %all_to_all.5.r_ref = bf16[512,4,128]{2,1,0:T(4,128)(2,1)} all-to-all(bf16[512,4,128]{2,1,0:T(4,128)(2,1)} %shard_map.46), channel_id=1, replica_groups=mesh['chan'=128,'tm'=4] {'tm','chan'}, dimensions={0} | all-to-all | bytes 1048576 | tf_op jit(solution)/shard_map/all_to_all | solution.py:106
  78.6 5.1 %shard_map.47 = f32[2,2,512,512]{3,2,1,0:T(8,128)} custom-call(bf16[512,4,128]{2,1,0:T(4,128)(2,1)} %all_to_all.5.r_ref), custom_call_target="tpu_custom_call" | custom-call | tf_op jit(solution)/shard_map/pallas_call | solution.py:148
  (8 shorter events, 0.1 us)
Async XLA Ops:
  0.0 10.7 %copy-start = (f32[12,1024]{1,0:T(8,128)S(1)}, f32[12,1024]{1,0:T(8,128)}, u32[]{:S(2)}) copy-start(f32[12,1024]{1,0:T(8,128)} %param.5) | copy-start | bytes 147460
  1.3 9.4 %collective-permute-start = (bf16[4,11,2,1024]{3,1,0,2:T(8,128)(2,1)S(1)}, bf16[4,11,2,1024]{3,1,0,2:T(8,128)(2,1)S(1)}, u32[]{:S(2)}, u32[]{:S(2)}) collective-permute-start(bf16[4,11,2,1024]{3,1,0,2:T(8,128)(2,1)S(1)} %slice.100), channel_id=1, source_target_pairs={{0,1},{1,2},{2,3},{4,5},{5,6},{6,7},{8,9},{9,10},{10,11},{12,13},{... | collective-permute-start | bytes 540680 | tf_op jit(solution)/shard_map/ppermute | solution.py:15
